TPU v7x, 32 devices: a whole 2x2x4 slice. The times are simulated.
32 devices in a mesh: lat: 8 (over y, x, core), wave: 4 (over z).
Axes of the slice: x: 2, y: 2, z: 4, core: 2. Of those that a mesh axis runs over, the one named last changes fastest.
Arguments:
- arnoldi_block: float32 [32, 4, 18, 2048], P(('lat', 'wave')), may hold values from -6 to 6
- legendre: bfloat16 [32, 2048, 2048], P(('lat', 'wave')), may hold values from -0.125 to 0.125
- wave_index: int32 [32], replicated, may hold values from 0 to 2047, as said below
- lat_index: int32 [2048], replicated, may hold values from 0 to 2047, each once
- quad_weight: float32 [2048], replicated, may hold values from 0.5 to 2
- zonal_flow: float32 [3, 2048], replicated, may hold values from -1 to 1
- layer_depth: float32 [3, 2048], replicated, may hold values from 0.3 to 3
- tide_height: float32 [2048, 4096], P(('lat', 'wave')), may hold values from -6 to 6
- mode_to_layer: float32 [3, 3], replicated, as said below
- layer_to_mode: float32 [3, 3], replicated, as said below
- mode_speed: float32 [3], replicated, may hold values from 0.3 to 3
Outputs:
- new_block: float32 [32, 4, 18, 2048], P(('lat', 'wave'))
- hessenberg: float32 [4, 4], replicated
- subdiagonal: float32 [4], replicated
Inputs may be any that keep to these rules, and one draw needn't show every extreme that they name: `wave_index`: 32 distinct wavenumbers, 0 and 2047 among them. `lat_index`: each row number once. `mode_to_layer`: diagonal entries 0.8 to 1.2, others within 0.35; drawn independently of layer_to_mode. `layer_to_mode`: diagonal entries 0.8 to 1.2, others within 0.35; drawn independently of mode_to_layer.
All inputs are finite; a program needn't handle non-finite values.
Results may differ from a plain program's by a relative error of at most 0.0065.
Values may be sent and summed in bfloat16 or wider, within the bound.
No kernel may reach another device: no remote copies, remote signals or barrier semaphores. Data moves between devices by JAX's collectives and lax.ppermute only.
A program may use at most 64 MiB of HBM per device.

v0:
```python
import functools
import math

import jax
import jax.numpy as jnp
from jax import lax
from jax.sharding import PartitionSpec as P
from jax.experimental import pallas as pl
from jax.experimental.pallas import tpu as pltpu

STEPS = 3


HIGHEST_PRECISION = lax.Precision.HIGHEST


def angle_tables(wave_ids, nlon):
    lon_steps = jnp.arange(nlon, dtype=jnp.int32)
    phase = wave_ids[:, None] * lon_steps[None, :] % nlon
    theta = phase.astype(jnp.float32) * (2.0 * math.pi / nlon)
    return jnp.concatenate([jnp.cos(theta), jnp.sin(theta)], axis=0)


def tide_kernel(items, pairs, rows, lhs_ref, tab_ref, tide_ref, hi_ref, lo_ref):
    step = pl.program_id(0)

    @pl.when(step == 0)
    def _():
        hi_ref[...] = jnp.zeros_like(hi_ref)
        lo_ref[...] = jnp.zeros_like(lo_ref)

    field = jnp.dot(lhs_ref[...], tab_ref[...], preferred_element_type=jnp.float32)
    width = field.shape[1]
    product = (field.reshape(items, rows, width) * tide_ref[...][None, :, :]).reshape(
        items * rows, width
    )
    product_hi = product.astype(jnp.bfloat16)
    product_lo = (product - product_hi.astype(jnp.float32)).astype(jnp.bfloat16)
    last_dims = (((1,), (1,)), ((), ()))
    hi_ref[...] += lax.dot_general(
        product_hi, tab_ref[...], last_dims, preferred_element_type=jnp.float32
    )
    lo_ref[...] += lax.dot_general(
        product_lo, tab_ref[0:pairs, :], last_dims, preferred_element_type=jnp.float32
    )


def tide_term(div_real, div_imag, tide_rows, tables_upper, tables_lower):
    slots, items, lays, rows = div_real.shape
    nlon = tables_upper.shape[1]
    pairs = 2 * slots
    stacked = jnp.concatenate([div_real, -div_imag], axis=0).reshape(pairs, items * lays * rows)
    lhs = jnp.concatenate([stacked, stacked], axis=0).T
    tabs = jnp.concatenate([tables_upper, tables_lower], axis=0)
    block = 1024
    mixed = items * lays * rows
    hi_part, lo_part = pl.pallas_call(
        functools.partial(tide_kernel, items * lays, pairs, rows),
        out_shape=(
            jax.ShapeDtypeStruct((mixed, 2 * pairs), jnp.float32),
            jax.ShapeDtypeStruct((mixed, pairs), jnp.float32),
        ),
        grid=(nlon // block,),
        in_specs=[
            pl.BlockSpec((mixed, 2 * pairs), lambda k: (0, 0)),
            pl.BlockSpec((2 * pairs, block), lambda k: (0, k)),
            pl.BlockSpec((rows, block), lambda k: (0, k)),
        ],
        out_specs=(
            pl.BlockSpec((mixed, 2 * pairs), lambda k: (0, 0)),
            pl.BlockSpec((mixed, pairs), lambda k: (0, 0)),
        ),
        compiler_params=pltpu.CompilerParams(dimension_semantics=("arbitrary",)),
        cost_estimate=pl.CostEstimate(
            flops=2 * mixed * nlon * (2 * pairs + 3 * pairs),
            transcendentals=0,
            bytes_accessed=2 * pairs * nlon * 2 + rows * nlon * 4 + mixed * 4 * pairs * 3,
        ),
    )(lhs, tabs, tide_rows)
    folded = (hi_part[:, :pairs] + hi_part[:, pairs:] + lo_part) * (2.0 / nlon)
    folded = folded.T.reshape(pairs, items, lays, rows)
    return (folded[:slots], -folded[slots:])


def tendency(grid_values, advect, coriolis, depth_rows, tide_real, tide_imag):
    vort_re = grid_values[:, :, :, 0, :]
    vort_im = grid_values[:, :, :, 1, :]
    div_re = grid_values[:, :, :, 2, :]
    div_im = grid_values[:, :, :, 3, :]
    height_re = grid_values[:, :, :, 4, :]
    height_im = grid_values[:, :, :, 5, :]
    depth_b = depth_rows[None, None, :, :]
    parts = [
        advect * vort_im - coriolis * div_re,
        -advect * vort_re - coriolis * div_im,
        advect * div_im + coriolis * vort_re,
        -advect * div_re + coriolis * vort_im,
        advect * height_im - depth_b * div_re - tide_real,
        -advect * height_re - depth_b * div_im - tide_imag,
    ]
    return jnp.stack(parts, axis=3)


def implicit_step(explicit, wave_ids, mode_to_layer, layer_to_mode, mode_speed, ntrunc):
    degrees = wave_ids[:, None] + jnp.arange(explicit.shape[-1], dtype=jnp.int32)[None, :]
    degree_f = degrees.astype(jnp.float32)
    laplace = (degree_f * (degree_f + 1.0) / float(ntrunc * ntrunc))[:, None, None, None, :]
    speeds = mode_speed[None, None, :, None, None]
    div_modes = jnp.einsum(
        "pk,svkrj->svprj", layer_to_mode, explicit[:, :, :, 2:4, :], precision=HIGHEST_PRECISION
    )
    height_modes = jnp.einsum(
        "pk,svkrj->svprj", layer_to_mode, explicit[:, :, :, 4:6, :], precision=HIGHEST_PRECISION
    )
    div_new = (div_modes + laplace * speeds * height_modes) / (1.0 + laplace * speeds * speeds)
    height_new = height_modes - speeds * div_new
    div_layers = jnp.einsum("kp,svprj->svkrj", mode_to_layer, div_new, precision=HIGHEST_PRECISION)
    height_layers = jnp.einsum(
        "kp,svprj->svkrj", mode_to_layer, height_new, precision=HIGHEST_PRECISION
    )
    return jnp.concatenate([explicit[:, :, :, 0:2, :], div_layers, height_layers], axis=3)


def exchange_sum(parts, device_count):
    flat = jnp.concatenate([p.reshape(-1) for p in parts])
    rows = jnp.broadcast_to(flat[None, :], (device_count, flat.shape[0]))
    gathered = lax.all_to_all(rows, ("lat", "wave"), 0, 0, tiled=True)
    total = jnp.sum(gathered, axis=0)
    out, start = [], 0
    for p in parts:
        out.append(total[start:start + p.size].reshape(p.shape))
        start += p.size
    return tuple(out)


def to_bands(values, device_count, lanes=128):
    ls, vecs, lays, parts, nlat = values.shape
    band = nlat // device_count
    split = values.reshape(ls, vecs, lays, parts, device_count, band)
    split = jnp.transpose(split, (4, 0, 1, 2, 3, 5))
    return split.reshape(device_count, ls * vecs * lays * parts * band // lanes, lanes)


def on_device(
    arnoldi_block,
    legendre,
    wave_index,
    lat_index,
    quad_weight,
    zonal_flow,
    layer_depth,
    tide_height,
    mode_to_layer,
    layer_to_mode,
    mode_speed,
):
    local_slots = arnoldi_block.shape[0]
    vectors = arnoldi_block.shape[1]
    channels = arnoldi_block.shape[2]
    nlat = legendre.shape[1]
    ndeg = legendre.shape[2]
    ntrunc = ndeg - 1
    layers = mode_speed.shape[0]
    band_rows = tide_height.shape[0]
    device_count = lax.axis_size("lat") * lax.axis_size("wave")
    device_rank = lax.axis_index("lat") * lax.axis_size("wave") + lax.axis_index("wave")
    all_slots = wave_index.shape[0]
    axes = ("lat", "wave")
    local_waves = lax.dynamic_slice_in_dim(wave_index, device_rank * local_slots, local_slots)
    degrees = local_waves[:, None] + jnp.arange(ndeg, dtype=jnp.int32)[None, :]
    truncation = (degrees <= ntrunc).astype(jnp.float32)[:, None, None, :]
    basis = arnoldi_block * truncation
    tables = angle_tables(wave_index, tide_height.shape[1])
    tables_upper = tables.astype(jnp.bfloat16)
    tables_lower = (tables - tables_upper.astype(jnp.float32)).astype(jnp.bfloat16)
    coriolis = (2 * lat_index + 1).astype(jnp.float32) / nlat - 1.0
    advect = (
        local_waves.astype(jnp.float32)[:, None, None, None] * zonal_flow[None, None, :, :] / ntrunc
    )
    def one_step(step_index, spectral):
        spectral_b = spectral.astype(jnp.bfloat16)
        grid_b = jnp.einsum(
            "svcj,slj->svcl", spectral_b, legendre, preferred_element_type=jnp.float32
        ).astype(jnp.bfloat16)
        grid_split = grid_b.reshape(local_slots, vectors, layers, 6, nlat)
        sent = to_bands(grid_split[:, :, :, 2:4, :], device_count)
        received = lax.all_to_all(sent, axes, 0, 0, tiled=True)
        band_div = received.reshape(all_slots, vectors, layers, 2, band_rows)
        tide_real, tide_imag = tide_term(
            band_div[:, :, :, 0, :],
            band_div[:, :, :, 1, :],
            tide_height,
            tables_upper,
            tables_lower,
        )
        tide_parts = jnp.stack([tide_real, tide_imag], axis=3)
        back = tide_parts.reshape(device_count, -1, 128)
        returned = lax.all_to_all(back, axes, 0, 0, tiled=True)
        returned = returned.reshape(device_count, local_slots, vectors, layers, 2, band_rows)
        tide_rows = jnp.transpose(returned, (1, 2, 3, 4, 0, 5)).reshape(
            local_slots, vectors, layers, 2, nlat
        )
        tendencies = tendency(
            grid_split.astype(jnp.float32),
            advect,
            coriolis,
            layer_depth,
            tide_rows[:, :, :, 0, :],
            tide_rows[:, :, :, 1, :],
        )
        weighted = (
            (quad_weight * tendencies)
            .astype(jnp.bfloat16)
            .reshape(local_slots, vectors, channels, nlat)
        )
        analysed = jnp.einsum(
            "svcl,slj->svcj", weighted, legendre, preferred_element_type=jnp.float32
        )
        analysed = analysed * truncation
        explicit = (spectral + analysed).reshape(local_slots, vectors, layers, 6, ndeg)
        spectral = (
            implicit_step(
                explicit, local_waves, mode_to_layer, layer_to_mode, mode_speed, ntrunc
            ).reshape(local_slots, vectors, channels, ndeg)
            * truncation
        )
        return spectral

    spectral = lax.fori_loop(0, STEPS, one_step, basis)
    entries = float(local_slots * device_count * channels * ndeg)
    local_proj = jnp.einsum("skcj,svcj->kv", basis, spectral, precision=HIGHEST_PRECISION)
    local_self = jnp.sum(spectral * spectral, axis=(0, 2, 3))
    local_gram = jnp.einsum("skcj,sqcj->kq", basis, basis, precision=HIGHEST_PRECISION)
    projection, self_sum, gram = exchange_sum((local_proj, local_self, local_gram), device_count)
    hessenberg = projection / entries
    residual = spectral - jnp.einsum(
        "skcj,kv->svcj", basis, hessenberg, precision=HIGHEST_PRECISION
    )
    quadratic = jnp.einsum("kv,kq,qv->v", hessenberg, gram, hessenberg, precision=HIGHEST_PRECISION)
    norm_sq = (self_sum - 2.0 * jnp.sum(hessenberg * projection, axis=0) + quadratic) / entries
    subdiagonal = jnp.sqrt(norm_sq + 1e-06)
    return (residual / subdiagonal[None, :, None, None], hessenberg, subdiagonal)


def solution(mesh):
    return jax.shard_map(
        on_device,
        mesh=mesh,
        in_specs=(
            P(("lat", "wave"), None, None, None),
            P(("lat", "wave"), None, None),
            P(),
            P(),
            P(),
            P(),
            P(),
            P(("lat", "wave"), None),
            P(),
            P(),
            P(),
        ),
        out_specs=(P(("lat", "wave"), None, None, None), P(), P()),
        check_vma=False,
    )
```

profile of v0, /device:TPU:0, one launch (start us, length us, event | category | flops | bytes accessed | tf_op | source)
XLA Modules:
  0.0 197.8 jit_solution(1071398243701595275)
XLA Ops:
  0.7 2.8 %fusion.52 = (f32[32,4096]{1,0:T(8,128)S(1)}, f32[32,4096]{1,0:T(8,128)S(1)}) fusion(s32[32]{0:T(128)} %param.15), kind=kLoop, calls=%fused_computation.83 | loop fusion | flops 1835008 | bytes 1048704 | tf_op jit(solution)/shard_map/cos | solution.py:21
  3.6 1.2 dynamic_slice.3
  5.5 0.7 fusion.54
  6.2 1.2 broadcast_multiply_fusion.2
  7.4 0.7 multiply_add_fusion.1
  8.1 0.8 negate_bitcast_fusion
  8.9 1.1 pad_maximum_fusion.3
  10.0 168.3 %while.13 = (s32[]{:T(128)}, f32[1,4,18,2048]{3,1,2,0:T(4,128)S(1)}, f32[2048]{0:T(1024)S(1)}, f32[1,1,3,2048]{3,2,1,0:T(4,128)S(1)}, bf16[1,2048,2048]{2,1,0:T(...) while((s32[]{:T(128)}, ...), condition=%wide.region_1.2_spmd.clone, body=%wide.region_0.1_spmd.clone.sunk | while | flops 3231582208 | bytes 42901892 | solution.py:229
  10.3 6.0 %fusion.93 = bf16[4,18,2048]{2,1,0:T(8,128)(2,1)S(1)} fusion(bf16[1,2048,2048]{2,1,0:T(8,128)(2,1)} %get-tuple-element.426, bf16[4,18,2048]{2,0,1:T(4,128)(2,1)S(1)} %convert_bitcast_fusion.2), kind=kOutput, calls=%fused_computation.8.clone.1 | convolution fusion | flops 604127232 | bytes 8978432 | tf_op jit(solution)/shard_map/while/body/eval_jaxpr/svcj,slj->svcl/dot_general | solution.py:182
  17.2 0.7 copy.160
  17.9 7.3 %all-to-all-start = ((bf16[32,12,128]{2,1,0:T(8,128)(2,1)}), bf16[32,12,128]{2,1,0:T(8,128)(2,1)S(1)}, u32[]{:S(2)}, u32[]{:S(2)}) async-start(bf16[32,12,128]{2,1,0:T(8,128)(2,1)} %copy.160), calls=%async_computation | async-start | bytes 262144 | tf_op jit(solution)/shard_map/while/body/eval_jaxpr/all_to_all | solution.py:187
  25.5 0.7 fusion.100
  26.1 0.7 compare_convert_fusion.2
  26.8 6.8 %all-to-all-done = bf16[32,12,128]{2,1,0:T(8,128)(2,1)S(1)} async-done(((bf16[32,12,128]{2,1,0:T(8,128)(2,1)}), bf16[32,12,128]{2,1,0:T(8,128)(2,1)S(1)}, u32[]{:S(2)}, u32[]{:S(2)}) %all-to-all-start) | async-done | bytes 98336 | tf_op jit(solution)/shard_map/while/body/eval_jaxpr/all_to_all | solution.py:187
  34.5 0.9 maximum_bitcast_fusion.2.lhs_ref
  35.4 7.5 %eval_jaxpr.3 = (f32[768,128]{1,0:T(8,128)}, f32[768,64]{1,0:T(8,128)}) custom-call(bf16[768,128]{1,0:T(8,128)(2,1)} %maximum_bitcast_fusion.2.lhs_ref, bf16[128,4096]{1,0:T(8,128)(2,1)} %get-tuple-element.430.tab_ref, f32[64,4096]{1,0:T(8,128)} %get-tuple-element.431.tide_ref), custom_call_target="tpu_custom_call" | custom-call | flops 2013265920 | bytes 2686976 | tf_op jit(solution)/shard_map/while/body/eval_jaxpr/pallas_call | solution.py:57
  42.9 1.4 multiply_bitcast_fusion.2
  45.5 0.8 copy.166
  46.3 2.6 %all-to-all-start.1 = ((f32[32,12,128]{2,1,0:T(8,128)}), f32[32,12,128]{2,1,0:T(8,128)S(1)}, u32[]{:S(2)}, u32[]{:S(2)}) async-start(f32[32,12,128]{2,1,0:T(8,128)} %copy.166), calls=%async_computation.1 | async-start | bytes 524288 | tf_op jit(solution)/shard_map/while/body/eval_jaxpr/all_to_all | solution.py:198
  49.0 10.1 %all-to-all-done.1 = f32[32,12,128]{2,1,0:T(8,128)S(1)} async-done(((f32[32,12,128]{2,1,0:T(8,128)}), f32[32,12,128]{2,1,0:T(8,128)S(1)}, u32[]{:S(2)}, u32[]{:S(2)}) %all-to-all-start.1) | async-done | bytes 196640 | tf_op jit(solution)/shard_map/while/body/eval_jaxpr/all_to_all | solution.py:198
  60.0 5.3 %fusion.98 = f32[1,4,18,2048]{3,2,1,0:T(8,128)S(1)} fusion(bf16[1,2048,2048]{2,1,0:T(8,128)(2,1)} %get-tuple-element.426, f32[1,4,18,2048]{3,1,2,0:T(4,128)S(1)} %get-tuple-element.407, bf16[4,18,2048]{2,0,1:T(4,128)(2,1)S(1)} %bitcast.205, f32[2048]{0:T(1024)S(1)} %bitcast.220), kind=kOutput, calls=%fused_computation.7.clone.1 | convolution fusion | flops 604274688 | bytes 9871360 | tf_op jit(solution)/shard_map/while/body/eval_jaxpr/svcl,slj->svcj/dot_general | solution.py:216
  65.7 0.7 convolution_bitcast_fusion.11
  66.4 0.7 fusion.101
  67.1 0.7 convolution_bitcast_fusion.12
  67.8 0.6 convolution_bitcast_fusion.13
  69.4 6.0 %fusion.93 = bf16[4,18,2048]{2,1,0:T(8,128)(2,1)S(1)} fusion(bf16[1,2048,2048]{2,1,0:T(8,128)(2,1)} %get-tuple-element.426, bf16[4,18,2048]{2,0,1:T(4,128)(2,1)S(1)} %convert_bitcast_fusion.2), kind=kOutput, calls=%fused_computation.8.clone.1 | convolution fusion | flops 604127232 | bytes 8978432 | tf_op jit(solution)/shard_map/while/body/eval_jaxpr/svcj,slj->svcl/dot_general | solution.py:182
  76.2 0.7 copy.160
  76.9 2.7 %all-to-all-start = ((bf16[32,12,128]{2,1,0:T(8,128)(2,1)}), bf16[32,12,128]{2,1,0:T(8,128)(2,1)S(1)}, u32[]{:S(2)}, u32[]{:S(2)}) async-start(bf16[32,12,128]{2,1,0:T(8,128)(2,1)} %copy.160), calls=%async_computation | async-start | bytes 262144 | tf_op jit(solution)/shard_map/while/body/eval_jaxpr/all_to_all | solution.py:187
  79.9 0.7 fusion.100
  80.5 0.7 compare_convert_fusion.2
  81.2 6.8 %all-to-all-done = bf16[32,12,128]{2,1,0:T(8,128)(2,1)S(1)} async-done(((bf16[32,12,128]{2,1,0:T(8,128)(2,1)}), bf16[32,12,128]{2,1,0:T(8,128)(2,1)S(1)}, u32[]{:S(2)}, u32[]{:S(2)}) %all-to-all-start) | async-done | bytes 98336 | tf_op jit(solution)/shard_map/while/body/eval_jaxpr/all_to_all | solution.py:187
  88.9 0.9 maximum_bitcast_fusion.2.lhs_ref
  89.9 7.5 %eval_jaxpr.3 = (f32[768,128]{1,0:T(8,128)}, f32[768,64]{1,0:T(8,128)}) custom-call(bf16[768,128]{1,0:T(8,128)(2,1)} %maximum_bitcast_fusion.2.lhs_ref, bf16[128,4096]{1,0:T(8,128)(2,1)} %get-tuple-element.430.tab_ref, f32[64,4096]{1,0:T(8,128)} %get-tuple-element.431.tide_ref), custom_call_target="tpu_custom_call" | custom-call | flops 2013265920 | bytes 2686976 | tf_op jit(solution)/shard_map/while/body/eval_jaxpr/pallas_call | solution.py:57
  97.4 1.4 multiply_bitcast_fusion.2
  100.0 0.8 copy.166
  100.8 2.6 %all-to-all-start.1 = ((f32[32,12,128]{2,1,0:T(8,128)}), f32[32,12,128]{2,1,0:T(8,128)S(1)}, u32[]{:S(2)}, u32[]{:S(2)}) async-start(f32[32,12,128]{2,1,0:T(8,128)} %copy.166), calls=%async_computation.1 | async-start | bytes 524288 | tf_op jit(solution)/shard_map/while/body/eval_jaxpr/all_to_all | solution.py:198
  103.5 10.1 %all-to-all-done.1 = f32[32,12,128]{2,1,0:T(8,128)S(1)} async-done(((f32[32,12,128]{2,1,0:T(8,128)}), f32[32,12,128]{2,1,0:T(8,128)S(1)}, u32[]{:S(2)}, u32[]{:S(2)}) %all-to-all-start.1) | async-done | bytes 196640 | tf_op jit(solution)/shard_map/while/body/eval_jaxpr/all_to_all | solution.py:198
  114.4 5.3 %fusion.98 = f32[1,4,18,2048]{3,2,1,0:T(8,128)S(1)} fusion(bf16[1,2048,2048]{2,1,0:T(8,128)(2,1)} %get-tuple-element.426, f32[1,4,18,2048]{3,1,2,0:T(4,128)S(1)} %get-tuple-element.407, bf16[4,18,2048]{2,0,1:T(4,128)(2,1)S(1)} %bitcast.205, f32[2048]{0:T(1024)S(1)} %bitcast.220), kind=kOutput, calls=%fused_computation.7.clone.1 | convolution fusion | flops 604274688 | bytes 9871360 | tf_op jit(solution)/shard_map/while/body/eval_jaxpr/svcl,slj->svcj/dot_general | solution.py:216
  120.1 0.7 convolution_bitcast_fusion.11
  120.8 0.7 fusion.101
  121.5 0.7 convolution_bitcast_fusion.12
  122.2 0.6 convolution_bitcast_fusion.13
  123.8 6.0 %fusion.93 = bf16[4,18,2048]{2,1,0:T(8,128)(2,1)S(1)} fusion(bf16[1,2048,2048]{2,1,0:T(8,128)(2,1)} %get-tuple-element.426, bf16[4,18,2048]{2,0,1:T(4,128)(2,1)S(1)} %convert_bitcast_fusion.2), kind=kOutput, calls=%fused_computation.8.clone.1 | convolution fusion | flops 604127232 | bytes 8978432 | tf_op jit(solution)/shard_map/while/body/eval_jaxpr/svcj,slj->svcl/dot_general | solution.py:182
  130.7 0.7 copy.160
  131.4 2.7 %all-to-all-start = ((bf16[32,12,128]{2,1,0:T(8,128)(2,1)}), bf16[32,12,128]{2,1,0:T(8,128)(2,1)S(1)}, u32[]{:S(2)}, u32[]{:S(2)}) async-start(bf16[32,12,128]{2,1,0:T(8,128)(2,1)} %copy.160), calls=%async_computation | async-start | bytes 262144 | tf_op jit(solution)/shard_map/while/body/eval_jaxpr/all_to_all | solution.py:187
  134.3 0.7 fusion.100
  135.0 0.7 compare_convert_fusion.2
  135.7 6.8 %all-to-all-done = bf16[32,12,128]{2,1,0:T(8,128)(2,1)S(1)} async-done(((bf16[32,12,128]{2,1,0:T(8,128)(2,1)}), bf16[32,12,128]{2,1,0:T(8,128)(2,1)S(1)}, u32[]{:S(2)}, u32[]{:S(2)}) %all-to-all-start) | async-done | bytes 98336 | tf_op jit(solution)/shard_map/while/body/eval_jaxpr/all_to_all | solution.py:187
  143.4 0.9 maximum_bitcast_fusion.2.lhs_ref
  144.3 7.5 %eval_jaxpr.3 = (f32[768,128]{1,0:T(8,128)}, f32[768,64]{1,0:T(8,128)}) custom-call(bf16[768,128]{1,0:T(8,128)(2,1)} %maximum_bitcast_fusion.2.lhs_ref, bf16[128,4096]{1,0:T(8,128)(2,1)} %get-tuple-element.430.tab_ref, f32[64,4096]{1,0:T(8,128)} %get-tuple-element.431.tide_ref), custom_call_target="tpu_custom_call" | custom-call | flops 2013265920 | bytes 2686976 | tf_op jit(solution)/shard_map/while/body/eval_jaxpr/pallas_call | solution.py:57
  151.8 1.4 multiply_bitcast_fusion.2
  154.4 0.8 copy.166
  155.2 2.6 %all-to-all-start.1 = ((f32[32,12,128]{2,1,0:T(8,128)}), f32[32,12,128]{2,1,0:T(8,128)S(1)}, u32[]{:S(2)}, u32[]{:S(2)}) async-start(f32[32,12,128]{2,1,0:T(8,128)} %copy.166), calls=%async_computation.1 | async-start | bytes 524288 | tf_op jit(solution)/shard_map/while/body/eval_jaxpr/all_to_all | solution.py:198
  157.9 10.1 %all-to-all-done.1 = f32[32,12,128]{2,1,0:T(8,128)S(1)} async-done(((f32[32,12,128]{2,1,0:T(8,128)}), f32[32,12,128]{2,1,0:T(8,128)S(1)}, u32[]{:S(2)}, u32[]{:S(2)}) %all-to-all-start.1) | async-done | bytes 196640 | tf_op jit(solution)/shard_map/while/body/eval_jaxpr/all_to_all | solution.py:198
  168.8 5.3 %fusion.98 = f32[1,4,18,2048]{3,2,1,0:T(8,128)S(1)} fusion(bf16[1,2048,2048]{2,1,0:T(8,128)(2,1)} %get-tuple-element.426, f32[1,4,18,2048]{3,1,2,0:T(4,128)S(1)} %get-tuple-element.407, bf16[4,18,2048]{2,0,1:T(4,128)(2,1)S(1)} %bitcast.205, f32[2048]{0:T(1024)S(1)} %bitcast.220), kind=kOutput, calls=%fused_computation.7.clone.1 | convolution fusion | flops 604274688 | bytes 9871360 | tf_op jit(solution)/shard_map/while/body/eval_jaxpr/svcl,slj->svcj/dot_general | solution.py:216
  174.6 0.7 convolution_bitcast_fusion.11
  175.3 0.7 fusion.101
  176.0 0.7 convolution_bitcast_fusion.12
  176.6 0.6 convolution_bitcast_fusion.13
  178.3 2.7 %convolution_bitcast_fusion.7 = f32[4,4]{1,0:T(4,128)S(1)} fusion(f32[1,4,18,2048]{3,1,2,0:T(4,128)S(1)} %get-tuple-element.178, f32[1,4,18,2048]{3,1,2,0:T(4,128)S(1)} %broadcast_multiply_fusion.2), kind=kOutput, calls=%fused_computation.61 | convolution fusion | flops 7077888 | bytes 1179712 | tf_op jit(solution)/shard_map/skcj,svcj->kv/dot_general | solution.py:231
  181.5 2.8 %convolution_bitcast_fusion.6 = f32[4,4]{1,0:T(4,128)S(1)} fusion(f32[1,4,18,2048]{3,1,2,0:T(4,128)S(1)} %broadcast_multiply_fusion.2), kind=kOutput, calls=%fused_computation.60 | convolution fusion | flops 7077888 | bytes 589888 | tf_op jit(solution)/shard_map/skcj,sqcj->kq/dot_general | solution.py:233
  184.5 9.7 %all_to_all.24 = f32[32,1,36]{2,1,0:T(1,128)S(1)} all-to-all(f32[32,1,36]{2,1,0:T(1,128)S(1)} %broadcast_in_dim.2), channel_id=1, replica_groups=mesh['lat'=8,'wave'=4] {'lat','wave'}, dimensions={0} | all-to-all | bytes 9216 | tf_op jit(solution)/shard_map/all_to_all | solution.py:127
  195.1 2.0 %fusion.37 = f32[1,4,18,2048]{3,1,2,0:T(4,128)} fusion(f32[1,4,18,2048]{3,1,2,0:T(4,128)S(1)} %get-tuple-element.178, f32[1,4,18,2048]{3,1,2,0:T(4,128)S(1)} %broadcast_multiply_fusion.2, f32[4]{0:T(128)S(1)} %add_sqrt_fusion, f32[4,4]{0,1:T(4,128)S(1)} %copy.109), kind=kOutput, calls=%fused_computation.57 | convolution fusion | flops 7372816 | bytes 1769552 | tf_op jit(solution)/shard_map/skcj,kv->svcj/dot_general | solution.py:236
  197.1 0.7 copy.111
  (134 shorter events, 17.8 us)
Async XLA Ops:
  0.6 9.3 %copy-start.1 = (f32[2048]{0:T(1024)S(1)}, f32[2048]{0:T(1024)}, u32[]{:S(2)}) copy-start(f32[2048]{0:T(1024)} %param.17) | copy-start | bytes 24580
  0.6 9.3 %copy-start = (f32[3,2048]{1,0:T(4,128)S(1)}, f32[3,2048]{1,0:T(4,128)}, u32[]{:S(2)}) copy-start(f32[3,2048]{1,0:T(4,128)} %param.19) | copy-start | bytes 73732
  0.7 9.3 %copy-start.2 = (f32[3,3]{1,0:T(4,128)S(1)}, f32[3,3]{1,0:T(4,128)}, u32[]{:S(2)}) copy-start(f32[3,3]{1,0:T(4,128)} %param.21) | copy-start | bytes 112
  0.7 9.3 %copy-start.3 = (f32[3,3]{1,0:T(4,128)S(1)}, f32[3,3]{1,0:T(4,128)}, u32[]{:S(2)}) copy-start(f32[3,3]{1,0:T(4,128)} %param.22) | copy-start | bytes 112
  0.7 9.3 %copy-start.4 = (f32[3]{0:T(128)S(1)}, f32[3]{0:T(128)}, u32[]{:S(2)}) copy-start(f32[3]{0:T(128)} %param.23) | copy-start | bytes 40
  17.9 15.7 %all-to-all-start = ((bf16[32,12,128]{2,1,0:T(8,128)(2,1)}), bf16[32,12,128]{2,1,0:T(8,128)(2,1)S(1)}, u32[]{:S(2)}, u32[]{:S(2)}) async-start(bf16[32,12,128]{2,1,0:T(8,128)(2,1)} %copy.160), calls=%async_computation | async-start | bytes 262144 | tf_op jit(solution)/shard_map/while/body/eval_jaxpr/all_to_all | solution.py:187
  46.3 12.8 %all-to-all-start.1 = ((f32[32,12,128]{2,1,0:T(8,128)}), f32[32,12,128]{2,1,0:T(8,128)S(1)}, u32[]{:S(2)}, u32[]{:S(2)}) async-start(f32[32,12,128]{2,1,0:T(8,128)} %copy.166), calls=%async_computation.1 | async-start | bytes 524288 | tf_op jit(solution)/shard_map/while/body/eval_jaxpr/all_to_all | solution.py:198
  76.9 11.1 %all-to-all-start = ((bf16[32,12,128]{2,1,0:T(8,128)(2,1)}), bf16[32,12,128]{2,1,0:T(8,128)(2,1)S(1)}, u32[]{:S(2)}, u32[]{:S(2)}) async-start(bf16[32,12,128]{2,1,0:T(8,128)(2,1)} %copy.160), calls=%async_computation | async-start | bytes 262144 | tf_op jit(solution)/shard_map/while/body/eval_jaxpr/all_to_all | solution.py:187
  100.8 12.8 %all-to-all-start.1 = ((f32[32,12,128]{2,1,0:T(8,128)}), f32[32,12,128]{2,1,0:T(8,128)S(1)}, u32[]{:S(2)}, u32[]{:S(2)}) async-start(f32[32,12,128]{2,1,0:T(8,128)} %copy.166), calls=%async_computation.1 | async-start | bytes 524288 | tf_op jit(solution)/shard_map/while/body/eval_jaxpr/all_to_all | solution.py:198
  131.4 11.1 %all-to-all-start = ((bf16[32,12,128]{2,1,0:T(8,128)(2,1)}), bf16[32,12,128]{2,1,0:T(8,128)(2,1)S(1)}, u32[]{:S(2)}, u32[]{:S(2)}) async-start(bf16[32,12,128]{2,1,0:T(8,128)(2,1)} %copy.160), calls=%async_computation | async-start | bytes 262144 | tf_op jit(solution)/shard_map/while/body/eval_jaxpr/all_to_all | solution.py:187
  155.2 12.8 %all-to-all-start.1 = ((f32[32,12,128]{2,1,0:T(8,128)}), f32[32,12,128]{2,1,0:T(8,128)S(1)}, u32[]{:S(2)}, u32[]{:S(2)}) async-start(f32[32,12,128]{2,1,0:T(8,128)} %copy.166), calls=%async_computation.1 | async-start | bytes 524288 | tf_op jit(solution)/shard_map/while/body/eval_jaxpr/all_to_all | solution.py:198
  195.1 2.7 %copy-start.5 = (f32[4]{0:T(128)}, f32[4]{0:T(128)S(1)}, u32[]{:S(2)}) copy-start(f32[4]{0:T(128)S(1)} %add_sqrt_fusion) | copy-start | bytes 52
where the time goes:
time: 199 us; the launch traced here: 198 us
  waiting for transfers between devices  50.8 us (26%)
  matrix products  49.5 us (25%)
  other arithmetic  25.2 us (13%)
  Pallas kernels  22.4 us (11%)
  starting transfers between devices  20.4 us (10%)
  local copies, waits for them, and re-layouts  17 us (9%)
  blocking collectives  9.67 us (5%)
    all_to_all x3, waiting for transfers between devices, one_step(): returned = lax.all_to_all(back, axes, 0, 0, tiled=True)  30.3 us
    pallas_call x3, Pallas kernels, tide_term(): pl.pallas_call(functools.partial(tide_kernel, items * lays, pairs, rows),...  22.4 us
    all_to_all x3, waiting for transfers between devices, one_step(): received = lax.all_to_all(sent, axes, 0, 0, tiled=True)  20.4 us
    dot_general x3, matrix products, one_step(): jnp.einsum('svcj,slj->svcl', spectral_b, legendre, preferred_element_type...  18.1 us
    dot_general x3, matrix products, one_step(): jnp.einsum('svcl,slj->svcj', weighted, legendre, preferred_element_type=j...  15.9 us
    all_to_all x3, starting transfers between devices, one_step(): received = lax.all_to_all(sent, axes, 0, 0, tiled=True)  12.7 us
    all_to_all x1, blocking collectives, exchange_sum(): gathered = lax.all_to_all(rows, ('lat', 'wave'), 0, 0, tiled=True)  9.67 us
    all_to_all x3, starting transfers between devices, one_step(): returned = lax.all_to_all(back, axes, 0, 0, tiled=True)  7.76 us
  transfers between devices with their start and end apart: 6, of which 6 were waited for; matrix products, arithmetic and copies ran while one was open for 2% of the time, Pallas kernels for 0%

commit v1 on v0

--- a/solution.py
+++ b/solution.py
@@ -131,6 +131,34 @@
         out.append(total[start:start + p.size].reshape(p.shape))
         start += p.size
     return tuple(out)
+
+
+def synthesis_kernel(table_ref, coeff_ref, out_ref):
+    out_ref[0] = jnp.dot(
+        table_ref[0], coeff_ref[0], preferred_element_type=jnp.float32
+    ).astype(out_ref.dtype)
+
+
+def synthesize(coeffs, tables):
+    slots, rows, ndeg = coeffs.shape
+    nlat = tables.shape[1]
+    block = 256
+    coeffs_t = jnp.swapaxes(coeffs, 1, 2)
+    return pl.pallas_call(
+        synthesis_kernel,
+        out_shape=jax.ShapeDtypeStruct((slots, nlat, rows), jnp.bfloat16),
+        grid=(slots, nlat // block),
+        in_specs=[
+            pl.BlockSpec((1, block, ndeg), lambda s, i: (s, i, 0)),
+            pl.BlockSpec((1, ndeg, rows), lambda s, i: (s, 0, 0)),
+        ],
+        out_specs=pl.BlockSpec((1, block, rows), lambda s, i: (s, i, 0)),
+        cost_estimate=pl.CostEstimate(
+            flops=2 * slots * nlat * ndeg * rows,
+            transcendentals=0,
+            bytes_accessed=slots * (nlat * ndeg + ndeg * rows + nlat * rows) * 2,
+        ),
+    )(tables, coeffs_t)
 
 
 def to_bands(values, device_count, lanes=128):
@@ -179,9 +207,10 @@
     )
     def one_step(step_index, spectral):
         spectral_b = spectral.astype(jnp.bfloat16)
-        grid_b = jnp.einsum(
-            "svcj,slj->svcl", spectral_b, legendre, preferred_element_type=jnp.float32
-        ).astype(jnp.bfloat16)
+        grid_t = synthesize(
+            spectral_b.reshape(local_slots, vectors * channels, ndeg), legendre
+        )
+        grid_b = jnp.swapaxes(grid_t, 1, 2).reshape(local_slots, vectors, channels, nlat)
         grid_split = grid_b.reshape(local_slots, vectors, layers, 6, nlat)
         sent = to_bands(grid_split[:, :, :, 2:4, :], device_count)
         received = lax.all_to_all(sent, axes, 0, 0, tiled=True)

time: 199 us -> 219 us (1.10)
  Pallas kernels: 22.4 us -> 47.2 us
  matrix products: 49.5 us -> 31.6 us
  local copies, waits for them, and re-layouts: 17 us -> 27.8 us
    pallas_call x0 -> x3, Pallas kernels: none -> 24.8 us  [synthesize(): pl.pallas_call(synthesis_kernel, out_shape=jax.ShapeDtypeStruct((slots, n...]
    dot_general x3 -> x0, matrix products: 18.1 us -> none  [one_step(): jnp.einsum('svcj,slj->svcl', spectral_b, legendre, preferred_element_type...]
    transpose x0 -> x3, local copies, waits for them, and re-layouts: none -> 3.69 us  [one_step(): jnp.swapaxes(grid_t, 1, 2).reshape(local_slots, vectors, channels, nlat)]
    reshape x0 -> x9, local copies, waits for them, and re-layouts: none -> 3.61 us  [the longest x6 3.3 us: one_step(): spectral_b.reshape(local_slots, vectors * channels, ndeg)]
    another operation x0 -> x3, local copies, waits for them, and re-layouts: none -> 2.83 us  [tendency(): return jnp.stack(parts, axis=3)]
    add x0 -> x3, other arithmetic: none -> 2.45 us  [tendency(): advect * div_im + coriolis * vort_re]
where the time goes in v1:
time: 219 us; the launch traced here: 217 us
  waiting for transfers between devices  51.4 us (23%)
  Pallas kernels  47.2 us (22%)
  matrix products  31.6 us (14%)
  local copies, waits for them, and re-layouts  27.8 us (13%)
  other arithmetic  26.4 us (12%)
  starting transfers between devices  20.4 us (9%)
  blocking collectives  9.66 us (4%)
    all_to_all x3, waiting for transfers between devices, one_step(): returned = lax.all_to_all(back, axes, 0, 0, tiled=True)  30.3 us
    pallas_call x3, Pallas kernels, synthesize(): pl.pallas_call(synthesis_kernel, out_shape=jax.ShapeDtypeStruct((slots, n...  24.8 us
    pallas_call x3, Pallas kernels, tide_term(): pl.pallas_call(functools.partial(tide_kernel, items * lays, pairs, rows),...  22.4 us
    all_to_all x3, waiting for transfers between devices, one_step(): received = lax.all_to_all(sent, axes, 0, 0, tiled=True)  21 us
    dot_general x3, matrix products, one_step(): jnp.einsum('svcl,slj->svcj', weighted, legendre, preferred_element_type=j...  16 us
    all_to_all x3, starting transfers between devices, one_step(): received = lax.all_to_all(sent, axes, 0, 0, tiled=True)  12.7 us
    all_to_all x1, blocking collectives, exchange_sum(): gathered = lax.all_to_all(rows, ('lat', 'wave'), 0, 0, tiled=True)  9.66 us
    all_to_all x3, starting transfers between devices, one_step(): returned = lax.all_to_all(back, axes, 0, 0, tiled=True)  7.76 us
  transfers between devices with their start and end apart: 6, of which 6 were waited for; matrix products, arithmetic and copies ran while one was open for 2% of the time, Pallas kernels for 0%

profile of v1, /device:TPU:0, one launch (start us, length us, event | category | flops | bytes accessed | tf_op | source)
XLA Modules:
  0.0 217.3 jit_solution(15490564623604205884)
XLA Ops:
  0.7 2.8 %fusion.44 = (f32[32,4096]{1,0:T(8,128)S(1)}, f32[32,4096]{1,0:T(8,128)S(1)}) fusion(s32[32]{0:T(128)} %param.15), kind=kLoop, calls=%fused_computation.76 | loop fusion | flops 1835008 | bytes 1048704 | tf_op jit(solution)/shard_map/cos | solution.py:21
  3.6 1.2 dynamic_slice.3
  6.2 1.2 broadcast_multiply_fusion.2
  7.4 0.7 multiply_add_fusion.3
  8.1 0.8 negate_bitcast_fusion
  8.9 1.0 pad_maximum_fusion.3
  10.0 187.9 %while.13 = (s32[]{:T(128)}, f32[1,4,18,2048]{3,1,2,0:T(4,128)S(1)}, f32[2048]{0:T(1024)S(1)}, f32[1,1,3,2048]{3,2,1,0:T(4,128)S(1)}, bf16[1,2048,2048]{2,1,0:T(...) while((s32[]{:T(128)}, ...), condition=%wide.region_1.2_spmd.clone, body=%wide.region_0.1_spmd.clone.sunk | while | flops 3231434752 | bytes 46236036 | solution.py:258
  10.6 1.0 copy.171
  11.6 8.3 %eval_jaxpr.6 = bf16[1,2048,72]{2,1,0:T(8,128)(2,1)} custom-call(bf16[1,2048,2048]{2,1,0:T(8,128)(2,1)} %get-tuple-element.462.table_ref, bf16[1,2048,72]{2,1,0:T(8,128)(2,1)} %bitcast.195), custom_call_target="tpu_custom_call" | custom-call | flops 603979776 | bytes 8978432 | tf_op jit(solution)/shard_map/while/body/eval_jaxpr/pallas_call | solution.py:147
  19.8 1.2 copy.172
  21.8 0.7 copy.174
  22.5 7.3 %all-to-all-start = ((bf16[32,12,128]{2,1,0:T(8,128)(2,1)}), bf16[32,12,128]{2,1,0:T(8,128)(2,1)S(1)}, u32[]{:S(2)}, u32[]{:S(2)}) async-start(bf16[32,12,128]{2,1,0:T(8,128)(2,1)} %copy.174), calls=%async_computation | async-start | bytes 262144 | tf_op jit(solution)/shard_map/while/body/eval_jaxpr/all_to_all | solution.py:216
  31.2 7.0 %all-to-all-done = bf16[32,12,128]{2,1,0:T(8,128)(2,1)S(1)} async-done(((bf16[32,12,128]{2,1,0:T(8,128)(2,1)}), bf16[32,12,128]{2,1,0:T(8,128)(2,1)S(1)}, u32[]{:S(2)}, u32[]{:S(2)}) %all-to-all-start) | async-done | bytes 98336 | tf_op jit(solution)/shard_map/while/body/eval_jaxpr/all_to_all | solution.py:216
  39.1 0.9 maximum_bitcast_fusion.2.lhs_ref
  40.1 7.5 %eval_jaxpr.7 = (f32[768,128]{1,0:T(8,128)}, f32[768,64]{1,0:T(8,128)}) custom-call(bf16[768,128]{1,0:T(8,128)(2,1)} %maximum_bitcast_fusion.2.lhs_ref, bf16[128,4096]{1,0:T(8,128)(2,1)} %get-tuple-element.466.tab_ref, f32[64,4096]{1,0:T(8,128)} %get-tuple-element.467.tide_ref), custom_call_target="tpu_custom_call" | custom-call | flops 2013265920 | bytes 2686976 | tf_op jit(solution)/shard_map/while/body/eval_jaxpr/pallas_call | solution.py:57
  47.5 1.4 multiply_bitcast_fusion.2
  50.1 0.8 copy.180
  51.0 2.6 %all-to-all-start.1 = ((f32[32,12,128]{2,1,0:T(8,128)}), f32[32,12,128]{2,1,0:T(8,128)S(1)}, u32[]{:S(2)}, u32[]{:S(2)}) async-start(f32[32,12,128]{2,1,0:T(8,128)} %copy.180), calls=%async_computation.1 | async-start | bytes 524288 | tf_op jit(solution)/shard_map/while/body/eval_jaxpr/all_to_all | solution.py:227
  53.6 10.1 %all-to-all-done.1 = f32[32,12,128]{2,1,0:T(8,128)S(1)} async-done(((f32[32,12,128]{2,1,0:T(8,128)}), f32[32,12,128]{2,1,0:T(8,128)S(1)}, u32[]{:S(2)}, u32[]{:S(2)}) %all-to-all-start.1) | async-done | bytes 196640 | tf_op jit(solution)/shard_map/while/body/eval_jaxpr/all_to_all | solution.py:227
  64.3 0.8 multiply_add_fusion.5
  65.2 0.9 stack.24
  66.4 5.3 %fusion.80 = f32[1,4,18,2048]{3,2,1,0:T(8,128)S(1)} fusion(bf16[1,2048,2048]{2,1,0:T(8,128)(2,1)} %get-tuple-element.462.table_ref, f32[1,4,18,2048]{3,1,2,0:T(4,128)S(1)} %get-tuple-element.443, bf16[4,18,2048]{2,0,1:T(4,128)(2,1)S(1)} %bitcast.194, f32[2048]{0:T(1024)S(1)} %bitcast.203), kind=kOutput, calls=%fused_computation.5.clone.1 | convolution fusion | flops 604274688 | bytes 9871360 | tf_op jit(solution)/shard_map/while/body/eval_jaxpr/svcl,slj->svcj/dot_general | solution.py:245
  72.9 0.7 fusion.83
  73.6 0.7 convolution_bitcast_fusion.12
  76.1 1.0 copy.171
  77.1 8.3 %eval_jaxpr.6 = bf16[1,2048,72]{2,1,0:T(8,128)(2,1)} custom-call(bf16[1,2048,2048]{2,1,0:T(8,128)(2,1)} %get-tuple-element.462.table_ref, bf16[1,2048,72]{2,1,0:T(8,128)(2,1)} %bitcast.195), custom_call_target="tpu_custom_call" | custom-call | flops 603979776 | bytes 8978432 | tf_op jit(solution)/shard_map/while/body/eval_jaxpr/pallas_call | solution.py:147
  85.4 1.2 copy.172
  87.4 0.7 copy.174
  88.1 2.7 %all-to-all-start = ((bf16[32,12,128]{2,1,0:T(8,128)(2,1)}), bf16[32,12,128]{2,1,0:T(8,128)(2,1)S(1)}, u32[]{:S(2)}, u32[]{:S(2)}) async-start(bf16[32,12,128]{2,1,0:T(8,128)(2,1)} %copy.174), calls=%async_computation | async-start | bytes 262144 | tf_op jit(solution)/shard_map/while/body/eval_jaxpr/all_to_all | solution.py:216
  92.2 7.0 %all-to-all-done = bf16[32,12,128]{2,1,0:T(8,128)(2,1)S(1)} async-done(((bf16[32,12,128]{2,1,0:T(8,128)(2,1)}), bf16[32,12,128]{2,1,0:T(8,128)(2,1)S(1)}, u32[]{:S(2)}, u32[]{:S(2)}) %all-to-all-start) | async-done | bytes 98336 | tf_op jit(solution)/shard_map/while/body/eval_jaxpr/all_to_all | solution.py:216
  100.1 0.9 maximum_bitcast_fusion.2.lhs_ref
  101.0 7.5 %eval_jaxpr.7 = (f32[768,128]{1,0:T(8,128)}, f32[768,64]{1,0:T(8,128)}) custom-call(bf16[768,128]{1,0:T(8,128)(2,1)} %maximum_bitcast_fusion.2.lhs_ref, bf16[128,4096]{1,0:T(8,128)(2,1)} %get-tuple-element.466.tab_ref, f32[64,4096]{1,0:T(8,128)} %get-tuple-element.467.tide_ref), custom_call_target="tpu_custom_call" | custom-call | flops 2013265920 | bytes 2686976 | tf_op jit(solution)/shard_map/while/body/eval_jaxpr/pallas_call | solution.py:57
  108.5 1.4 multiply_bitcast_fusion.2
  111.1 0.8 copy.180
  111.9 2.6 %all-to-all-start.1 = ((f32[32,12,128]{2,1,0:T(8,128)}), f32[32,12,128]{2,1,0:T(8,128)S(1)}, u32[]{:S(2)}, u32[]{:S(2)}) async-start(f32[32,12,128]{2,1,0:T(8,128)} %copy.180), calls=%async_computation.1 | async-start | bytes 524288 | tf_op jit(solution)/shard_map/while/body/eval_jaxpr/all_to_all | solution.py:227
  114.6 10.1 %all-to-all-done.1 = f32[32,12,128]{2,1,0:T(8,128)S(1)} async-done(((f32[32,12,128]{2,1,0:T(8,128)}), f32[32,12,128]{2,1,0:T(8,128)S(1)}, u32[]{:S(2)}, u32[]{:S(2)}) %all-to-all-start.1) | async-done | bytes 196640 | tf_op jit(solution)/shard_map/while/body/eval_jaxpr/all_to_all | solution.py:227
  125.3 0.8 multiply_add_fusion.5
  126.1 0.9 stack.24
  127.4 5.3 %fusion.80 = f32[1,4,18,2048]{3,2,1,0:T(8,128)S(1)} fusion(bf16[1,2048,2048]{2,1,0:T(8,128)(2,1)} %get-tuple-element.462.table_ref, f32[1,4,18,2048]{3,1,2,0:T(4,128)S(1)} %get-tuple-element.443, bf16[4,18,2048]{2,0,1:T(4,128)(2,1)S(1)} %bitcast.194, f32[2048]{0:T(1024)S(1)} %bitcast.203), kind=kOutput, calls=%fused_computation.5.clone.1 | convolution fusion | flops 604274688 | bytes 9871360 | tf_op jit(solution)/shard_map/while/body/eval_jaxpr/svcl,slj->svcj/dot_general | solution.py:245
  133.2 0.7 convolution_bitcast_fusion.11
  133.8 0.7 fusion.83
  134.5 0.7 convolution_bitcast_fusion.12
  137.1 1.0 copy.171
  138.1 8.3 %eval_jaxpr.6 = bf16[1,2048,72]{2,1,0:T(8,128)(2,1)} custom-call(bf16[1,2048,2048]{2,1,0:T(8,128)(2,1)} %get-tuple-element.462.table_ref, bf16[1,2048,72]{2,1,0:T(8,128)(2,1)} %bitcast.195), custom_call_target="tpu_custom_call" | custom-call | flops 603979776 | bytes 8978432 | tf_op jit(solution)/shard_map/while/body/eval_jaxpr/pallas_call | solution.py:147
  146.4 1.2 copy.172
  148.3 0.7 copy.174
  149.0 2.7 %all-to-all-start = ((bf16[32,12,128]{2,1,0:T(8,128)(2,1)}), bf16[32,12,128]{2,1,0:T(8,128)(2,1)S(1)}, u32[]{:S(2)}, u32[]{:S(2)}) async-start(bf16[32,12,128]{2,1,0:T(8,128)(2,1)} %copy.174), calls=%async_computation | async-start | bytes 262144 | tf_op jit(solution)/shard_map/while/body/eval_jaxpr/all_to_all | solution.py:216
  153.1 7.0 %all-to-all-done = bf16[32,12,128]{2,1,0:T(8,128)(2,1)S(1)} async-done(((bf16[32,12,128]{2,1,0:T(8,128)(2,1)}), bf16[32,12,128]{2,1,0:T(8,128)(2,1)S(1)}, u32[]{:S(2)}, u32[]{:S(2)}) %all-to-all-start) | async-done | bytes 98336 | tf_op jit(solution)/shard_map/while/body/eval_jaxpr/all_to_all | solution.py:216
  161.1 0.9 maximum_bitcast_fusion.2.lhs_ref
  162.0 7.5 %eval_jaxpr.7 = (f32[768,128]{1,0:T(8,128)}, f32[768,64]{1,0:T(8,128)}) custom-call(bf16[768,128]{1,0:T(8,128)(2,1)} %maximum_bitcast_fusion.2.lhs_ref, bf16[128,4096]{1,0:T(8,128)(2,1)} %get-tuple-element.466.tab_ref, f32[64,4096]{1,0:T(8,128)} %get-tuple-element.467.tide_ref), custom_call_target="tpu_custom_call" | custom-call | flops 2013265920 | bytes 2686976 | tf_op jit(solution)/shard_map/while/body/eval_jaxpr/pallas_call | solution.py:57
  169.5 1.4 multiply_bitcast_fusion.2
  172.1 0.8 copy.180
  172.9 2.6 %all-to-all-start.1 = ((f32[32,12,128]{2,1,0:T(8,128)}), f32[32,12,128]{2,1,0:T(8,128)S(1)}, u32[]{:S(2)}, u32[]{:S(2)}) async-start(f32[32,12,128]{2,1,0:T(8,128)} %copy.180), calls=%async_computation.1 | async-start | bytes 524288 | tf_op jit(solution)/shard_map/while/body/eval_jaxpr/all_to_all | solution.py:227
  175.6 10.1 %all-to-all-done.1 = f32[32,12,128]{2,1,0:T(8,128)S(1)} async-done(((f32[32,12,128]{2,1,0:T(8,128)}), f32[32,12,128]{2,1,0:T(8,128)S(1)}, u32[]{:S(2)}, u32[]{:S(2)}) %all-to-all-start.1) | async-done | bytes 196640 | tf_op jit(solution)/shard_map/while/body/eval_jaxpr/all_to_all | solution.py:227
  186.3 0.8 multiply_add_fusion.5
  187.1 0.9 stack.24
  188.3 5.3 %fusion.80 = f32[1,4,18,2048]{3,2,1,0:T(8,128)S(1)} fusion(bf16[1,2048,2048]{2,1,0:T(8,128)(2,1)} %get-tuple-element.462.table_ref, f32[1,4,18,2048]{3,1,2,0:T(4,128)S(1)} %get-tuple-element.443, bf16[4,18,2048]{2,0,1:T(4,128)(2,1)S(1)} %bitcast.194, f32[2048]{0:T(1024)S(1)} %bitcast.203), kind=kOutput, calls=%fused_computation.5.clone.1 | convolution fusion | flops 604274688 | bytes 9871360 | tf_op jit(solution)/shard_map/while/body/eval_jaxpr/svcl,slj->svcj/dot_general | solution.py:245
  194.1 0.7 convolution_bitcast_fusion.11
  194.8 0.7 fusion.83
  195.5 0.7 convolution_bitcast_fusion.12
  197.9 2.7 %convolution_bitcast_fusion.7 = f32[4,4]{1,0:T(4,128)S(1)} fusion(f32[1,4,18,2048]{3,1,2,0:T(4,128)S(1)} %get-tuple-element.177, f32[1,4,18,2048]{3,1,2,0:T(4,128)S(1)} %broadcast_multiply_fusion.2), kind=kOutput, calls=%fused_computation.54 | convolution fusion | flops 7077888 | bytes 1179712 | tf_op jit(solution)/shard_map/skcj,svcj->kv/dot_general | solution.py:260
  201.0 2.8 %convolution_bitcast_fusion.6 = f32[4,4]{1,0:T(4,128)S(1)} fusion(f32[1,4,18,2048]{3,1,2,0:T(4,128)S(1)} %broadcast_multiply_fusion.2), kind=kOutput, calls=%fused_computation.53 | convolution fusion | flops 7077888 | bytes 589888 | tf_op jit(solution)/shard_map/skcj,sqcj->kq/dot_general | solution.py:262
  204.1 9.7 %all_to_all.24 = f32[32,1,36]{2,1,0:T(1,128)S(1)} all-to-all(f32[32,1,36]{2,1,0:T(1,128)S(1)} %broadcast_in_dim.2), channel_id=1, replica_groups=mesh['lat'=8,'wave'=4] {'lat','wave'}, dimensions={0} | all-to-all | bytes 9216 | tf_op jit(solution)/shard_map/all_to_all | solution.py:127
  214.6 2.0 fusion.29
  (137 shorter events, 25.6 us)
Async XLA Ops:
  0.6 9.3 %copy-start.1 = (f32[2048]{0:T(1024)S(1)}, f32[2048]{0:T(1024)}, u32[]{:S(2)}) copy-start(f32[2048]{0:T(1024)} %param.17) | copy-start | bytes 24580
  0.6 9.3 %copy-start = (f32[3,2048]{1,0:T(4,128)S(1)}, f32[3,2048]{1,0:T(4,128)}, u32[]{:S(2)}) copy-start(f32[3,2048]{1,0:T(4,128)} %param.19) | copy-start | bytes 73732
  0.7 9.3 %copy-start.2 = (f32[3,3]{1,0:T(4,128)S(1)}, f32[3,3]{1,0:T(4,128)}, u32[]{:S(2)}) copy-start(f32[3,3]{1,0:T(4,128)} %param.21) | copy-start | bytes 112
  0.7 9.3 %copy-start.3 = (f32[3,3]{1,0:T(4,128)S(1)}, f32[3,3]{1,0:T(4,128)}, u32[]{:S(2)}) copy-start(f32[3,3]{1,0:T(4,128)} %param.22) | copy-start | bytes 112
  0.7 9.3 %copy-start.4 = (f32[3]{0:T(128)S(1)}, f32[3]{0:T(128)}, u32[]{:S(2)}) copy-start(f32[3]{0:T(128)} %param.23) | copy-start | bytes 40
  22.5 15.7 %all-to-all-start = ((bf16[32,12,128]{2,1,0:T(8,128)(2,1)}), bf16[32,12,128]{2,1,0:T(8,128)(2,1)S(1)}, u32[]{:S(2)}, u32[]{:S(2)}) async-start(bf16[32,12,128]{2,1,0:T(8,128)(2,1)} %copy.174), calls=%async_computation | async-start | bytes 262144 | tf_op jit(solution)/shard_map/while/body/eval_jaxpr/all_to_all | solution.py:216
  51.0 12.8 %all-to-all-start.1 = ((f32[32,12,128]{2,1,0:T(8,128)}), f32[32,12,128]{2,1,0:T(8,128)S(1)}, u32[]{:S(2)}, u32[]{:S(2)}) async-start(f32[32,12,128]{2,1,0:T(8,128)} %copy.180), calls=%async_computation.1 | async-start | bytes 524288 | tf_op jit(solution)/shard_map/while/body/eval_jaxpr/all_to_all | solution.py:227
  88.1 11.1 %all-to-all-start = ((bf16[32,12,128]{2,1,0:T(8,128)(2,1)}), bf16[32,12,128]{2,1,0:T(8,128)(2,1)S(1)}, u32[]{:S(2)}, u32[]{:S(2)}) async-start(bf16[32,12,128]{2,1,0:T(8,128)(2,1)} %copy.174), calls=%async_computation | async-start | bytes 262144 | tf_op jit(solution)/shard_map/while/body/eval_jaxpr/all_to_all | solution.py:216
  111.9 12.8 %all-to-all-start.1 = ((f32[32,12,128]{2,1,0:T(8,128)}), f32[32,12,128]{2,1,0:T(8,128)S(1)}, u32[]{:S(2)}, u32[]{:S(2)}) async-start(f32[32,12,128]{2,1,0:T(8,128)} %copy.180), calls=%async_computation.1 | async-start | bytes 524288 | tf_op jit(solution)/shard_map/while/body/eval_jaxpr/all_to_all | solution.py:227
  149.0 11.1 %all-to-all-start = ((bf16[32,12,128]{2,1,0:T(8,128)(2,1)}), bf16[32,12,128]{2,1,0:T(8,128)(2,1)S(1)}, u32[]{:S(2)}, u32[]{:S(2)}) async-start(bf16[32,12,128]{2,1,0:T(8,128)(2,1)} %copy.174), calls=%async_computation | async-start | bytes 262144 | tf_op jit(solution)/shard_map/while/body/eval_jaxpr/all_to_all | solution.py:216
  172.9 12.8 %all-to-all-start.1 = ((f32[32,12,128]{2,1,0:T(8,128)}), f32[32,12,128]{2,1,0:T(8,128)S(1)}, u32[]{:S(2)}, u32[]{:S(2)}) async-start(f32[32,12,128]{2,1,0:T(8,128)} %copy.180), calls=%async_computation.1 | async-start | bytes 524288 | tf_op jit(solution)/shard_map/while/body/eval_jaxpr/all_to_all | solution.py:227
  214.6 2.7 %copy-start.5 = (f32[4]{0:T(128)}, f32[4]{0:T(128)S(1)}, u32[]{:S(2)}) copy-start(f32[4]{0:T(128)S(1)} %add_sqrt_fusion) | copy-start | bytes 52

commit v2 on v0

--- a/solution.py
+++ b/solution.py
@@ -52,7 +52,7 @@
     stacked = jnp.concatenate([div_real, -div_imag], axis=0).reshape(pairs, items * lays * rows)
     lhs = jnp.concatenate([stacked, stacked], axis=0).T
     tabs = jnp.concatenate([tables_upper, tables_lower], axis=0)
-    block = 1024
+    block = 2048
     mixed = items * lays * rows
     hi_part, lo_part = pl.pallas_call(
         functools.partial(tide_kernel, items * lays, pairs, rows),

time: 199 us -> 198 us (level)
  no operation moved by 1% of the time
where the time goes in v2:
time: 198 us; the launch traced here: 197 us
  waiting for transfers between devices  50.8 us (26%)
  matrix products  49.5 us (25%)
  other arithmetic  25.2 us (13%)
  Pallas kernels  22 us (11%)
  starting transfers between devices  20.4 us (10%)
  local copies, waits for them, and re-layouts  17 us (9%)
  blocking collectives  9.67 us (5%)
    all_to_all x3, waiting for transfers between devices, one_step(): returned = lax.all_to_all(back, axes, 0, 0, tiled=True)  30.3 us
    pallas_call x3, Pallas kernels, tide_term(): pl.pallas_call(functools.partial(tide_kernel, items * lays, pairs, rows),...  22 us
    all_to_all x3, waiting for transfers between devices, one_step(): received = lax.all_to_all(sent, axes, 0, 0, tiled=True)  20.4 us
    dot_general x3, matrix products, one_step(): jnp.einsum('svcj,slj->svcl', spectral_b, legendre, preferred_element_type...  18.1 us
    dot_general x3, matrix products, one_step(): jnp.einsum('svcl,slj->svcj', weighted, legendre, preferred_element_type=j...  15.9 us
    all_to_all x3, starting transfers between devices, one_step(): received = lax.all_to_all(sent, axes, 0, 0, tiled=True)  12.7 us
    all_to_all x1, blocking collectives, exchange_sum(): gathered = lax.all_to_all(rows, ('lat', 'wave'), 0, 0, tiled=True)  9.67 us
    all_to_all x3, starting transfers between devices, one_step(): returned = lax.all_to_all(back, axes, 0, 0, tiled=True)  7.76 us
  transfers between devices with their start and end apart: 6, of which 6 were waited for; matrix products, arithmetic and copies ran while one was open for 2% of the time, Pallas kernels for 0%

profile of v2, /device:TPU:0, one launch (start us, length us, event | category | flops | bytes accessed | tf_op | source)
XLA Modules:
  0.0 197.3 jit_solution(17898034595868220348)
XLA Ops:
  0.7 2.8 %fusion.52 = (f32[32,4096]{1,0:T(8,128)S(1)}, f32[32,4096]{1,0:T(8,128)S(1)}) fusion(s32[32]{0:T(128)} %param.15), kind=kLoop, calls=%fused_computation.83 | loop fusion | flops 1835008 | bytes 1048704 | tf_op jit(solution)/shard_map/cos | solution.py:21
  3.6 1.2 dynamic_slice.3
  5.5 0.7 fusion.54
  6.2 1.2 broadcast_multiply_fusion.2
  7.4 0.7 multiply_add_fusion.1
  8.1 0.8 negate_bitcast_fusion
  8.9 1.1 pad_maximum_fusion.3
  10.0 167.9 %while.13 = (s32[]{:T(128)}, f32[1,4,18,2048]{3,1,2,0:T(4,128)S(1)}, f32[2048]{0:T(1024)S(1)}, f32[1,1,3,2048]{3,2,1,0:T(4,128)S(1)}, bf16[1,2048,2048]{2,1,0:T(...) while((s32[]{:T(128)}, ...), condition=%wide.region_1.2_spmd.clone, body=%wide.region_0.1_spmd.clone.sunk | while | flops 3231582208 | bytes 42901892 | solution.py:229
  10.3 6.0 %fusion.93 = bf16[4,18,2048]{2,1,0:T(8,128)(2,1)S(1)} fusion(bf16[1,2048,2048]{2,1,0:T(8,128)(2,1)} %get-tuple-element.426, bf16[4,18,2048]{2,0,1:T(4,128)(2,1)S(1)} %convert_bitcast_fusion.2), kind=kOutput, calls=%fused_computation.8.clone.1 | convolution fusion | flops 604127232 | bytes 8978432 | tf_op jit(solution)/shard_map/while/body/eval_jaxpr/svcj,slj->svcl/dot_general | solution.py:182
  17.2 0.7 copy.160
  17.9 7.3 %all-to-all-start = ((bf16[32,12,128]{2,1,0:T(8,128)(2,1)}), bf16[32,12,128]{2,1,0:T(8,128)(2,1)S(1)}, u32[]{:S(2)}, u32[]{:S(2)}) async-start(bf16[32,12,128]{2,1,0:T(8,128)(2,1)} %copy.160), calls=%async_computation | async-start | bytes 262144 | tf_op jit(solution)/shard_map/while/body/eval_jaxpr/all_to_all | solution.py:187
  25.5 0.7 fusion.100
  26.1 0.7 compare_convert_fusion.2
  26.8 6.8 %all-to-all-done = bf16[32,12,128]{2,1,0:T(8,128)(2,1)S(1)} async-done(((bf16[32,12,128]{2,1,0:T(8,128)(2,1)}), bf16[32,12,128]{2,1,0:T(8,128)(2,1)S(1)}, u32[]{:S(2)}, u32[]{:S(2)}) %all-to-all-start) | async-done | bytes 98336 | tf_op jit(solution)/shard_map/while/body/eval_jaxpr/all_to_all | solution.py:187
  34.5 0.9 maximum_bitcast_fusion.2.lhs_ref
  35.4 7.3 %eval_jaxpr.3 = (f32[768,128]{1,0:T(8,128)}, f32[768,64]{1,0:T(8,128)}) custom-call(bf16[768,128]{1,0:T(8,128)(2,1)} %maximum_bitcast_fusion.2.lhs_ref, bf16[128,4096]{1,0:T(8,128)(2,1)} %get-tuple-element.430.tab_ref, f32[64,4096]{1,0:T(8,128)} %get-tuple-element.431.tide_ref), custom_call_target="tpu_custom_call" | custom-call | flops 2013265920 | bytes 2686976 | tf_op jit(solution)/shard_map/while/body/eval_jaxpr/pallas_call | solution.py:57
  42.8 1.4 multiply_bitcast_fusion.2
  45.4 0.8 copy.166
  46.2 2.6 %all-to-all-start.1 = ((f32[32,12,128]{2,1,0:T(8,128)}), f32[32,12,128]{2,1,0:T(8,128)S(1)}, u32[]{:S(2)}, u32[]{:S(2)}) async-start(f32[32,12,128]{2,1,0:T(8,128)} %copy.166), calls=%async_computation.1 | async-start | bytes 524288 | tf_op jit(solution)/shard_map/while/body/eval_jaxpr/all_to_all | solution.py:198
  48.9 10.1 %all-to-all-done.1 = f32[32,12,128]{2,1,0:T(8,128)S(1)} async-done(((f32[32,12,128]{2,1,0:T(8,128)}), f32[32,12,128]{2,1,0:T(8,128)S(1)}, u32[]{:S(2)}, u32[]{:S(2)}) %all-to-all-start.1) | async-done | bytes 196640 | tf_op jit(solution)/shard_map/while/body/eval_jaxpr/all_to_all | solution.py:198
  59.8 5.3 %fusion.98 = f32[1,4,18,2048]{3,2,1,0:T(8,128)S(1)} fusion(bf16[1,2048,2048]{2,1,0:T(8,128)(2,1)} %get-tuple-element.426, f32[1,4,18,2048]{3,1,2,0:T(4,128)S(1)} %get-tuple-element.407, bf16[4,18,2048]{2,0,1:T(4,128)(2,1)S(1)} %bitcast.205, f32[2048]{0:T(1024)S(1)} %bitcast.220), kind=kOutput, calls=%fused_computation.7.clone.1 | convolution fusion | flops 604274688 | bytes 9871360 | tf_op jit(solution)/shard_map/while/body/eval_jaxpr/svcl,slj->svcj/dot_general | solution.py:216
  65.6 0.7 convolution_bitcast_fusion.11
  66.2 0.7 fusion.101
  66.9 0.7 convolution_bitcast_fusion.12
  67.6 0.6 convolution_bitcast_fusion.13
  69.2 6.0 %fusion.93 = bf16[4,18,2048]{2,1,0:T(8,128)(2,1)S(1)} fusion(bf16[1,2048,2048]{2,1,0:T(8,128)(2,1)} %get-tuple-element.426, bf16[4,18,2048]{2,0,1:T(4,128)(2,1)S(1)} %convert_bitcast_fusion.2), kind=kOutput, calls=%fused_computation.8.clone.1 | convolution fusion | flops 604127232 | bytes 8978432 | tf_op jit(solution)/shard_map/while/body/eval_jaxpr/svcj,slj->svcl/dot_general | solution.py:182
  76.1 0.7 copy.160
  76.8 2.7 %all-to-all-start = ((bf16[32,12,128]{2,1,0:T(8,128)(2,1)}), bf16[32,12,128]{2,1,0:T(8,128)(2,1)S(1)}, u32[]{:S(2)}, u32[]{:S(2)}) async-start(bf16[32,12,128]{2,1,0:T(8,128)(2,1)} %copy.160), calls=%async_computation | async-start | bytes 262144 | tf_op jit(solution)/shard_map/while/body/eval_jaxpr/all_to_all | solution.py:187
  79.8 0.7 fusion.100
  80.4 0.7 compare_convert_fusion.2
  81.1 6.8 %all-to-all-done = bf16[32,12,128]{2,1,0:T(8,128)(2,1)S(1)} async-done(((bf16[32,12,128]{2,1,0:T(8,128)(2,1)}), bf16[32,12,128]{2,1,0:T(8,128)(2,1)S(1)}, u32[]{:S(2)}, u32[]{:S(2)}) %all-to-all-start) | async-done | bytes 98336 | tf_op jit(solution)/shard_map/while/body/eval_jaxpr/all_to_all | solution.py:187
  88.8 0.9 maximum_bitcast_fusion.2.lhs_ref
  89.7 7.3 %eval_jaxpr.3 = (f32[768,128]{1,0:T(8,128)}, f32[768,64]{1,0:T(8,128)}) custom-call(bf16[768,128]{1,0:T(8,128)(2,1)} %maximum_bitcast_fusion.2.lhs_ref, bf16[128,4096]{1,0:T(8,128)(2,1)} %get-tuple-element.430.tab_ref, f32[64,4096]{1,0:T(8,128)} %get-tuple-element.431.tide_ref), custom_call_target="tpu_custom_call" | custom-call | flops 2013265920 | bytes 2686976 | tf_op jit(solution)/shard_map/while/body/eval_jaxpr/pallas_call | solution.py:57
  97.1 1.4 multiply_bitcast_fusion.2
  99.7 0.8 copy.166
  100.5 2.6 %all-to-all-start.1 = ((f32[32,12,128]{2,1,0:T(8,128)}), f32[32,12,128]{2,1,0:T(8,128)S(1)}, u32[]{:S(2)}, u32[]{:S(2)}) async-start(f32[32,12,128]{2,1,0:T(8,128)} %copy.166), calls=%async_computation.1 | async-start | bytes 524288 | tf_op jit(solution)/shard_map/while/body/eval_jaxpr/all_to_all | solution.py:198
  103.2 10.1 %all-to-all-done.1 = f32[32,12,128]{2,1,0:T(8,128)S(1)} async-done(((f32[32,12,128]{2,1,0:T(8,128)}), f32[32,12,128]{2,1,0:T(8,128)S(1)}, u32[]{:S(2)}, u32[]{:S(2)}) %all-to-all-start.1) | async-done | bytes 196640 | tf_op jit(solution)/shard_map/while/body/eval_jaxpr/all_to_all | solution.py:198
  114.1 5.3 %fusion.98 = f32[1,4,18,2048]{3,2,1,0:T(8,128)S(1)} fusion(bf16[1,2048,2048]{2,1,0:T(8,128)(2,1)} %get-tuple-element.426, f32[1,4,18,2048]{3,1,2,0:T(4,128)S(1)} %get-tuple-element.407, bf16[4,18,2048]{2,0,1:T(4,128)(2,1)S(1)} %bitcast.205, f32[2048]{0:T(1024)S(1)} %bitcast.220), kind=kOutput, calls=%fused_computation.7.clone.1 | convolution fusion | flops 604274688 | bytes 9871360 | tf_op jit(solution)/shard_map/while/body/eval_jaxpr/svcl,slj->svcj/dot_general | solution.py:216
  119.9 0.7 convolution_bitcast_fusion.11
  120.5 0.7 fusion.101
  121.3 0.7 convolution_bitcast_fusion.12
  121.9 0.6 convolution_bitcast_fusion.13
  123.5 6.0 %fusion.93 = bf16[4,18,2048]{2,1,0:T(8,128)(2,1)S(1)} fusion(bf16[1,2048,2048]{2,1,0:T(8,128)(2,1)} %get-tuple-element.426, bf16[4,18,2048]{2,0,1:T(4,128)(2,1)S(1)} %convert_bitcast_fusion.2), kind=kOutput, calls=%fused_computation.8.clone.1 | convolution fusion | flops 604127232 | bytes 8978432 | tf_op jit(solution)/shard_map/while/body/eval_jaxpr/svcj,slj->svcl/dot_general | solution.py:182
  130.4 0.7 copy.160
  131.1 2.7 %all-to-all-start = ((bf16[32,12,128]{2,1,0:T(8,128)(2,1)}), bf16[32,12,128]{2,1,0:T(8,128)(2,1)S(1)}, u32[]{:S(2)}, u32[]{:S(2)}) async-start(bf16[32,12,128]{2,1,0:T(8,128)(2,1)} %copy.160), calls=%async_computation | async-start | bytes 262144 | tf_op jit(solution)/shard_map/while/body/eval_jaxpr/all_to_all | solution.py:187
  134.1 0.7 fusion.100
  134.7 0.7 compare_convert_fusion.2
  135.4 6.8 %all-to-all-done = bf16[32,12,128]{2,1,0:T(8,128)(2,1)S(1)} async-done(((bf16[32,12,128]{2,1,0:T(8,128)(2,1)}), bf16[32,12,128]{2,1,0:T(8,128)(2,1)S(1)}, u32[]{:S(2)}, u32[]{:S(2)}) %all-to-all-start) | async-done | bytes 98336 | tf_op jit(solution)/shard_map/while/body/eval_jaxpr/all_to_all | solution.py:187
  143.1 0.9 maximum_bitcast_fusion.2.lhs_ref
  144.0 7.3 %eval_jaxpr.3 = (f32[768,128]{1,0:T(8,128)}, f32[768,64]{1,0:T(8,128)}) custom-call(bf16[768,128]{1,0:T(8,128)(2,1)} %maximum_bitcast_fusion.2.lhs_ref, bf16[128,4096]{1,0:T(8,128)(2,1)} %get-tuple-element.430.tab_ref, f32[64,4096]{1,0:T(8,128)} %get-tuple-element.431.tide_ref), custom_call_target="tpu_custom_call" | custom-call | flops 2013265920 | bytes 2686976 | tf_op jit(solution)/shard_map/while/body/eval_jaxpr/pallas_call | solution.py:57
  151.4 1.4 multiply_bitcast_fusion.2
  154.0 0.8 copy.166
  154.8 2.6 %all-to-all-start.1 = ((f32[32,12,128]{2,1,0:T(8,128)}), f32[32,12,128]{2,1,0:T(8,128)S(1)}, u32[]{:S(2)}, u32[]{:S(2)}) async-start(f32[32,12,128]{2,1,0:T(8,128)} %copy.166), calls=%async_computation.1 | async-start | bytes 524288 | tf_op jit(solution)/shard_map/while/body/eval_jaxpr/all_to_all | solution.py:198
  157.5 10.1 %all-to-all-done.1 = f32[32,12,128]{2,1,0:T(8,128)S(1)} async-done(((f32[32,12,128]{2,1,0:T(8,128)}), f32[32,12,128]{2,1,0:T(8,128)S(1)}, u32[]{:S(2)}, u32[]{:S(2)}) %all-to-all-start.1) | async-done | bytes 196640 | tf_op jit(solution)/shard_map/while/body/eval_jaxpr/all_to_all | solution.py:198
  168.4 5.3 %fusion.98 = f32[1,4,18,2048]{3,2,1,0:T(8,128)S(1)} fusion(bf16[1,2048,2048]{2,1,0:T(8,128)(2,1)} %get-tuple-element.426, f32[1,4,18,2048]{3,1,2,0:T(4,128)S(1)} %get-tuple-element.407, bf16[4,18,2048]{2,0,1:T(4,128)(2,1)S(1)} %bitcast.205, f32[2048]{0:T(1024)S(1)} %bitcast.220), kind=kOutput, calls=%fused_computation.7.clone.1 | convolution fusion | flops 604274688 | bytes 9871360 | tf_op jit(solution)/shard_map/while/body/eval_jaxpr/svcl,slj->svcj/dot_general | solution.py:216
  174.2 0.7 convolution_bitcast_fusion.11
  174.8 0.7 fusion.101
  175.5 0.7 convolution_bitcast_fusion.12
  176.2 0.6 convolution_bitcast_fusion.13
  177.9 2.7 %convolution_bitcast_fusion.7 = f32[4,4]{1,0:T(4,128)S(1)} fusion(f32[1,4,18,2048]{3,1,2,0:T(4,128)S(1)} %get-tuple-element.178, f32[1,4,18,2048]{3,1,2,0:T(4,128)S(1)} %broadcast_multiply_fusion.2), kind=kOutput, calls=%fused_computation.61 | convolution fusion | flops 7077888 | bytes 1179712 | tf_op jit(solution)/shard_map/skcj,svcj->kv/dot_general | solution.py:231
  181.1 2.8 %convolution_bitcast_fusion.6 = f32[4,4]{1,0:T(4,128)S(1)} fusion(f32[1,4,18,2048]{3,1,2,0:T(4,128)S(1)} %broadcast_multiply_fusion.2), kind=kOutput, calls=%fused_computation.60 | convolution fusion | flops 7077888 | bytes 589888 | tf_op jit(solution)/shard_map/skcj,sqcj->kq/dot_general | solution.py:233
  184.1 9.7 %all_to_all.24 = f32[32,1,36]{2,1,0:T(1,128)S(1)} all-to-all(f32[32,1,36]{2,1,0:T(1,128)S(1)} %broadcast_in_dim.2), channel_id=1, replica_groups=mesh['lat'=8,'wave'=4] {'lat','wave'}, dimensions={0} | all-to-all | bytes 9216 | tf_op jit(solution)/shard_map/all_to_all | solution.py:127
  194.7 2.0 %fusion.37 = f32[1,4,18,2048]{3,1,2,0:T(4,128)} fusion(f32[1,4,18,2048]{3,1,2,0:T(4,128)S(1)} %get-tuple-element.178, f32[1,4,18,2048]{3,1,2,0:T(4,128)S(1)} %broadcast_multiply_fusion.2, f32[4]{0:T(128)S(1)} %add_sqrt_fusion, f32[4,4]{0,1:T(4,128)S(1)} %copy.109), kind=kOutput, calls=%fused_computation.57 | convolution fusion | flops 7372816 | bytes 1769552 | tf_op jit(solution)/shard_map/skcj,kv->svcj/dot_general | solution.py:236
  196.7 0.7 copy.111
  (134 shorter events, 17.8 us)
Async XLA Ops:
  0.6 9.3 %copy-start.1 = (f32[2048]{0:T(1024)S(1)}, f32[2048]{0:T(1024)}, u32[]{:S(2)}) copy-start(f32[2048]{0:T(1024)} %param.17) | copy-start | bytes 24580
  0.6 9.3 %copy-start = (f32[3,2048]{1,0:T(4,128)S(1)}, f32[3,2048]{1,0:T(4,128)}, u32[]{:S(2)}) copy-start(f32[3,2048]{1,0:T(4,128)} %param.19) | copy-start | bytes 73732
  0.7 9.3 %copy-start.2 = (f32[3,3]{1,0:T(4,128)S(1)}, f32[3,3]{1,0:T(4,128)}, u32[]{:S(2)}) copy-start(f32[3,3]{1,0:T(4,128)} %param.21) | copy-start | bytes 112
  0.7 9.3 %copy-start.3 = (f32[3,3]{1,0:T(4,128)S(1)}, f32[3,3]{1,0:T(4,128)}, u32[]{:S(2)}) copy-start(f32[3,3]{1,0:T(4,128)} %param.22) | copy-start | bytes 112
  0.7 9.3 %copy-start.4 = (f32[3]{0:T(128)S(1)}, f32[3]{0:T(128)}, u32[]{:S(2)}) copy-start(f32[3]{0:T(128)} %param.23) | copy-start | bytes 40
  17.9 15.7 %all-to-all-start = ((bf16[32,12,128]{2,1,0:T(8,128)(2,1)}), bf16[32,12,128]{2,1,0:T(8,128)(2,1)S(1)}, u32[]{:S(2)}, u32[]{:S(2)}) async-start(bf16[32,12,128]{2,1,0:T(8,128)(2,1)} %copy.160), calls=%async_computation | async-start | bytes 262144 | tf_op jit(solution)/shard_map/while/body/eval_jaxpr/all_to_all | solution.py:187
  46.2 12.8 %all-to-all-start.1 = ((f32[32,12,128]{2,1,0:T(8,128)}), f32[32,12,128]{2,1,0:T(8,128)S(1)}, u32[]{:S(2)}, u32[]{:S(2)}) async-start(f32[32,12,128]{2,1,0:T(8,128)} %copy.166), calls=%async_computation.1 | async-start | bytes 524288 | tf_op jit(solution)/shard_map/while/body/eval_jaxpr/all_to_all | solution.py:198
  76.8 11.1 %all-to-all-start = ((bf16[32,12,128]{2,1,0:T(8,128)(2,1)}), bf16[32,12,128]{2,1,0:T(8,128)(2,1)S(1)}, u32[]{:S(2)}, u32[]{:S(2)}) async-start(bf16[32,12,128]{2,1,0:T(8,128)(2,1)} %copy.160), calls=%async_computation | async-start | bytes 262144 | tf_op jit(solution)/shard_map/while/body/eval_jaxpr/all_to_all | solution.py:187
  100.5 12.8 %all-to-all-start.1 = ((f32[32,12,128]{2,1,0:T(8,128)}), f32[32,12,128]{2,1,0:T(8,128)S(1)}, u32[]{:S(2)}, u32[]{:S(2)}) async-start(f32[32,12,128]{2,1,0:T(8,128)} %copy.166), calls=%async_computation.1 | async-start | bytes 524288 | tf_op jit(solution)/shard_map/while/body/eval_jaxpr/all_to_all | solution.py:198
  131.1 11.1 %all-to-all-start = ((bf16[32,12,128]{2,1,0:T(8,128)(2,1)}), bf16[32,12,128]{2,1,0:T(8,128)(2,1)S(1)}, u32[]{:S(2)}, u32[]{:S(2)}) async-start(bf16[32,12,128]{2,1,0:T(8,128)(2,1)} %copy.160), calls=%async_computation | async-start | bytes 262144 | tf_op jit(solution)/shard_map/while/body/eval_jaxpr/all_to_all | solution.py:187
  154.8 12.8 %all-to-all-start.1 = ((f32[32,12,128]{2,1,0:T(8,128)}), f32[32,12,128]{2,1,0:T(8,128)S(1)}, u32[]{:S(2)}, u32[]{:S(2)}) async-start(f32[32,12,128]{2,1,0:T(8,128)} %copy.166), calls=%async_computation.1 | async-start | bytes 524288 | tf_op jit(solution)/shard_map/while/body/eval_jaxpr/all_to_all | solution.py:198
  194.7 2.7 %copy-start.5 = (f32[4]{0:T(128)}, f32[4]{0:T(128)S(1)}, u32[]{:S(2)}) copy-start(f32[4]{0:T(128)S(1)} %add_sqrt_fusion) | copy-start | bytes 52

commit v3 on v2

--- a/solution.py
+++ b/solution.py
@@ -101,24 +101,35 @@
     return jnp.stack(parts, axis=3)
 
 
+def mix(matrix, parts):
+    return [
+        sum(matrix[row, col] * parts[col] for col in range(len(parts)))
+        for row in range(matrix.shape[0])
+    ]
+
+
 def implicit_step(explicit, wave_ids, mode_to_layer, layer_to_mode, mode_speed, ntrunc):
     degrees = wave_ids[:, None] + jnp.arange(explicit.shape[-1], dtype=jnp.int32)[None, :]
     degree_f = degrees.astype(jnp.float32)
-    laplace = (degree_f * (degree_f + 1.0) / float(ntrunc * ntrunc))[:, None, None, None, :]
-    speeds = mode_speed[None, None, :, None, None]
-    div_modes = jnp.einsum(
-        "pk,svkrj->svprj", layer_to_mode, explicit[:, :, :, 2:4, :], precision=HIGHEST_PRECISION
-    )
-    height_modes = jnp.einsum(
-        "pk,svkrj->svprj", layer_to_mode, explicit[:, :, :, 4:6, :], precision=HIGHEST_PRECISION
-    )
-    div_new = (div_modes + laplace * speeds * height_modes) / (1.0 + laplace * speeds * speeds)
-    height_new = height_modes - speeds * div_new
-    div_layers = jnp.einsum("kp,svprj->svkrj", mode_to_layer, div_new, precision=HIGHEST_PRECISION)
-    height_layers = jnp.einsum(
-        "kp,svprj->svkrj", mode_to_layer, height_new, precision=HIGHEST_PRECISION
-    )
-    return jnp.concatenate([explicit[:, :, :, 0:2, :], div_layers, height_layers], axis=3)
+    laplace = (degree_f * (degree_f + 1.0) / float(ntrunc * ntrunc))[:, None, None, :]
+    layers = mode_speed.shape[0]
+    div_in = [explicit[:, :, k, 2:4, :] for k in range(layers)]
+    height_in = [explicit[:, :, k, 4:6, :] for k in range(layers)]
+    div_modes = mix(layer_to_mode, div_in)
+    height_modes = mix(layer_to_mode, height_in)
+    div_new, height_new = [], []
+    for p in range(layers):
+        speed = mode_speed[p]
+        div_p = (div_modes[p] + laplace * speed * height_modes[p]) / (1.0 + laplace * speed * speed)
+        div_new.append(div_p)
+        height_new.append(height_modes[p] - speed * div_p)
+    div_layers = mix(mode_to_layer, div_new)
+    height_layers = mix(mode_to_layer, height_new)
+    out = [
+        jnp.concatenate([explicit[:, :, k, 0:2, :], div_layers[k], height_layers[k]], axis=2)
+        for k in range(layers)
+    ]
+    return jnp.stack(out, axis=2)
 
 
 def exchange_sum(parts, device_count):

time: 198 us -> 271 us (1.37)
  other arithmetic: 25.2 us -> 108 us
  waiting for transfers between devices: 50.8 us -> 37.3 us
  matrix products: 49.5 us -> 42 us
  local copies, waits for them, and re-layouts: 17 us -> 20.9 us
  starting transfers between devices: 20.4 us -> 23.4 us
    add x0 -> x18, other arithmetic: none -> 83.1 us  [the longest x12 73.5 us: mix(): sum((matrix[row, col] * parts[col] for col in range(len(parts))))]
    all_to_all x3, waiting for transfers between devices: 20.4 us -> 6.86 us  [one_step(): received = lax.all_to_all(sent, axes, 0, 0, tiled=True)]
    dot_general x12 -> x0, matrix products: 7.81 us -> none  [the longest x3 2.09 us: implicit_step(): jnp.einsum('pk,svkrj->svprj', layer_to_mode, explicit[:, :, :, 2:4, :], p...]
    slice x3 -> x7, local copies, waits for them, and re-layouts: 0.12 us -> 5.52 us  [the longest x4 3.4 us: implicit_step(): speed = mode_speed[p]]
    all_to_all x3, starting transfers between devices: 7.76 us -> 10.7 us  [one_step(): returned = lax.all_to_all(back, axes, 0, 0, tiled=True)]
  transfers between devices with their start and end apart: 6 -> 6, of which waited for: 6 -> 6; matrix products, arithmetic and copies ran while one was open for 2% -> 7% of each run, Pallas kernels for 0% -> 0%
where the time goes in v3:
time: 271 us; the launch traced here: 268 us
  other arithmetic  108 us (40%)
  matrix products  42 us (15%)
  waiting for transfers between devices  37.3 us (14%)
  starting transfers between devices  23.4 us (9%)
  Pallas kernels  22 us (8%)
  local copies, waits for them, and re-layouts  20.9 us (8%)
  blocking collectives  9.71 us (4%)
  between operations  3.34 us (1%)
    add x12, other arithmetic, mix(): sum((matrix[row, col] * parts[col] for col in range(len(parts))))  73.5 us
    all_to_all x3, waiting for transfers between devices, one_step(): returned = lax.all_to_all(back, axes, 0, 0, tiled=True)  30.4 us
    pallas_call x3, Pallas kernels, tide_term(): pl.pallas_call(functools.partial(tide_kernel, items * lays, pairs, rows),...  22 us
    dot_general x3, matrix products, one_step(): jnp.einsum('svcj,slj->svcl', spectral_b, legendre, preferred_element_type...  18.1 us
    dot_general x3, matrix products, one_step(): jnp.einsum('svcl,slj->svcj', weighted, legendre, preferred_element_type=j...  16.1 us
    all_to_all x3, starting transfers between devices, one_step(): received = lax.all_to_all(sent, axes, 0, 0, tiled=True)  12.7 us
    all_to_all x3, starting transfers between devices, one_step(): returned = lax.all_to_all(back, axes, 0, 0, tiled=True)  10.7 us
    all_to_all x1, blocking collectives, exchange_sum(): gathered = lax.all_to_all(rows, ('lat', 'wave'), 0, 0, tiled=True)  9.71 us
  transfers between devices with their start and end apart: 6, of which 6 were waited for; matrix products, arithmetic and copies ran while one was open for 7% of the time, Pallas kernels for 0%

profile of v3, /device:TPU:0, one launch (start us, length us, event | category | flops | bytes accessed | tf_op | source)
XLA Modules:
  0.0 268.4 jit_solution(1065719836997799922)
XLA Ops:
  0.7 2.8 %fusion.49 = (f32[32,4096]{1,0:T(8,128)S(1)}, f32[32,4096]{1,0:T(8,128)S(1)}) fusion(s32[32]{0:T(128)} %param.15), kind=kLoop, calls=%fused_computation.96 | loop fusion | flops 1835008 | bytes 1048704 | tf_op jit(solution)/shard_map/cos | solution.py:21
  3.7 1.2 dynamic_slice.3
  6.2 1.2 broadcast_multiply_fusion.1
  7.4 1.4 fusion.65
  10.8 0.7 multiply_add_fusion.12
  11.5 0.8 negate_bitcast_fusion
  12.3 1.1 pad_maximum_fusion.3
  13.4 235.6 %while.14 = (s32[]{:T(128)}, f32[1,4,18,2048]{3,1,2,0:T(4,128)S(1)}, f32[2048]{0:T(1024)S(1)}, f32[1,1,3,2048]{3,2,1,0:T(4,128)S(1)}, bf16[1,2048,2048]{2,1,0:T(...) while((s32[]{:T(128)}, ...), condition=%wide.region_1.2_spmd.clone, body=%wide.region_0.1_spmd.clone.sunk | while | flops 3226048512 | bytes 41706084 | solution.py:240
  13.7 6.0 %fusion.86 = bf16[4,18,2048]{2,1,0:T(8,128)(2,1)S(1)} fusion(bf16[1,2048,2048]{2,1,0:T(8,128)(2,1)} %get-tuple-element.659, bf16[4,18,2048]{2,0,1:T(4,128)(2,1)S(1)} %convert_bitcast_fusion.2), kind=kOutput, calls=%fused_computation.8.clone.1 | convolution fusion | flops 604127232 | bytes 8978432 | tf_op jit(solution)/shard_map/while/body/eval_jaxpr/svcj,slj->svcl/dot_general | solution.py:193
  21.3 7.3 %all-to-all-start = ((bf16[32,12,128]{2,1,0:T(8,128)(2,1)}), bf16[32,12,128]{2,1,0:T(8,128)(2,1)S(1)}, u32[]{:S(2)}, u32[]{:S(2)}) async-start(bf16[32,12,128]{2,1,0:T(8,128)(2,1)} %copy.135), calls=%async_computation | async-start | bytes 262144 | tf_op jit(solution)/shard_map/while/body/eval_jaxpr/all_to_all | solution.py:198
  29.5 0.7 fusion.84
  30.8 1.2 multiply_add_fusion.19
  32.0 2.0 multiply_add_fusion.20
  34.7 2.3 all-to-all-done
  37.9 0.9 maximum_bitcast_fusion.8.lhs_ref
  38.8 7.3 %eval_jaxpr.4 = (f32[768,128]{1,0:T(8,128)}, f32[768,64]{1,0:T(8,128)}) custom-call(bf16[768,128]{1,0:T(8,128)(2,1)} %maximum_bitcast_fusion.8.lhs_ref, bf16[128,4096]{1,0:T(8,128)(2,1)} %get-tuple-element.663.tab_ref, f32[64,4096]{1,0:T(8,128)} %get-tuple-element.664.tide_ref), custom_call_target="tpu_custom_call" | custom-call | flops 2013265920 | bytes 2686976 | tf_op jit(solution)/shard_map/while/body/eval_jaxpr/pallas_call | solution.py:57
  46.2 1.4 multiply_bitcast_fusion.2
  48.8 0.8 copy.141
  49.6 3.6 %all-to-all-start.1 = ((f32[32,12,128]{2,1,0:T(8,128)}), f32[32,12,128]{2,1,0:T(8,128)S(1)}, u32[]{:S(2)}, u32[]{:S(2)}) async-start(f32[32,12,128]{2,1,0:T(8,128)} %copy.141), calls=%async_computation.1 | async-start | bytes 524288 | tf_op jit(solution)/shard_map/while/body/eval_jaxpr/all_to_all | solution.py:209
  53.3 10.1 %all-to-all-done.1 = f32[32,12,128]{2,1,0:T(8,128)S(1)} async-done(((f32[32,12,128]{2,1,0:T(8,128)}), f32[32,12,128]{2,1,0:T(8,128)S(1)}, u32[]{:S(2)}, u32[]{:S(2)}) %all-to-all-start.1) | async-done | bytes 196640 | tf_op jit(solution)/shard_map/while/body/eval_jaxpr/all_to_all | solution.py:209
  64.2 5.4 %fusion.91 = f32[1,4,18,2048]{3,2,1,0:T(8,128)S(1)} fusion(bf16[1,2048,2048]{2,1,0:T(8,128)(2,1)} %get-tuple-element.659, f32[1,4,18,2048]{3,1,2,0:T(4,128)S(1)} %get-tuple-element.637, bf16[4,18,2048]{2,0,1:T(4,128)(2,1)S(1)} %bitcast.289, f32[2048]{0:T(1024)S(1)} %bitcast.314), kind=kOutput, calls=%fused_computation.7.clone.1 | convolution fusion | flops 604274688 | bytes 9871360 | tf_op jit(solution)/shard_map/while/body/eval_jaxpr/svcl,slj->svcj/dot_general | solution.py:227
  70.0 7.5 %multiply_add_fusion.21 = (f32[1,4,2,2048]{3,1,2,0:T(4,128)S(1)}, f32[1,4,2,2048]{3,1,2,0:T(4,128)S(1)}, f32[1,4,2,2048]{3,1,2,0:T(4,128)S(1)}, f32[1,4,2,2048]{3,1,2,0:T(4,128)S(1)}) fusion(f32[]{:T(128)} %bitcast.240, f32[]{:T(128)} %bitcast.241, f32[]{:T(128)} %bitcast.242, f32[2048]{0:T(1024)S(1)} %get-tuple-element.573, ...), kind=kLoop, calls=%fused_computation.56.clone.1 | loop fusion | flops 720896 | bytes 704560 | tf_op jit(solution)/shard_map/while/body/eval_jaxpr/add | solution.py:106
  77.6 9.4 %multiply_add_fusion.22 = (f32[1,4,2,2048]{3,1,2,0:T(4,128)S(1)}, f32[1,4,2,2048]{3,1,2,0:T(4,128)S(1)}, f32[1,4,2,2048]{3,1,2,0:T(4,128)S(1)}, f32[1,4,2,2048]{3,1,2,0:T(4,128)S(1)}) fusion(f32[]{:T(128)} %bitcast.240, f32[]{:T(128)} %bitcast.241, f32[]{:T(128)} %bitcast.242, f32[1,4,2,2048]{3,1,2,0:T(4,128)S(1)} %get-tuple-element.596, ...), kind=kLoop, calls=%fused_computation.55.clone.1 | loop fusion | flops 425984 | bytes 655420 | tf_op jit(solution)/shard_map/while/body/eval_jaxpr/add | solution.py:106
  87.0 3.8 %multiply_add_fusion.24 = (f32[1,8,1,2048]{3,1,2,0:T(8,128)S(1)}, f32[1,8,1,2048]{3,1,2,0:T(8,128)S(1)}) fusion(f32[1,8,1,2048]{3,1,2,0:T(8,128)S(1)} %bitcast.300, f32[1,8,1,2048]{3,1,2,0:T(8,128)S(1)} %bitcast.299, f32[1,8,1,2048]{3,1,2,0:T(8,128)S(1)} %bitcast.298, f32[]{:T(128)} %bitcast.271, f32[]{:T(128)} %bitcast.272, f32[]{:T(128)} %bitcast.273, ...), kind=kLoop, calls=%fused_computation.54.clone.1 | loop fusion | flops 163840 | bytes 327704 | tf_op jit(solution)/shard_map/while/body/eval_jaxpr/add | solution.py:106
  90.8 3.8 %multiply_add_fusion.23 = (f32[1,8,1,2048]{3,1,2,0:T(8,128)S(1)}, f32[1,8,1,2048]{3,1,2,0:T(8,128)S(1)}) fusion(f32[1,8,1,2048]{3,1,2,0:T(8,128)S(1)} %bitcast.309, f32[1,8,1,2048]{3,1,2,0:T(8,128)S(1)} %bitcast.308, f32[1,8,1,2048]{3,1,2,0:T(8,128)S(1)} %bitcast.307, f32[]{:T(128)} %bitcast.271, f32[]{:T(128)} %bitcast.272, f32[]{:T(128)} %bitcast.273, ...), kind=kLoop, calls=%fused_computation.53.clone.1 | loop fusion | flops 163840 | bytes 327704 | tf_op jit(solution)/shard_map/while/body/eval_jaxpr/add | solution.py:106
  95.1 6.0 %fusion.86 = bf16[4,18,2048]{2,1,0:T(8,128)(2,1)S(1)} fusion(bf16[1,2048,2048]{2,1,0:T(8,128)(2,1)} %get-tuple-element.659, bf16[4,18,2048]{2,0,1:T(4,128)(2,1)S(1)} %convert_bitcast_fusion.2), kind=kOutput, calls=%fused_computation.8.clone.1 | convolution fusion | flops 604127232 | bytes 8978432 | tf_op jit(solution)/shard_map/while/body/eval_jaxpr/svcj,slj->svcl/dot_general | solution.py:193
  102.0 0.7 copy.135
  102.7 2.7 %all-to-all-start = ((bf16[32,12,128]{2,1,0:T(8,128)(2,1)}), bf16[32,12,128]{2,1,0:T(8,128)(2,1)S(1)}, u32[]{:S(2)}, u32[]{:S(2)}) async-start(bf16[32,12,128]{2,1,0:T(8,128)(2,1)} %copy.135), calls=%async_computation | async-start | bytes 262144 | tf_op jit(solution)/shard_map/while/body/eval_jaxpr/all_to_all | solution.py:198
  106.3 0.7 fusion.84
  107.7 1.2 multiply_add_fusion.19
  108.9 2.0 multiply_add_fusion.20
  111.6 2.3 all-to-all-done
  114.8 0.9 maximum_bitcast_fusion.8.lhs_ref
  115.7 7.3 %eval_jaxpr.4 = (f32[768,128]{1,0:T(8,128)}, f32[768,64]{1,0:T(8,128)}) custom-call(bf16[768,128]{1,0:T(8,128)(2,1)} %maximum_bitcast_fusion.8.lhs_ref, bf16[128,4096]{1,0:T(8,128)(2,1)} %get-tuple-element.663.tab_ref, f32[64,4096]{1,0:T(8,128)} %get-tuple-element.664.tide_ref), custom_call_target="tpu_custom_call" | custom-call | flops 2013265920 | bytes 2686976 | tf_op jit(solution)/shard_map/while/body/eval_jaxpr/pallas_call | solution.py:57
  123.0 1.4 multiply_bitcast_fusion.2
  125.7 0.8 copy.141
  126.5 3.6 %all-to-all-start.1 = ((f32[32,12,128]{2,1,0:T(8,128)}), f32[32,12,128]{2,1,0:T(8,128)S(1)}, u32[]{:S(2)}, u32[]{:S(2)}) async-start(f32[32,12,128]{2,1,0:T(8,128)} %copy.141), calls=%async_computation.1 | async-start | bytes 524288 | tf_op jit(solution)/shard_map/while/body/eval_jaxpr/all_to_all | solution.py:209
  130.1 10.1 %all-to-all-done.1 = f32[32,12,128]{2,1,0:T(8,128)S(1)} async-done(((f32[32,12,128]{2,1,0:T(8,128)}), f32[32,12,128]{2,1,0:T(8,128)S(1)}, u32[]{:S(2)}, u32[]{:S(2)}) %all-to-all-start.1) | async-done | bytes 196640 | tf_op jit(solution)/shard_map/while/body/eval_jaxpr/all_to_all | solution.py:209
  141.1 5.4 %fusion.91 = f32[1,4,18,2048]{3,2,1,0:T(8,128)S(1)} fusion(bf16[1,2048,2048]{2,1,0:T(8,128)(2,1)} %get-tuple-element.659, f32[1,4,18,2048]{3,1,2,0:T(4,128)S(1)} %get-tuple-element.637, bf16[4,18,2048]{2,0,1:T(4,128)(2,1)S(1)} %bitcast.289, f32[2048]{0:T(1024)S(1)} %bitcast.314), kind=kOutput, calls=%fused_computation.7.clone.1 | convolution fusion | flops 604274688 | bytes 9871360 | tf_op jit(solution)/shard_map/while/body/eval_jaxpr/svcl,slj->svcj/dot_general | solution.py:227
  146.9 7.5 %multiply_add_fusion.21 = (f32[1,4,2,2048]{3,1,2,0:T(4,128)S(1)}, f32[1,4,2,2048]{3,1,2,0:T(4,128)S(1)}, f32[1,4,2,2048]{3,1,2,0:T(4,128)S(1)}, f32[1,4,2,2048]{3,1,2,0:T(4,128)S(1)}) fusion(f32[]{:T(128)} %bitcast.240, f32[]{:T(128)} %bitcast.241, f32[]{:T(128)} %bitcast.242, f32[2048]{0:T(1024)S(1)} %get-tuple-element.573, ...), kind=kLoop, calls=%fused_computation.56.clone.1 | loop fusion | flops 720896 | bytes 704560 | tf_op jit(solution)/shard_map/while/body/eval_jaxpr/add | solution.py:106
  154.4 9.4 %multiply_add_fusion.22 = (f32[1,4,2,2048]{3,1,2,0:T(4,128)S(1)}, f32[1,4,2,2048]{3,1,2,0:T(4,128)S(1)}, f32[1,4,2,2048]{3,1,2,0:T(4,128)S(1)}, f32[1,4,2,2048]{3,1,2,0:T(4,128)S(1)}) fusion(f32[]{:T(128)} %bitcast.240, f32[]{:T(128)} %bitcast.241, f32[]{:T(128)} %bitcast.242, f32[1,4,2,2048]{3,1,2,0:T(4,128)S(1)} %get-tuple-element.596, ...), kind=kLoop, calls=%fused_computation.55.clone.1 | loop fusion | flops 425984 | bytes 655420 | tf_op jit(solution)/shard_map/while/body/eval_jaxpr/add | solution.py:106
  163.9 3.8 %multiply_add_fusion.24 = (f32[1,8,1,2048]{3,1,2,0:T(8,128)S(1)}, f32[1,8,1,2048]{3,1,2,0:T(8,128)S(1)}) fusion(f32[1,8,1,2048]{3,1,2,0:T(8,128)S(1)} %bitcast.300, f32[1,8,1,2048]{3,1,2,0:T(8,128)S(1)} %bitcast.299, f32[1,8,1,2048]{3,1,2,0:T(8,128)S(1)} %bitcast.298, f32[]{:T(128)} %bitcast.271, f32[]{:T(128)} %bitcast.272, f32[]{:T(128)} %bitcast.273, ...), kind=kLoop, calls=%fused_computation.54.clone.1 | loop fusion | flops 163840 | bytes 327704 | tf_op jit(solution)/shard_map/while/body/eval_jaxpr/add | solution.py:106
  167.7 3.8 %multiply_add_fusion.23 = (f32[1,8,1,2048]{3,1,2,0:T(8,128)S(1)}, f32[1,8,1,2048]{3,1,2,0:T(8,128)S(1)}) fusion(f32[1,8,1,2048]{3,1,2,0:T(8,128)S(1)} %bitcast.309, f32[1,8,1,2048]{3,1,2,0:T(8,128)S(1)} %bitcast.308, f32[1,8,1,2048]{3,1,2,0:T(8,128)S(1)} %bitcast.307, f32[]{:T(128)} %bitcast.271, f32[]{:T(128)} %bitcast.272, f32[]{:T(128)} %bitcast.273, ...), kind=kLoop, calls=%fused_computation.53.clone.1 | loop fusion | flops 163840 | bytes 327704 | tf_op jit(solution)/shard_map/while/body/eval_jaxpr/add | solution.py:106
  172.0 6.0 %fusion.86 = bf16[4,18,2048]{2,1,0:T(8,128)(2,1)S(1)} fusion(bf16[1,2048,2048]{2,1,0:T(8,128)(2,1)} %get-tuple-element.659, bf16[4,18,2048]{2,0,1:T(4,128)(2,1)S(1)} %convert_bitcast_fusion.2), kind=kOutput, calls=%fused_computation.8.clone.1 | convolution fusion | flops 604127232 | bytes 8978432 | tf_op jit(solution)/shard_map/while/body/eval_jaxpr/svcj,slj->svcl/dot_general | solution.py:193
  179.6 2.7 %all-to-all-start = ((bf16[32,12,128]{2,1,0:T(8,128)(2,1)}), bf16[32,12,128]{2,1,0:T(8,128)(2,1)S(1)}, u32[]{:S(2)}, u32[]{:S(2)}) async-start(bf16[32,12,128]{2,1,0:T(8,128)(2,1)} %copy.135), calls=%async_computation | async-start | bytes 262144 | tf_op jit(solution)/shard_map/while/body/eval_jaxpr/all_to_all | solution.py:198
  183.2 0.7 fusion.84
  184.6 1.2 multiply_add_fusion.19
  185.8 2.0 multiply_add_fusion.20
  188.4 2.3 all-to-all-done
  191.7 0.9 maximum_bitcast_fusion.8.lhs_ref
  192.6 7.3 %eval_jaxpr.4 = (f32[768,128]{1,0:T(8,128)}, f32[768,64]{1,0:T(8,128)}) custom-call(bf16[768,128]{1,0:T(8,128)(2,1)} %maximum_bitcast_fusion.8.lhs_ref, bf16[128,4096]{1,0:T(8,128)(2,1)} %get-tuple-element.663.tab_ref, f32[64,4096]{1,0:T(8,128)} %get-tuple-element.664.tide_ref), custom_call_target="tpu_custom_call" | custom-call | flops 2013265920 | bytes 2686976 | tf_op jit(solution)/shard_map/while/body/eval_jaxpr/pallas_call | solution.py:57
  199.9 1.4 multiply_bitcast_fusion.2
  202.5 0.8 copy.141
  203.4 3.6 %all-to-all-start.1 = ((f32[32,12,128]{2,1,0:T(8,128)}), f32[32,12,128]{2,1,0:T(8,128)S(1)}, u32[]{:S(2)}, u32[]{:S(2)}) async-start(f32[32,12,128]{2,1,0:T(8,128)} %copy.141), calls=%async_computation.1 | async-start | bytes 524288 | tf_op jit(solution)/shard_map/while/body/eval_jaxpr/all_to_all | solution.py:209
  207.0 10.1 %all-to-all-done.1 = f32[32,12,128]{2,1,0:T(8,128)S(1)} async-done(((f32[32,12,128]{2,1,0:T(8,128)}), f32[32,12,128]{2,1,0:T(8,128)S(1)}, u32[]{:S(2)}, u32[]{:S(2)}) %all-to-all-start.1) | async-done | bytes 196640 | tf_op jit(solution)/shard_map/while/body/eval_jaxpr/all_to_all | solution.py:209
  218.0 5.4 %fusion.91 = f32[1,4,18,2048]{3,2,1,0:T(8,128)S(1)} fusion(bf16[1,2048,2048]{2,1,0:T(8,128)(2,1)} %get-tuple-element.659, f32[1,4,18,2048]{3,1,2,0:T(4,128)S(1)} %get-tuple-element.637, bf16[4,18,2048]{2,0,1:T(4,128)(2,1)S(1)} %bitcast.289, f32[2048]{0:T(1024)S(1)} %bitcast.314), kind=kOutput, calls=%fused_computation.7.clone.1 | convolution fusion | flops 604274688 | bytes 9871360 | tf_op jit(solution)/shard_map/while/body/eval_jaxpr/svcl,slj->svcj/dot_general | solution.py:227
  223.7 7.5 %multiply_add_fusion.21 = (f32[1,4,2,2048]{3,1,2,0:T(4,128)S(1)}, f32[1,4,2,2048]{3,1,2,0:T(4,128)S(1)}, f32[1,4,2,2048]{3,1,2,0:T(4,128)S(1)}, f32[1,4,2,2048]{3,1,2,0:T(4,128)S(1)}) fusion(f32[]{:T(128)} %bitcast.240, f32[]{:T(128)} %bitcast.241, f32[]{:T(128)} %bitcast.242, f32[2048]{0:T(1024)S(1)} %get-tuple-element.573, ...), kind=kLoop, calls=%fused_computation.56.clone.1 | loop fusion | flops 720896 | bytes 704560 | tf_op jit(solution)/shard_map/while/body/eval_jaxpr/add | solution.py:106
  231.3 9.4 %multiply_add_fusion.22 = (f32[1,4,2,2048]{3,1,2,0:T(4,128)S(1)}, f32[1,4,2,2048]{3,1,2,0:T(4,128)S(1)}, f32[1,4,2,2048]{3,1,2,0:T(4,128)S(1)}, f32[1,4,2,2048]{3,1,2,0:T(4,128)S(1)}) fusion(f32[]{:T(128)} %bitcast.240, f32[]{:T(128)} %bitcast.241, f32[]{:T(128)} %bitcast.242, f32[1,4,2,2048]{3,1,2,0:T(4,128)S(1)} %get-tuple-element.596, ...), kind=kLoop, calls=%fused_computation.55.clone.1 | loop fusion | flops 425984 | bytes 655420 | tf_op jit(solution)/shard_map/while/body/eval_jaxpr/add | solution.py:106
  240.7 3.8 %multiply_add_fusion.24 = (f32[1,8,1,2048]{3,1,2,0:T(8,128)S(1)}, f32[1,8,1,2048]{3,1,2,0:T(8,128)S(1)}) fusion(f32[1,8,1,2048]{3,1,2,0:T(8,128)S(1)} %bitcast.300, f32[1,8,1,2048]{3,1,2,0:T(8,128)S(1)} %bitcast.299, f32[1,8,1,2048]{3,1,2,0:T(8,128)S(1)} %bitcast.298, f32[]{:T(128)} %bitcast.271, f32[]{:T(128)} %bitcast.272, f32[]{:T(128)} %bitcast.273, ...), kind=kLoop, calls=%fused_computation.54.clone.1 | loop fusion | flops 163840 | bytes 327704 | tf_op jit(solution)/shard_map/while/body/eval_jaxpr/add | solution.py:106
  244.5 3.8 %multiply_add_fusion.23 = (f32[1,8,1,2048]{3,1,2,0:T(8,128)S(1)}, f32[1,8,1,2048]{3,1,2,0:T(8,128)S(1)}) fusion(f32[1,8,1,2048]{3,1,2,0:T(8,128)S(1)} %bitcast.309, f32[1,8,1,2048]{3,1,2,0:T(8,128)S(1)} %bitcast.308, f32[1,8,1,2048]{3,1,2,0:T(8,128)S(1)} %bitcast.307, f32[]{:T(128)} %bitcast.271, f32[]{:T(128)} %bitcast.272, f32[]{:T(128)} %bitcast.273, ...), kind=kLoop, calls=%fused_computation.53.clone.1 | loop fusion | flops 163840 | bytes 327704 | tf_op jit(solution)/shard_map/while/body/eval_jaxpr/add | solution.py:106
  248.9 2.7 %convolution_bitcast_fusion.3 = f32[4,4]{1,0:T(4,128)S(1)} fusion(f32[1,4,18,2048]{3,1,2,0:T(4,128)S(1)} %get-tuple-element.244, f32[1,4,18,2048]{3,1,2,0:T(4,128)S(1)} %broadcast_multiply_fusion.1), kind=kOutput, calls=%fused_computation.74 | convolution fusion | flops 7077888 | bytes 1179712 | tf_op jit(solution)/shard_map/skcj,svcj->kv/dot_general | solution.py:242
  252.1 2.8 %convolution_bitcast_fusion.2 = f32[4,4]{1,0:T(4,128)S(1)} fusion(f32[1,4,18,2048]{3,1,2,0:T(4,128)S(1)} %broadcast_multiply_fusion.1), kind=kOutput, calls=%fused_computation.73 | convolution fusion | flops 7077888 | bytes 589888 | tf_op jit(solution)/shard_map/skcj,sqcj->kq/dot_general | solution.py:244
  255.2 9.7 %all_to_all.26 = f32[32,1,36]{2,1,0:T(1,128)S(1)} all-to-all(f32[32,1,36]{2,1,0:T(1,128)S(1)} %broadcast_in_dim.2), channel_id=1, replica_groups=mesh['lat'=8,'wave'=4] {'lat','wave'}, dimensions={0} | all-to-all | bytes 9216 | tf_op jit(solution)/shard_map/all_to_all | solution.py:138
  265.7 2.0 fusion.34
  (147 shorter events, 24.9 us)
Async XLA Ops:
  0.6 12.7 %copy-start.4 = (f32[3]{0:T(128)S(1)}, f32[3]{0:T(128)}, u32[]{:S(2)}) copy-start(f32[3]{0:T(128)} %param.23) | copy-start | bytes 40
  0.6 12.7 %copy-start.3 = (f32[2048]{0:T(1024)S(1)}, f32[2048]{0:T(1024)}, u32[]{:S(2)}) copy-start(f32[2048]{0:T(1024)} %param.17) | copy-start | bytes 24580
  0.7 12.7 %copy-start = (f32[3,2048]{1,0:T(4,128)S(1)}, f32[3,2048]{1,0:T(4,128)}, u32[]{:S(2)}) copy-start(f32[3,2048]{1,0:T(4,128)} %param.19) | copy-start | bytes 73732
  0.7 12.7 %copy-start.1 = (f32[3,3]{1,0:T(4,128)S(1)}, f32[3,3]{1,0:T(4,128)}, u32[]{:S(2)}) copy-start(f32[3,3]{1,0:T(4,128)} %param.21) | copy-start | bytes 112
  0.7 12.7 %copy-start.2 = (f32[3,3]{1,0:T(4,128)S(1)}, f32[3,3]{1,0:T(4,128)}, u32[]{:S(2)}) copy-start(f32[3,3]{1,0:T(4,128)} %param.22) | copy-start | bytes 112
  21.3 15.7 %all-to-all-start = ((bf16[32,12,128]{2,1,0:T(8,128)(2,1)}), bf16[32,12,128]{2,1,0:T(8,128)(2,1)S(1)}, u32[]{:S(2)}, u32[]{:S(2)}) async-start(bf16[32,12,128]{2,1,0:T(8,128)(2,1)} %copy.135), calls=%async_computation | async-start | bytes 262144 | tf_op jit(solution)/shard_map/while/body/eval_jaxpr/all_to_all | solution.py:198
  49.6 13.8 %all-to-all-start.1 = ((f32[32,12,128]{2,1,0:T(8,128)}), f32[32,12,128]{2,1,0:T(8,128)S(1)}, u32[]{:S(2)}, u32[]{:S(2)}) async-start(f32[32,12,128]{2,1,0:T(8,128)} %copy.141), calls=%async_computation.1 | async-start | bytes 524288 | tf_op jit(solution)/shard_map/while/body/eval_jaxpr/all_to_all | solution.py:209
  102.7 11.1 %all-to-all-start = ((bf16[32,12,128]{2,1,0:T(8,128)(2,1)}), bf16[32,12,128]{2,1,0:T(8,128)(2,1)S(1)}, u32[]{:S(2)}, u32[]{:S(2)}) async-start(bf16[32,12,128]{2,1,0:T(8,128)(2,1)} %copy.135), calls=%async_computation | async-start | bytes 262144 | tf_op jit(solution)/shard_map/while/body/eval_jaxpr/all_to_all | solution.py:198
  126.5 13.8 %all-to-all-start.1 = ((f32[32,12,128]{2,1,0:T(8,128)}), f32[32,12,128]{2,1,0:T(8,128)S(1)}, u32[]{:S(2)}, u32[]{:S(2)}) async-start(f32[32,12,128]{2,1,0:T(8,128)} %copy.141), calls=%async_computation.1 | async-start | bytes 524288 | tf_op jit(solution)/shard_map/while/body/eval_jaxpr/all_to_all | solution.py:209
  179.6 11.1 %all-to-all-start = ((bf16[32,12,128]{2,1,0:T(8,128)(2,1)}), bf16[32,12,128]{2,1,0:T(8,128)(2,1)S(1)}, u32[]{:S(2)}, u32[]{:S(2)}) async-start(bf16[32,12,128]{2,1,0:T(8,128)(2,1)} %copy.135), calls=%async_computation | async-start | bytes 262144 | tf_op jit(solution)/shard_map/while/body/eval_jaxpr/all_to_all | solution.py:198
  203.4 13.8 %all-to-all-start.1 = ((f32[32,12,128]{2,1,0:T(8,128)}), f32[32,12,128]{2,1,0:T(8,128)S(1)}, u32[]{:S(2)}, u32[]{:S(2)}) async-start(f32[32,12,128]{2,1,0:T(8,128)} %copy.141), calls=%async_computation.1 | async-start | bytes 524288 | tf_op jit(solution)/shard_map/while/body/eval_jaxpr/all_to_all | solution.py:209
  265.7 2.7 copy-start.5

commit v4 on v2

--- a/solution.py
+++ b/solution.py
@@ -228,9 +228,9 @@
 
     spectral = lax.fori_loop(0, STEPS, one_step, basis)
     entries = float(local_slots * device_count * channels * ndeg)
-    local_proj = jnp.einsum("skcj,svcj->kv", basis, spectral, precision=HIGHEST_PRECISION)
+    local_proj = jnp.sum(basis[:, :, None] * spectral[:, None, :], axis=(0, 3, 4))
     local_self = jnp.sum(spectral * spectral, axis=(0, 2, 3))
-    local_gram = jnp.einsum("skcj,sqcj->kq", basis, basis, precision=HIGHEST_PRECISION)
+    local_gram = jnp.sum(basis[:, :, None] * basis[:, None, :], axis=(0, 3, 4))
     projection, self_sum, gram = exchange_sum((local_proj, local_self, local_gram), device_count)
     hessenberg = projection / entries
     residual = spectral - jnp.einsum(

time: 198 us -> 193 us (0.975)
  matrix products: 49.5 us -> 43.7 us
    dot_general x2 -> x0, matrix products: 5.51 us -> none  [the longest x1 2.78 us: on_device(): jnp.einsum('skcj,sqcj->kq', basis, basis, precision=HIGHEST_PRECISION)]
    reduce_sum x0 -> x1, other arithmetic: none -> 2.38 us  [on_device(): jnp.sum(basis[:, :, None] * spectral[:, None, :], axis=(0, 3, 4))]
  transfers between devices with their start and end apart: 6 -> 6, of which waited for: 6 -> 6; matrix products, arithmetic and copies ran while one was open for 2% -> 3% of each run, Pallas kernels for 0% -> 0%
where the time goes in v4:
time: 193 us; the launch traced here: 192 us
  waiting for transfers between devices  50.8 us (26%)
  matrix products  43.7 us (23%)
  other arithmetic  25.2 us (13%)
  Pallas kernels  21.9 us (11%)
  starting transfers between devices  20.4 us (11%)
  local copies, waits for them, and re-layouts  17.7 us (9%)
  blocking collectives  9.66 us (5%)
    all_to_all x3, waiting for transfers between devices, one_step(): returned = lax.all_to_all(back, axes, 0, 0, tiled=True)  30.3 us
    pallas_call x3, Pallas kernels, tide_term(): pl.pallas_call(functools.partial(tide_kernel, items * lays, pairs, rows),...  21.9 us
    all_to_all x3, waiting for transfers between devices, one_step(): received = lax.all_to_all(sent, axes, 0, 0, tiled=True)  20.4 us
    dot_general x3, matrix products, one_step(): jnp.einsum('svcj,slj->svcl', spectral_b, legendre, preferred_element_type...  18.1 us
    dot_general x3, matrix products, one_step(): jnp.einsum('svcl,slj->svcj', weighted, legendre, preferred_element_type=j...  15.6 us
    all_to_all x3, starting transfers between devices, one_step(): received = lax.all_to_all(sent, axes, 0, 0, tiled=True)  12.7 us
    all_to_all x1, blocking collectives, exchange_sum(): gathered = lax.all_to_all(rows, ('lat', 'wave'), 0, 0, tiled=True)  9.66 us
    all_to_all x3, starting transfers between devices, one_step(): returned = lax.all_to_all(back, axes, 0, 0, tiled=True)  7.75 us
  transfers between devices with their start and end apart: 6, of which 6 were waited for; matrix products, arithmetic and copies ran while one was open for 3% of the time, Pallas kernels for 0%

profile of v4, /device:TPU:0, one launch (start us, length us, event | category | flops | bytes accessed | tf_op | source)
XLA Modules:
  0.0 192.2 jit_solution(11174723193293706643)
XLA Ops:
  0.7 2.8 %fusion.48 = (f32[32,4096]{1,0:T(8,128)S(1)}, f32[32,4096]{1,0:T(8,128)S(1)}) fusion(s32[32]{0:T(128)} %param.15), kind=kLoop, calls=%fused_computation.79 | loop fusion | flops 1835008 | bytes 1048704 | tf_op jit(solution)/shard_map/cos | solution.py:21
  3.6 0.6 dynamic_slice.3
  4.9 0.7 fusion.50
  6.0 1.3 copy.111
  7.3 1.0 pad_maximum_fusion.3
  8.4 167.6 %while.13 = (s32[]{:T(128)}, f32[1,4,18,2048]{3,1,2,0:T(4,128)S(1)}, f32[2048]{0:T(1024)S(1)}, f32[1,1,3,2048]{3,2,1,0:T(4,128)S(1)}, bf16[1,2048,2048]{2,1,0:T(...) while((s32[]{:T(128)}, ...), condition=%wide.region_1.2_spmd.clone, body=%wide.region_0.1_spmd.clone.sunk | while | flops 3231582208 | bytes 42901892 | solution.py:229
  8.7 6.0 %fusion.91 = bf16[4,18,2048]{2,1,0:T(8,128)(2,1)S(1)} fusion(bf16[1,2048,2048]{2,1,0:T(8,128)(2,1)} %get-tuple-element.428, bf16[4,18,2048]{2,0,1:T(4,128)(2,1)S(1)} %convert_bitcast_fusion.2), kind=kOutput, calls=%fused_computation.8.clone.1 | convolution fusion | flops 604127232 | bytes 8978432 | tf_op jit(solution)/shard_map/while/body/eval_jaxpr/svcj,slj->svcl/dot_general | solution.py:182
  15.6 0.7 copy.164
  16.3 7.3 %all-to-all-start = ((bf16[32,12,128]{2,1,0:T(8,128)(2,1)}), bf16[32,12,128]{2,1,0:T(8,128)(2,1)S(1)}, u32[]{:S(2)}, u32[]{:S(2)}) async-start(bf16[32,12,128]{2,1,0:T(8,128)(2,1)} %copy.164), calls=%async_computation | async-start | bytes 262144 | tf_op jit(solution)/shard_map/while/body/eval_jaxpr/all_to_all | solution.py:187
  23.8 0.7 fusion.98
  24.5 0.7 compare_convert_fusion.2
  25.2 6.8 %all-to-all-done = bf16[32,12,128]{2,1,0:T(8,128)(2,1)S(1)} async-done(((bf16[32,12,128]{2,1,0:T(8,128)(2,1)}), bf16[32,12,128]{2,1,0:T(8,128)(2,1)S(1)}, u32[]{:S(2)}, u32[]{:S(2)}) %all-to-all-start) | async-done | bytes 98336 | tf_op jit(solution)/shard_map/while/body/eval_jaxpr/all_to_all | solution.py:187
  32.9 0.9 maximum_bitcast_fusion.2.lhs_ref
  33.8 7.3 %eval_jaxpr.3 = (f32[768,128]{1,0:T(8,128)}, f32[768,64]{1,0:T(8,128)}) custom-call(bf16[768,128]{1,0:T(8,128)(2,1)} %maximum_bitcast_fusion.2.lhs_ref, bf16[128,4096]{1,0:T(8,128)(2,1)} %get-tuple-element.432.tab_ref, f32[64,4096]{1,0:T(8,128)} %get-tuple-element.433.tide_ref), custom_call_target="tpu_custom_call" | custom-call | flops 2013265920 | bytes 2686976 | tf_op jit(solution)/shard_map/while/body/eval_jaxpr/pallas_call | solution.py:57
  41.1 1.4 multiply_bitcast_fusion.2
  43.0 0.4 pad_maximum_fusion.7
  43.7 0.8 copy.170
  44.5 2.6 %all-to-all-start.1 = ((f32[32,12,128]{2,1,0:T(8,128)}), f32[32,12,128]{2,1,0:T(8,128)S(1)}, u32[]{:S(2)}, u32[]{:S(2)}) async-start(f32[32,12,128]{2,1,0:T(8,128)} %copy.170), calls=%async_computation.1 | async-start | bytes 524288 | tf_op jit(solution)/shard_map/while/body/eval_jaxpr/all_to_all | solution.py:198
  47.2 10.1 %all-to-all-done.1 = f32[32,12,128]{2,1,0:T(8,128)S(1)} async-done(((f32[32,12,128]{2,1,0:T(8,128)}), f32[32,12,128]{2,1,0:T(8,128)S(1)}, u32[]{:S(2)}, u32[]{:S(2)}) %all-to-all-start.1) | async-done | bytes 196640 | tf_op jit(solution)/shard_map/while/body/eval_jaxpr/all_to_all | solution.py:198
  58.2 5.2 %fusion.96 = f32[1,4,18,2048]{3,2,1,0:T(8,128)S(1)} fusion(bf16[1,2048,2048]{2,1,0:T(8,128)(2,1)} %get-tuple-element.428, f32[1,4,18,2048]{3,1,2,0:T(4,128)S(1)} %get-tuple-element.409, bf16[4,18,2048]{2,0,1:T(4,128)(2,1)S(1)} %bitcast.197, f32[2048]{0:T(1024)S(1)} %bitcast.212), kind=kOutput, calls=%fused_computation.7.clone.1 | convolution fusion | flops 604274688 | bytes 9871360 | tf_op jit(solution)/shard_map/while/body/eval_jaxpr/svcl,slj->svcj/dot_general | solution.py:216
  63.8 0.7 convolution_bitcast_fusion.9
  64.5 0.7 fusion.99
  65.2 0.7 convolution_bitcast_fusion.10
  65.9 0.6 convolution_bitcast_fusion.11
  67.5 6.0 %fusion.91 = bf16[4,18,2048]{2,1,0:T(8,128)(2,1)S(1)} fusion(bf16[1,2048,2048]{2,1,0:T(8,128)(2,1)} %get-tuple-element.428, bf16[4,18,2048]{2,0,1:T(4,128)(2,1)S(1)} %convert_bitcast_fusion.2), kind=kOutput, calls=%fused_computation.8.clone.1 | convolution fusion | flops 604127232 | bytes 8978432 | tf_op jit(solution)/shard_map/while/body/eval_jaxpr/svcj,slj->svcl/dot_general | solution.py:182
  74.4 0.7 copy.164
  75.1 2.7 %all-to-all-start = ((bf16[32,12,128]{2,1,0:T(8,128)(2,1)}), bf16[32,12,128]{2,1,0:T(8,128)(2,1)S(1)}, u32[]{:S(2)}, u32[]{:S(2)}) async-start(bf16[32,12,128]{2,1,0:T(8,128)(2,1)} %copy.164), calls=%async_computation | async-start | bytes 262144 | tf_op jit(solution)/shard_map/while/body/eval_jaxpr/all_to_all | solution.py:187
  78.0 0.7 fusion.98
  78.7 0.7 compare_convert_fusion.2
  79.3 6.8 %all-to-all-done = bf16[32,12,128]{2,1,0:T(8,128)(2,1)S(1)} async-done(((bf16[32,12,128]{2,1,0:T(8,128)(2,1)}), bf16[32,12,128]{2,1,0:T(8,128)(2,1)S(1)}, u32[]{:S(2)}, u32[]{:S(2)}) %all-to-all-start) | async-done | bytes 98336 | tf_op jit(solution)/shard_map/while/body/eval_jaxpr/all_to_all | solution.py:187
  87.1 0.9 maximum_bitcast_fusion.2.lhs_ref
  88.0 7.3 %eval_jaxpr.3 = (f32[768,128]{1,0:T(8,128)}, f32[768,64]{1,0:T(8,128)}) custom-call(bf16[768,128]{1,0:T(8,128)(2,1)} %maximum_bitcast_fusion.2.lhs_ref, bf16[128,4096]{1,0:T(8,128)(2,1)} %get-tuple-element.432.tab_ref, f32[64,4096]{1,0:T(8,128)} %get-tuple-element.433.tide_ref), custom_call_target="tpu_custom_call" | custom-call | flops 2013265920 | bytes 2686976 | tf_op jit(solution)/shard_map/while/body/eval_jaxpr/pallas_call | solution.py:57
  95.3 1.4 multiply_bitcast_fusion.2
  97.2 0.4 pad_maximum_fusion.7
  97.9 0.8 copy.170
  98.7 2.6 %all-to-all-start.1 = ((f32[32,12,128]{2,1,0:T(8,128)}), f32[32,12,128]{2,1,0:T(8,128)S(1)}, u32[]{:S(2)}, u32[]{:S(2)}) async-start(f32[32,12,128]{2,1,0:T(8,128)} %copy.170), calls=%async_computation.1 | async-start | bytes 524288 | tf_op jit(solution)/shard_map/while/body/eval_jaxpr/all_to_all | solution.py:198
  101.4 10.1 %all-to-all-done.1 = f32[32,12,128]{2,1,0:T(8,128)S(1)} async-done(((f32[32,12,128]{2,1,0:T(8,128)}), f32[32,12,128]{2,1,0:T(8,128)S(1)}, u32[]{:S(2)}, u32[]{:S(2)}) %all-to-all-start.1) | async-done | bytes 196640 | tf_op jit(solution)/shard_map/while/body/eval_jaxpr/all_to_all | solution.py:198
  112.3 5.2 %fusion.96 = f32[1,4,18,2048]{3,2,1,0:T(8,128)S(1)} fusion(bf16[1,2048,2048]{2,1,0:T(8,128)(2,1)} %get-tuple-element.428, f32[1,4,18,2048]{3,1,2,0:T(4,128)S(1)} %get-tuple-element.409, bf16[4,18,2048]{2,0,1:T(4,128)(2,1)S(1)} %bitcast.197, f32[2048]{0:T(1024)S(1)} %bitcast.212), kind=kOutput, calls=%fused_computation.7.clone.1 | convolution fusion | flops 604274688 | bytes 9871360 | tf_op jit(solution)/shard_map/while/body/eval_jaxpr/svcl,slj->svcj/dot_general | solution.py:216
  118.0 0.7 convolution_bitcast_fusion.9
  118.7 0.7 fusion.99
  119.4 0.7 convolution_bitcast_fusion.10
  120.1 0.6 convolution_bitcast_fusion.11
  121.7 6.0 %fusion.91 = bf16[4,18,2048]{2,1,0:T(8,128)(2,1)S(1)} fusion(bf16[1,2048,2048]{2,1,0:T(8,128)(2,1)} %get-tuple-element.428, bf16[4,18,2048]{2,0,1:T(4,128)(2,1)S(1)} %convert_bitcast_fusion.2), kind=kOutput, calls=%fused_computation.8.clone.1 | convolution fusion | flops 604127232 | bytes 8978432 | tf_op jit(solution)/shard_map/while/body/eval_jaxpr/svcj,slj->svcl/dot_general | solution.py:182
  128.6 0.7 copy.164
  129.2 2.7 %all-to-all-start = ((bf16[32,12,128]{2,1,0:T(8,128)(2,1)}), bf16[32,12,128]{2,1,0:T(8,128)(2,1)S(1)}, u32[]{:S(2)}, u32[]{:S(2)}) async-start(bf16[32,12,128]{2,1,0:T(8,128)(2,1)} %copy.164), calls=%async_computation | async-start | bytes 262144 | tf_op jit(solution)/shard_map/while/body/eval_jaxpr/all_to_all | solution.py:187
  132.2 0.7 fusion.98
  132.9 0.7 compare_convert_fusion.2
  133.5 6.8 %all-to-all-done = bf16[32,12,128]{2,1,0:T(8,128)(2,1)S(1)} async-done(((bf16[32,12,128]{2,1,0:T(8,128)(2,1)}), bf16[32,12,128]{2,1,0:T(8,128)(2,1)S(1)}, u32[]{:S(2)}, u32[]{:S(2)}) %all-to-all-start) | async-done | bytes 98336 | tf_op jit(solution)/shard_map/while/body/eval_jaxpr/all_to_all | solution.py:187
  141.3 0.9 maximum_bitcast_fusion.2.lhs_ref
  142.2 7.3 %eval_jaxpr.3 = (f32[768,128]{1,0:T(8,128)}, f32[768,64]{1,0:T(8,128)}) custom-call(bf16[768,128]{1,0:T(8,128)(2,1)} %maximum_bitcast_fusion.2.lhs_ref, bf16[128,4096]{1,0:T(8,128)(2,1)} %get-tuple-element.432.tab_ref, f32[64,4096]{1,0:T(8,128)} %get-tuple-element.433.tide_ref), custom_call_target="tpu_custom_call" | custom-call | flops 2013265920 | bytes 2686976 | tf_op jit(solution)/shard_map/while/body/eval_jaxpr/pallas_call | solution.py:57
  149.5 1.4 multiply_bitcast_fusion.2
  151.4 0.4 pad_maximum_fusion.7
  152.1 0.8 copy.170
  152.9 2.6 %all-to-all-start.1 = ((f32[32,12,128]{2,1,0:T(8,128)}), f32[32,12,128]{2,1,0:T(8,128)S(1)}, u32[]{:S(2)}, u32[]{:S(2)}) async-start(f32[32,12,128]{2,1,0:T(8,128)} %copy.170), calls=%async_computation.1 | async-start | bytes 524288 | tf_op jit(solution)/shard_map/while/body/eval_jaxpr/all_to_all | solution.py:198
  155.6 10.1 %all-to-all-done.1 = f32[32,12,128]{2,1,0:T(8,128)S(1)} async-done(((f32[32,12,128]{2,1,0:T(8,128)}), f32[32,12,128]{2,1,0:T(8,128)S(1)}, u32[]{:S(2)}, u32[]{:S(2)}) %all-to-all-start.1) | async-done | bytes 196640 | tf_op jit(solution)/shard_map/while/body/eval_jaxpr/all_to_all | solution.py:198
  166.5 5.2 %fusion.96 = f32[1,4,18,2048]{3,2,1,0:T(8,128)S(1)} fusion(bf16[1,2048,2048]{2,1,0:T(8,128)(2,1)} %get-tuple-element.428, f32[1,4,18,2048]{3,1,2,0:T(4,128)S(1)} %get-tuple-element.409, bf16[4,18,2048]{2,0,1:T(4,128)(2,1)S(1)} %bitcast.197, f32[2048]{0:T(1024)S(1)} %bitcast.212), kind=kOutput, calls=%fused_computation.7.clone.1 | convolution fusion | flops 604274688 | bytes 9871360 | tf_op jit(solution)/shard_map/while/body/eval_jaxpr/svcl,slj->svcj/dot_general | solution.py:216
  172.2 0.7 convolution_bitcast_fusion.9
  172.8 0.7 fusion.99
  173.6 0.7 convolution_bitcast_fusion.10
  174.2 0.6 convolution_bitcast_fusion.11
  176.4 2.4 %multiply_reduce_fusion.1 = (f32[4,4]{1,0:T(4,128)S(1)}, f32[4,4]{1,0:T(4,128)S(1)}) fusion(f32[4,18,2048]{2,0,1:T(4,128)S(1)} %bitcast.194, f32[4,18,2048]{2,1,0:T(8,128)} %copy.111, f32[4,18,2048]{2,0,1:T(4,128)S(1)} %fusion.61), kind=kLoop, calls=%fused_computation.56 | loop fusion | flops 2359264 | bytes 1769600 | tf_op jit(solution)/shard_map/reduce_sum | solution.py:231
  179.0 9.7 %all_to_all.24 = f32[32,1,36]{2,1,0:T(1,128)S(1)} all-to-all(f32[32,1,36]{2,1,0:T(1,128)S(1)} %broadcast_in_dim.2), channel_id=1, replica_groups=mesh['lat'=8,'wave'=4] {'lat','wave'}, dimensions={0} | all-to-all | bytes 9216 | tf_op jit(solution)/shard_map/all_to_all | solution.py:127
  189.6 1.9 %fusion.37 = f32[1,4,18,2048]{3,1,2,0:T(4,128)} fusion(f32[1,4,18,2048]{3,1,2,0:T(4,128)S(1)} %get-tuple-element.178, f32[4]{0:T(128)S(1)} %add_sqrt_fusion, f32[4,4]{0,1:T(4,128)S(1)} %copy.113, f32[1,4,18,2048]{3,1,2,0:T(4,128)S(1)} %copy-done.3), kind=kOutput, calls=%fused_computation.59 | convolution fusion | flops 7372816 | bytes 1769552 | tf_op jit(solution)/shard_map/skcj,kv->svcj/dot_general | solution.py:236
  191.5 0.7 copy.115
  (147 shorter events, 16.9 us)
Async XLA Ops:
  0.6 3.0 %copy-start.10 = (s32[32]{0:T(128)S(1)}, s32[32]{0:T(128)}, u32[]{:S(2)}) copy-start(s32[32]{0:T(128)} %param.15) | copy-start | bytes 388
  0.6 4.9 %copy-start.1 = (f32[1,4,18,2048]{3,1,2,0:T(4,128)S(1)}, f32[1,4,18,2048]{3,1,2,0:T(4,128)}, u32[]{:S(2)}) copy-start(f32[1,4,18,2048]{3,1,2,0:T(4,128)} %param.13) | copy-start | bytes 1769476
  3.5 2.4 %copy-start.9 = (s32[2048]{0:T(1024)S(1)}, s32[2048]{0:T(1024)}, u32[]{:S(2)}) copy-start(s32[2048]{0:T(1024)} %param.16) | copy-start | bytes 24580
  5.5 1.7 copy-start.8
  5.7 1.6 copy-start.2
  5.9 2.5 %copy-start = (f32[3,2048]{1,0:T(4,128)S(1)}, f32[3,2048]{1,0:T(4,128)}, u32[]{:S(2)}) copy-start(f32[3,2048]{1,0:T(4,128)} %param.19) | copy-start | bytes 73732
  5.9 2.5 %copy-start.4 = (f32[2048]{0:T(1024)S(1)}, f32[2048]{0:T(1024)}, u32[]{:S(2)}) copy-start(f32[2048]{0:T(1024)} %param.17) | copy-start | bytes 24580
  5.9 2.5 %copy-start.5 = (f32[3,3]{1,0:T(4,128)S(1)}, f32[3,3]{1,0:T(4,128)}, u32[]{:S(2)}) copy-start(f32[3,3]{1,0:T(4,128)} %param.21) | copy-start | bytes 112
  5.9 2.5 %copy-start.6 = (f32[3,3]{1,0:T(4,128)S(1)}, f32[3,3]{1,0:T(4,128)}, u32[]{:S(2)}) copy-start(f32[3,3]{1,0:T(4,128)} %param.22) | copy-start | bytes 112
  5.9 2.4 %copy-start.7 = (f32[3]{0:T(128)S(1)}, f32[3]{0:T(128)}, u32[]{:S(2)}) copy-start(f32[3]{0:T(128)} %param.23) | copy-start | bytes 40
  16.3 15.7 %all-to-all-start = ((bf16[32,12,128]{2,1,0:T(8,128)(2,1)}), bf16[32,12,128]{2,1,0:T(8,128)(2,1)S(1)}, u32[]{:S(2)}, u32[]{:S(2)}) async-start(bf16[32,12,128]{2,1,0:T(8,128)(2,1)} %copy.164), calls=%async_computation | async-start | bytes 262144 | tf_op jit(solution)/shard_map/while/body/eval_jaxpr/all_to_all | solution.py:187
  44.5 12.8 %all-to-all-start.1 = ((f32[32,12,128]{2,1,0:T(8,128)}), f32[32,12,128]{2,1,0:T(8,128)S(1)}, u32[]{:S(2)}, u32[]{:S(2)}) async-start(f32[32,12,128]{2,1,0:T(8,128)} %copy.170), calls=%async_computation.1 | async-start | bytes 524288 | tf_op jit(solution)/shard_map/while/body/eval_jaxpr/all_to_all | solution.py:198
  75.1 11.1 %all-to-all-start = ((bf16[32,12,128]{2,1,0:T(8,128)(2,1)}), bf16[32,12,128]{2,1,0:T(8,128)(2,1)S(1)}, u32[]{:S(2)}, u32[]{:S(2)}) async-start(bf16[32,12,128]{2,1,0:T(8,128)(2,1)} %copy.164), calls=%async_computation | async-start | bytes 262144 | tf_op jit(solution)/shard_map/while/body/eval_jaxpr/all_to_all | solution.py:187
  98.7 12.8 %all-to-all-start.1 = ((f32[32,12,128]{2,1,0:T(8,128)}), f32[32,12,128]{2,1,0:T(8,128)S(1)}, u32[]{:S(2)}, u32[]{:S(2)}) async-start(f32[32,12,128]{2,1,0:T(8,128)} %copy.170), calls=%async_computation.1 | async-start | bytes 524288 | tf_op jit(solution)/shard_map/while/body/eval_jaxpr/all_to_all | solution.py:198
  129.2 11.1 %all-to-all-start = ((bf16[32,12,128]{2,1,0:T(8,128)(2,1)}), bf16[32,12,128]{2,1,0:T(8,128)(2,1)S(1)}, u32[]{:S(2)}, u32[]{:S(2)}) async-start(bf16[32,12,128]{2,1,0:T(8,128)(2,1)} %copy.164), calls=%async_computation | async-start | bytes 262144 | tf_op jit(solution)/shard_map/while/body/eval_jaxpr/all_to_all | solution.py:187
  152.9 12.8 %all-to-all-start.1 = ((f32[32,12,128]{2,1,0:T(8,128)}), f32[32,12,128]{2,1,0:T(8,128)S(1)}, u32[]{:S(2)}, u32[]{:S(2)}) async-start(f32[32,12,128]{2,1,0:T(8,128)} %copy.170), calls=%async_computation.1 | async-start | bytes 524288 | tf_op jit(solution)/shard_map/while/body/eval_jaxpr/all_to_all | solution.py:198
  175.9 13.6 %copy-start.3 = (f32[1,4,18,2048]{3,1,2,0:T(4,128)S(1)}, f32[1,4,18,2048]{3,1,2,0:T(4,128)}, u32[]{:S(2)}) copy-start(f32[1,4,18,2048]{3,1,2,0:T(4,128)} %copy-done.2) | copy-start | bytes 1769476
  189.5 2.6 %copy-start.11 = (f32[4]{0:T(128)}, f32[4]{0:T(128)S(1)}, u32[]{:S(2)}) copy-start(f32[4]{0:T(128)S(1)} %add_sqrt_fusion) | copy-start | bytes 52

commit v5 on v4

--- a/solution.py
+++ b/solution.py
@@ -177,11 +177,13 @@
     advect = (
         local_waves.astype(jnp.float32)[:, None, None, None] * zonal_flow[None, None, :, :] / ntrunc
     )
-    def one_step(step_index, spectral):
-        spectral_b = spectral.astype(jnp.bfloat16)
-        grid_b = jnp.einsum(
-            "svcj,slj->svcl", spectral_b, legendre, preferred_element_type=jnp.float32
+    def synthesize(spectral):
+        return jnp.einsum(
+            "svcj,slj->svcl", spectral.astype(jnp.bfloat16), legendre,
+            preferred_element_type=jnp.float32,
         ).astype(jnp.bfloat16)
+
+    def advance(spectral, grid_b):
         grid_split = grid_b.reshape(local_slots, vectors, layers, 6, nlat)
         sent = to_bands(grid_split[:, :, :, 2:4, :], device_count)
         received = lax.all_to_all(sent, axes, 0, 0, tiled=True)
@@ -226,7 +228,12 @@
         )
         return spectral
 
-    spectral = lax.fori_loop(0, STEPS, one_step, basis)
+    def rotated_step(step_index, carry):
+        spectral = advance(*carry)
+        return spectral, synthesize(spectral)
+
+    carry = lax.fori_loop(0, STEPS - 1, rotated_step, (basis, synthesize(basis)))
+    spectral = advance(*carry)
     entries = float(local_slots * device_count * channels * ndeg)
     local_proj = jnp.sum(basis[:, :, None] * spectral[:, None, :], axis=(0, 3, 4))
     local_self = jnp.sum(spectral * spectral, axis=(0, 2, 3))

time: 193 us -> 205 us (1.062)
  loops' own time: 1.3 us -> 13.4 us
  matrix products: 43.7 us -> 36.3 us
  other arithmetic: 25.2 us -> 31 us
  local copies, waits for them, and re-layouts: 17.7 us -> 21.6 us
    another operation x1, loops' own time: 1.3 us -> 13.4 us  [on_device(): lax.fori_loop(0, STEPS - 1, rotated_step, (basis, synthesize(basis)))]
    dot_general x6, matrix products: 33.7 us -> 27.2 us  [the longest x3 15.9 us: advance(): jnp.einsum('svcl,slj->svcj', weighted, legendre, preferred_element_type=j...]
    unnamed x27 -> x21, local copies, waits for them, and re-layouts: 0.87 us -> 2.98 us
where the time goes in v5:
time: 205 us; the launch traced here: 206 us
  waiting for transfers between devices  49.6 us (24%)
  matrix products  36.3 us (18%)
  other arithmetic  31 us (15%)
  Pallas kernels  22 us (11%)
  local copies, waits for them, and re-layouts  21.6 us (11%)
  starting transfers between devices  20.4 us (10%)
  loops' own time  13.4 us (7%)
  blocking collectives  9.66 us (5%)
    all_to_all x3, waiting for transfers between devices, advance(): returned = lax.all_to_all(back, axes, 0, 0, tiled=True)  29.7 us
    pallas_call x3, Pallas kernels, tide_term(): pl.pallas_call(functools.partial(tide_kernel, items * lays, pairs, rows),...  22 us
    all_to_all x3, waiting for transfers between devices, advance(): received = lax.all_to_all(sent, axes, 0, 0, tiled=True)  19.9 us
    dot_general x3, matrix products, advance(): jnp.einsum('svcl,slj->svcj', weighted, legendre, preferred_element_type=j...  15.9 us
    another operation x1, loops' own time, on_device(): lax.fori_loop(0, STEPS - 1, rotated_step, (basis, synthesize(basis)))  13.4 us
    all_to_all x3, starting transfers between devices, advance(): received = lax.all_to_all(sent, axes, 0, 0, tiled=True)  12.7 us
    dot_general x3, matrix products, synthesize(): jnp.einsum('svcj,slj->svcl', spectral.astype(jnp.bfloat16), legendre, pre...  11.3 us
    all_to_all x1, blocking collectives, exchange_sum(): gathered = lax.all_to_all(rows, ('lat', 'wave'), 0, 0, tiled=True)  9.66 us
  transfers between devices with their start and end apart: 6, of which 6 were waited for; matrix products, arithmetic and copies ran while one was open for 3% of the time, Pallas kernels for 0%

profile of v5, /device:TPU:0, one launch (start us, length us, event | category | flops | bytes accessed | tf_op | source)
XLA Modules:
  0.0 205.9 jit_solution(11050569958329284122)
XLA Ops:
  0.6 2.8 %fusion.80 = (f32[32,4096]{1,0:T(8,128)S(1)}, f32[32,4096]{1,0:T(8,128)S(1)}) fusion(s32[32]{0:T(128)} %param.15), kind=kLoop, calls=%fused_computation.112 | loop fusion | flops 1835008 | bytes 1048704 | tf_op jit(solution)/shard_map/cos | solution.py:21
  3.5 1.2 dynamic_slice.3
  6.2 1.3 convert_bitcast_fusion
  7.5 0.8 fusion.99
  8.3 0.7 multiply_add_fusion.2
  9.0 6.0 %fusion.57 = bf16[1,4,18,2048]{3,2,1,0:T(8,128)(2,1)S(1)} fusion(bf16[1,2048,2048]{2,1,0:T(8,128)(2,1)} %param.14, bf16[4,18,2048]{2,0,1:T(4,128)(2,1)S(1)} %get-tuple-element.289), kind=kOutput, calls=%fused_computation.68 | convolution fusion | flops 604127232 | bytes 8978432 | tf_op jit(solution)/shard_map/svcj,slj->svcl/dot_general | solution.py:181
  15.0 1.1 pad_maximum_fusion.3.tab_ref
  16.1 118.6 %while.15 = (s32[]{:T(128)}, f32[1,4,18,2048]{3,1,2,0:T(4,128)S(1)}, bf16[1,4,18,2048]{3,2,1,0:T(8,128)(2,1)S(1)}, f32[2048]{0:T(1024)S(1)}, f32[1,1,3,2048]{3,2...) while((s32[]{:T(128)}, ...), condition=%wide.region_1.2_spmd.clone, body=%wide.region_0.1_spmd.clone.sunk | while | flops 3231729664 | bytes 66699708 | solution.py:235
  17.2 0.7 copy.329
  17.9 7.3 %all-to-all-start = ((bf16[32,12,128]{2,1,0:T(8,128)(2,1)}), bf16[32,12,128]{2,1,0:T(8,128)(2,1)S(1)}, u32[]{:S(2)}, u32[]{:S(2)}) async-start(bf16[32,12,128]{2,1,0:T(8,128)(2,1)} %copy.329), calls=%async_computation | async-start | bytes 262144 | tf_op jit(solution)/shard_map/while/body/eval_jaxpr/all_to_all | solution.py:189
  26.8 6.8 %all-to-all-done = bf16[32,12,128]{2,1,0:T(8,128)(2,1)S(1)} async-done(((bf16[32,12,128]{2,1,0:T(8,128)(2,1)}), bf16[32,12,128]{2,1,0:T(8,128)(2,1)S(1)}, u32[]{:S(2)}, u32[]{:S(2)}) %all-to-all-start) | async-done | bytes 98336 | tf_op jit(solution)/shard_map/while/body/eval_jaxpr/all_to_all | solution.py:189
  34.6 0.9 maximum_bitcast_fusion.3.lhs_ref
  35.5 7.3 %eval_jaxpr.3 = (f32[768,128]{1,0:T(8,128)}, f32[768,64]{1,0:T(8,128)}) custom-call(bf16[768,128]{1,0:T(8,128)(2,1)} %maximum_bitcast_fusion.3.lhs_ref, bf16[128,4096]{1,0:T(8,128)(2,1)} %get-tuple-element.489.tab_ref, f32[64,4096]{1,0:T(8,128)} %get-tuple-element.490.tide_ref), custom_call_target="tpu_custom_call" | custom-call | flops 2013265920 | bytes 2686976 | tf_op jit(solution)/shard_map/while/body/eval_jaxpr/pallas_call | solution.py:57
  42.8 1.4 multiply_bitcast_fusion.3
  45.4 0.8 copy.335
  46.2 2.6 %all-to-all-start.1 = ((f32[32,12,128]{2,1,0:T(8,128)}), f32[32,12,128]{2,1,0:T(8,128)S(1)}, u32[]{:S(2)}, u32[]{:S(2)}) async-start(f32[32,12,128]{2,1,0:T(8,128)} %copy.335), calls=%async_computation.1 | async-start | bytes 524288 | tf_op jit(solution)/shard_map/while/body/eval_jaxpr/all_to_all | solution.py:200
  48.9 10.1 %all-to-all-done.1 = f32[32,12,128]{2,1,0:T(8,128)S(1)} async-done(((f32[32,12,128]{2,1,0:T(8,128)}), f32[32,12,128]{2,1,0:T(8,128)S(1)}, u32[]{:S(2)}, u32[]{:S(2)}) %all-to-all-start.1) | async-done | bytes 196640 | tf_op jit(solution)/shard_map/while/body/eval_jaxpr/all_to_all | solution.py:200
  59.9 5.3 %fusion.143 = f32[1,4,18,2048]{3,2,1,0:T(8,128)S(1)} fusion(bf16[1,2048,2048]{2,1,0:T(8,128)(2,1)} %get-tuple-element.491, f32[1,4,18,2048]{3,1,2,0:T(4,128)S(1)} %get-tuple-element.465, bf16[4,18,2048]{2,0,1:T(4,128)(2,1)S(1)} %bitcast.295, f32[2048]{0:T(1024)S(1)} %bitcast.318), kind=kOutput, calls=%fused_computation.7.clone.1 | convolution fusion | flops 604274688 | bytes 9871360 | tf_op jit(solution)/shard_map/while/body/eval_jaxpr/svcl,slj->svcj/dot_general | solution.py:218
  65.7 0.7 convolution_bitcast_fusion.8
  66.3 0.7 fusion.146
  67.0 0.7 fusion.147
  69.0 2.7 %fusion.149 = bf16[1,4,18,2048]{3,2,1,0:T(8,128)(2,1)S(1)} fusion(bf16[1,2048,2048]{2,1,0:T(8,128)(2,1)S(1)} %bitcast.291, bf16[4,18,2048]{2,0,1:T(4,128)(2,1)S(1)} %bitcast.292), kind=kOutput, calls=%fused_computation.9.clone.1 | convolution fusion | flops 604127232 | bytes 8978432 | tf_op jit(solution)/shard_map/while/body/eval_jaxpr/svcj,slj->svcl/dot_general | solution.py:181
  72.5 0.7 copy.329
  73.2 2.7 %all-to-all-start = ((bf16[32,12,128]{2,1,0:T(8,128)(2,1)}), bf16[32,12,128]{2,1,0:T(8,128)(2,1)S(1)}, u32[]{:S(2)}, u32[]{:S(2)}) async-start(bf16[32,12,128]{2,1,0:T(8,128)(2,1)} %copy.329), calls=%async_computation | async-start | bytes 262144 | tf_op jit(solution)/shard_map/while/body/eval_jaxpr/all_to_all | solution.py:189
  77.5 6.8 %all-to-all-done = bf16[32,12,128]{2,1,0:T(8,128)(2,1)S(1)} async-done(((bf16[32,12,128]{2,1,0:T(8,128)(2,1)}), bf16[32,12,128]{2,1,0:T(8,128)(2,1)S(1)}, u32[]{:S(2)}, u32[]{:S(2)}) %all-to-all-start) | async-done | bytes 98336 | tf_op jit(solution)/shard_map/while/body/eval_jaxpr/all_to_all | solution.py:189
  85.2 0.9 maximum_bitcast_fusion.3.lhs_ref
  86.1 7.3 %eval_jaxpr.3 = (f32[768,128]{1,0:T(8,128)}, f32[768,64]{1,0:T(8,128)}) custom-call(bf16[768,128]{1,0:T(8,128)(2,1)} %maximum_bitcast_fusion.3.lhs_ref, bf16[128,4096]{1,0:T(8,128)(2,1)} %get-tuple-element.489.tab_ref, f32[64,4096]{1,0:T(8,128)} %get-tuple-element.490.tide_ref), custom_call_target="tpu_custom_call" | custom-call | flops 2013265920 | bytes 2686976 | tf_op jit(solution)/shard_map/while/body/eval_jaxpr/pallas_call | solution.py:57
  93.5 1.4 multiply_bitcast_fusion.3
  96.1 0.8 copy.335
  96.9 2.6 %all-to-all-start.1 = ((f32[32,12,128]{2,1,0:T(8,128)}), f32[32,12,128]{2,1,0:T(8,128)S(1)}, u32[]{:S(2)}, u32[]{:S(2)}) async-start(f32[32,12,128]{2,1,0:T(8,128)} %copy.335), calls=%async_computation.1 | async-start | bytes 524288 | tf_op jit(solution)/shard_map/while/body/eval_jaxpr/all_to_all | solution.py:200
  99.6 10.1 %all-to-all-done.1 = f32[32,12,128]{2,1,0:T(8,128)S(1)} async-done(((f32[32,12,128]{2,1,0:T(8,128)}), f32[32,12,128]{2,1,0:T(8,128)S(1)}, u32[]{:S(2)}, u32[]{:S(2)}) %all-to-all-start.1) | async-done | bytes 196640 | tf_op jit(solution)/shard_map/while/body/eval_jaxpr/all_to_all | solution.py:200
  110.5 5.3 %fusion.143 = f32[1,4,18,2048]{3,2,1,0:T(8,128)S(1)} fusion(bf16[1,2048,2048]{2,1,0:T(8,128)(2,1)} %get-tuple-element.491, f32[1,4,18,2048]{3,1,2,0:T(4,128)S(1)} %get-tuple-element.465, bf16[4,18,2048]{2,0,1:T(4,128)(2,1)S(1)} %bitcast.295, f32[2048]{0:T(1024)S(1)} %bitcast.318), kind=kOutput, calls=%fused_computation.7.clone.1 | convolution fusion | flops 604274688 | bytes 9871360 | tf_op jit(solution)/shard_map/while/body/eval_jaxpr/svcl,slj->svcj/dot_general | solution.py:218
  116.3 0.7 convolution_bitcast_fusion.8
  117.0 0.7 fusion.146
  117.7 0.7 fusion.147
  119.6 2.7 %fusion.149 = bf16[1,4,18,2048]{3,2,1,0:T(8,128)(2,1)S(1)} fusion(bf16[1,2048,2048]{2,1,0:T(8,128)(2,1)S(1)} %bitcast.291, bf16[4,18,2048]{2,0,1:T(4,128)(2,1)S(1)} %bitcast.292), kind=kOutput, calls=%fused_computation.9.clone.1 | convolution fusion | flops 604127232 | bytes 8978432 | tf_op jit(solution)/shard_map/while/body/eval_jaxpr/svcj,slj->svcl/dot_general | solution.py:181
  135.6 0.7 copy.231
  136.3 2.7 %all-to-all-start.2 = ((bf16[32,12,128]{2,1,0:T(8,128)(2,1)}), bf16[32,12,128]{2,1,0:T(8,128)(2,1)S(1)}, u32[]{:S(2)}, u32[]{:S(2)}) async-start(bf16[32,12,128]{2,1,0:T(8,128)(2,1)} %copy.231), calls=%async_computation.2 | async-start | bytes 262144 | tf_op jit(solution)/shard_map/all_to_all | solution.py:189
  139.3 0.8 copy-done.1
  141.1 6.3 %all-to-all-done.2 = bf16[32,12,128]{2,1,0:T(8,128)(2,1)S(1)} async-done(((bf16[32,12,128]{2,1,0:T(8,128)(2,1)}), bf16[32,12,128]{2,1,0:T(8,128)(2,1)S(1)}, u32[]{:S(2)}, u32[]{:S(2)}) %all-to-all-start.2) | async-done | bytes 98336 | tf_op jit(solution)/shard_map/all_to_all | solution.py:189
  148.3 0.9 maximum_bitcast_fusion.1.lhs_ref
  149.2 7.3 %shard_map.130 = (f32[768,128]{1,0:T(8,128)}, f32[768,64]{1,0:T(8,128)}) custom-call(bf16[768,128]{1,0:T(8,128)(2,1)} %maximum_bitcast_fusion.1.lhs_ref, bf16[128,4096]{1,0:T(8,128)(2,1)} %get-tuple-element.505, f32[64,4096]{1,0:T(8,128)} %get-tuple-element.511), custom_call_target="tpu_custom_call" | custom-call | flops 2013265920 | bytes 2686976 | tf_op jit(solution)/shard_map/pallas_call | solution.py:57
  156.5 1.4 multiply_bitcast_fusion.1
  157.9 0.9 fusion.104
  158.8 1.8 copy.235
  160.6 0.8 copy.236
  161.5 1.5 pad_maximum_fusion.5
  163.2 0.8 copy.237
  164.0 2.6 %all-to-all-start.3 = ((f32[32,12,128]{2,1,0:T(8,128)}), f32[32,12,128]{2,1,0:T(8,128)S(1)}, u32[]{:S(2)}, u32[]{:S(2)}) async-start(f32[32,12,128]{2,1,0:T(8,128)} %copy.237), calls=%async_computation.3 | async-start | bytes 524288 | tf_op jit(solution)/shard_map/all_to_all | solution.py:200
  166.6 0.7 broadcast_multiply_fusion.3
  167.3 9.5 %all-to-all-done.3 = f32[32,12,128]{2,1,0:T(8,128)S(1)} async-done(((f32[32,12,128]{2,1,0:T(8,128)}), f32[32,12,128]{2,1,0:T(8,128)S(1)}, u32[]{:S(2)}, u32[]{:S(2)}) %all-to-all-start.3) | async-done | bytes 196640 | tf_op jit(solution)/shard_map/all_to_all | solution.py:200
  177.3 0.7 fusion.84
  178.0 0.7 fusion.82
  178.7 1.2 multiply_convert_fusion.2
  179.9 5.2 %fusion.51 = f32[1,4,18,2048]{3,2,1,0:T(8,128)S(1)} fusion(bf16[1,2048,2048]{2,1,0:T(8,128)(2,1)} %get-tuple-element.498, f32[1,4,18,2048]{3,1,2,0:T(4,128)S(1)} %get-tuple-element.192, bf16[4,18,2048]{2,0,1:T(4,128)(2,1)S(1)} %bitcast.322, f32[2048]{0:T(1024)S(1)} %fusion.88), kind=kOutput, calls=%fused_computation.64 | convolution fusion | flops 604274688 | bytes 9871360 | tf_op jit(solution)/shard_map/svcl,slj->svcj/dot_general | solution.py:218
  185.5 0.7 convolution_bitcast_fusion.4
  186.2 0.7 fusion.61
  186.9 0.7 convolution_bitcast_fusion.2
  189.9 1.3 multiply_reduce_fusion.1
  191.5 9.7 %all_to_all.34 = f32[32,1,36]{2,1,0:T(1,128)S(1)} all-to-all(f32[32,1,36]{2,1,0:T(1,128)S(1)} %broadcast_in_dim.2), channel_id=1, replica_groups=mesh['lat'=8,'wave'=4] {'lat','wave'}, dimensions={0} | all-to-all | bytes 9216 | tf_op jit(solution)/shard_map/all_to_all | solution.py:127
  201.6 1.1 fusion.89
  203.1 0.7 fusion.66
  203.8 1.2 copy.254
  205.0 0.7 copy.255
  (145 shorter events, 22.2 us)
Async XLA Ops:
  6.1 10.0 %copy-start = (f32[3,2048]{1,0:T(4,128)S(1)}, f32[3,2048]{1,0:T(4,128)}, u32[]{:S(2)}) copy-start(f32[3,2048]{1,0:T(4,128)} %param.19) | copy-start | bytes 73732
  6.1 10.0 %copy-start.2 = (f32[2048]{0:T(1024)S(1)}, f32[2048]{0:T(1024)}, u32[]{:S(2)}) copy-start(f32[2048]{0:T(1024)} %param.17) | copy-start | bytes 24580
  6.1 10.0 %copy-start.3 = (f32[3,3]{1,0:T(4,128)S(1)}, f32[3,3]{1,0:T(4,128)}, u32[]{:S(2)}) copy-start(f32[3,3]{1,0:T(4,128)} %param.21) | copy-start | bytes 112
  6.1 10.0 %copy-start.4 = (f32[3,3]{1,0:T(4,128)S(1)}, f32[3,3]{1,0:T(4,128)}, u32[]{:S(2)}) copy-start(f32[3,3]{1,0:T(4,128)} %param.22) | copy-start | bytes 112
  6.1 10.0 %copy-start.5 = (f32[3]{0:T(128)S(1)}, f32[3]{0:T(128)}, u32[]{:S(2)}) copy-start(f32[3]{0:T(128)} %param.23) | copy-start | bytes 40
  17.9 15.7 %all-to-all-start = ((bf16[32,12,128]{2,1,0:T(8,128)(2,1)}), bf16[32,12,128]{2,1,0:T(8,128)(2,1)S(1)}, u32[]{:S(2)}, u32[]{:S(2)}) async-start(bf16[32,12,128]{2,1,0:T(8,128)(2,1)} %copy.329), calls=%async_computation | async-start | bytes 262144 | tf_op jit(solution)/shard_map/while/body/eval_jaxpr/all_to_all | solution.py:189
  46.2 12.8 %all-to-all-start.1 = ((f32[32,12,128]{2,1,0:T(8,128)}), f32[32,12,128]{2,1,0:T(8,128)S(1)}, u32[]{:S(2)}, u32[]{:S(2)}) async-start(f32[32,12,128]{2,1,0:T(8,128)} %copy.335), calls=%async_computation.1 | async-start | bytes 524288 | tf_op jit(solution)/shard_map/while/body/eval_jaxpr/all_to_all | solution.py:200
  59.9 9.1 %slice-start = ((s8[8388608]{0:T(1024)(128)(4,1)}), s8[4194304]{0:T(1024)(128)(4,1)S(1)}, s32[]{:S(2)}) async-start(s8[8388608]{0:T(1024)(128)(4,1)} %bitcast.290), calls=%async_computation.5 | async-start | bytes 8388608 | tf_op jit(solution)/shard_map/while
  59.9 9.1 %slice-start.1 = ((s8[8388608]{0:T(1024)(128)(4,1)}), s8[4194304]{0:T(1024)(128)(4,1)S(1)}, s32[]{:S(2)}) async-start(s8[8388608]{0:T(1024)(128)(4,1)} %bitcast.290), calls=%async_computation.6 | async-start | bytes 8388608 | tf_op jit(solution)/shard_map/while
  73.2 11.1 %all-to-all-start = ((bf16[32,12,128]{2,1,0:T(8,128)(2,1)}), bf16[32,12,128]{2,1,0:T(8,128)(2,1)S(1)}, u32[]{:S(2)}, u32[]{:S(2)}) async-start(bf16[32,12,128]{2,1,0:T(8,128)(2,1)} %copy.329), calls=%async_computation | async-start | bytes 262144 | tf_op jit(solution)/shard_map/while/body/eval_jaxpr/all_to_all | solution.py:189
  96.9 12.8 %all-to-all-start.1 = ((f32[32,12,128]{2,1,0:T(8,128)}), f32[32,12,128]{2,1,0:T(8,128)S(1)}, u32[]{:S(2)}, u32[]{:S(2)}) async-start(f32[32,12,128]{2,1,0:T(8,128)} %copy.335), calls=%async_computation.1 | async-start | bytes 524288 | tf_op jit(solution)/shard_map/while/body/eval_jaxpr/all_to_all | solution.py:200
  110.5 9.1 %slice-start = ((s8[8388608]{0:T(1024)(128)(4,1)}), s8[4194304]{0:T(1024)(128)(4,1)S(1)}, s32[]{:S(2)}) async-start(s8[8388608]{0:T(1024)(128)(4,1)} %bitcast.290), calls=%async_computation.5 | async-start | bytes 8388608 | tf_op jit(solution)/shard_map/while
  110.5 9.1 %slice-start.1 = ((s8[8388608]{0:T(1024)(128)(4,1)}), s8[4194304]{0:T(1024)(128)(4,1)S(1)}, s32[]{:S(2)}) async-start(s8[8388608]{0:T(1024)(128)(4,1)} %bitcast.290), calls=%async_computation.6 | async-start | bytes 8388608 | tf_op jit(solution)/shard_map/while
  136.3 11.1 %all-to-all-start.2 = ((bf16[32,12,128]{2,1,0:T(8,128)(2,1)}), bf16[32,12,128]{2,1,0:T(8,128)(2,1)S(1)}, u32[]{:S(2)}, u32[]{:S(2)}) async-start(bf16[32,12,128]{2,1,0:T(8,128)(2,1)} %copy.231), calls=%async_computation.2 | async-start | bytes 262144 | tf_op jit(solution)/shard_map/all_to_all | solution.py:189
  139.3 0.8 copy-start.1
  164.0 12.8 %all-to-all-start.3 = ((f32[32,12,128]{2,1,0:T(8,128)}), f32[32,12,128]{2,1,0:T(8,128)S(1)}, u32[]{:S(2)}, u32[]{:S(2)}) async-start(f32[32,12,128]{2,1,0:T(8,128)} %copy.237), calls=%async_computation.3 | async-start | bytes 524288 | tf_op jit(solution)/shard_map/all_to_all | solution.py:200
  178.7 7.5 %copy-start.6 = (f32[3,2048]{1,0:T(4,128)S(1)}, f32[3,2048]{1,0:T(4,128)}, u32[]{:S(2)}) copy-start(f32[3,2048]{1,0:T(4,128)} %get-tuple-element.312) | copy-start | bytes 73732
  203.1 2.5 %copy-start.7 = (f32[4]{0:T(128)}, f32[4]{0:T(128)S(1)}, u32[]{:S(2)}) copy-start(f32[4]{0:T(128)S(1)} %add_sqrt_fusion) | copy-start | bytes 52

commit v6 on v4

--- a/solution.py
+++ b/solution.py
@@ -29,7 +29,9 @@
         hi_ref[...] = jnp.zeros_like(hi_ref)
         lo_ref[...] = jnp.zeros_like(lo_ref)
 
-    field = jnp.dot(lhs_ref[...], tab_ref[...], preferred_element_type=jnp.float32)
+    lhs = lhs_ref[...]
+    field = jnp.dot(lhs, tab_ref[0:pairs, :], preferred_element_type=jnp.float32)
+    field = field + jnp.dot(lhs, tab_ref[pairs:2 * pairs, :], preferred_element_type=jnp.float32)
     width = field.shape[1]
     product = (field.reshape(items, rows, width) * tide_ref[...][None, :, :]).reshape(
         items * rows, width
@@ -50,7 +52,7 @@
     nlon = tables_upper.shape[1]
     pairs = 2 * slots
     stacked = jnp.concatenate([div_real, -div_imag], axis=0).reshape(pairs, items * lays * rows)
-    lhs = jnp.concatenate([stacked, stacked], axis=0).T
+    lhs = stacked.T
     tabs = jnp.concatenate([tables_upper, tables_lower], axis=0)
     block = 2048
     mixed = items * lays * rows
@@ -62,7 +64,7 @@
         ),
         grid=(nlon // block,),
         in_specs=[
-            pl.BlockSpec((mixed, 2 * pairs), lambda k: (0, 0)),
+            pl.BlockSpec((mixed, pairs), lambda k: (0, 0)),
             pl.BlockSpec((2 * pairs, block), lambda k: (0, k)),
             pl.BlockSpec((rows, block), lambda k: (0, k)),
         ],

time: 193 us -> 198 us (1.026)
  Pallas kernels: 21.9 us -> 26.7 us
    pallas_call x3, Pallas kernels: 21.9 us -> 26.7 us  [tide_term(): pl.pallas_call(functools.partial(tide_kernel, items * lays, pairs, rows),...]
where the time goes in v6:
time: 198 us; the launch traced here: 197 us
  waiting for transfers between devices  50.8 us (26%)
  matrix products  43.7 us (22%)
  Pallas kernels  26.7 us (13%)
  other arithmetic  24.9 us (13%)
  starting transfers between devices  20.4 us (10%)
  local copies, waits for them, and re-layouts  17.7 us (9%)
  blocking collectives  9.67 us (5%)
    all_to_all x3, waiting for transfers between devices, one_step(): returned = lax.all_to_all(back, axes, 0, 0, tiled=True)  30.3 us
    pallas_call x3, Pallas kernels, tide_term(): pl.pallas_call(functools.partial(tide_kernel, items * lays, pairs, rows),...  26.7 us
    all_to_all x3, waiting for transfers between devices, one_step(): received = lax.all_to_all(sent, axes, 0, 0, tiled=True)  20.4 us
    dot_general x3, matrix products, one_step(): jnp.einsum('svcj,slj->svcl', spectral_b, legendre, preferred_element_type...  18.1 us
    dot_general x3, matrix products, one_step(): jnp.einsum('svcl,slj->svcj', weighted, legendre, preferred_element_type=j...  15.6 us
    all_to_all x3, starting transfers between devices, one_step(): received = lax.all_to_all(sent, axes, 0, 0, tiled=True)  12.7 us
    all_to_all x1, blocking collectives, exchange_sum(): gathered = lax.all_to_all(rows, ('lat', 'wave'), 0, 0, tiled=True)  9.67 us
    all_to_all x3, starting transfers between devices, one_step(): returned = lax.all_to_all(back, axes, 0, 0, tiled=True)  7.75 us
  transfers between devices with their start and end apart: 6, of which 6 were waited for; matrix products, arithmetic and copies ran while one was open for 3% of the time, Pallas kernels for 0%

profile of v6, /device:TPU:0, one launch (start us, length us, event | category | flops | bytes accessed | tf_op | source)
XLA Modules:
  0.0 196.6 jit_solution(1432254199789277898)
XLA Ops:
  0.7 2.8 %fusion.48 = (f32[32,4096]{1,0:T(8,128)S(1)}, f32[32,4096]{1,0:T(8,128)S(1)}) fusion(s32[32]{0:T(128)} %param.15), kind=kLoop, calls=%fused_computation.79 | loop fusion | flops 1835008 | bytes 1048704 | tf_op jit(solution)/shard_map/cos | solution.py:21
  3.6 0.6 dynamic_slice.3
  4.9 0.7 fusion.50
  6.0 1.3 copy.111
  7.3 1.0 pad_maximum_fusion.3
  8.4 172.0 %while.13 = (s32[]{:T(128)}, f32[1,4,18,2048]{3,1,2,0:T(4,128)S(1)}, f32[2048]{0:T(1024)S(1)}, f32[1,1,3,2048]{3,2,1,0:T(4,128)S(1)}, bf16[1,2048,2048]{2,1,0:T(...) while((s32[]{:T(128)}, ...), condition=%wide.region_1.2_spmd.clone, body=%wide.region_0.1_spmd.clone.sunk | while | flops 3230992384 | bytes 42803588 | solution.py:231
  8.7 6.0 %fusion.91 = bf16[4,18,2048]{2,1,0:T(8,128)(2,1)S(1)} fusion(bf16[1,2048,2048]{2,1,0:T(8,128)(2,1)} %get-tuple-element.428, bf16[4,18,2048]{2,0,1:T(4,128)(2,1)S(1)} %convert_bitcast_fusion.2), kind=kOutput, calls=%fused_computation.8.clone.1 | convolution fusion | flops 604127232 | bytes 8978432 | tf_op jit(solution)/shard_map/while/body/eval_jaxpr/svcj,slj->svcl/dot_general | solution.py:184
  15.6 0.7 copy.164
  16.3 7.3 %all-to-all-start = ((bf16[32,12,128]{2,1,0:T(8,128)(2,1)}), bf16[32,12,128]{2,1,0:T(8,128)(2,1)S(1)}, u32[]{:S(2)}, u32[]{:S(2)}) async-start(bf16[32,12,128]{2,1,0:T(8,128)(2,1)} %copy.164), calls=%async_computation | async-start | bytes 262144 | tf_op jit(solution)/shard_map/while/body/eval_jaxpr/all_to_all | solution.py:189
  23.8 0.7 fusion.98
  24.5 0.7 compare_convert_fusion.2
  25.2 6.8 %all-to-all-done = bf16[32,12,128]{2,1,0:T(8,128)(2,1)S(1)} async-done(((bf16[32,12,128]{2,1,0:T(8,128)(2,1)}), bf16[32,12,128]{2,1,0:T(8,128)(2,1)S(1)}, u32[]{:S(2)}, u32[]{:S(2)}) %all-to-all-start) | async-done | bytes 98336 | tf_op jit(solution)/shard_map/while/body/eval_jaxpr/all_to_all | solution.py:189
  32.9 0.8 maximum_bitcast_fusion.2.lhs_ref
  33.7 8.9 %eval_jaxpr.3 = (f32[768,128]{1,0:T(8,128)}, f32[768,64]{1,0:T(8,128)}) custom-call(bf16[768,64]{1,0:T(8,128)(2,1)} %maximum_bitcast_fusion.2.lhs_ref, bf16[128,4096]{1,0:T(8,128)(2,1)} %get-tuple-element.432.tab_ref, f32[64,4096]{1,0:T(8,128)} %get-tuple-element.433.tide_ref), custom_call_target="tpu_custom_call" | custom-call | flops 2013265920 | bytes 2686976 | tf_op jit(solution)/shard_map/while/body/eval_jaxpr/pallas_call | solution.py:59
  42.6 1.4 multiply_bitcast_fusion.2
  44.5 0.4 pad_maximum_fusion.7
  45.2 0.8 copy.170
  46.0 2.6 %all-to-all-start.1 = ((f32[32,12,128]{2,1,0:T(8,128)}), f32[32,12,128]{2,1,0:T(8,128)S(1)}, u32[]{:S(2)}, u32[]{:S(2)}) async-start(f32[32,12,128]{2,1,0:T(8,128)} %copy.170), calls=%async_computation.1 | async-start | bytes 524288 | tf_op jit(solution)/shard_map/while/body/eval_jaxpr/all_to_all | solution.py:200
  48.7 10.1 %all-to-all-done.1 = f32[32,12,128]{2,1,0:T(8,128)S(1)} async-done(((f32[32,12,128]{2,1,0:T(8,128)}), f32[32,12,128]{2,1,0:T(8,128)S(1)}, u32[]{:S(2)}, u32[]{:S(2)}) %all-to-all-start.1) | async-done | bytes 196640 | tf_op jit(solution)/shard_map/while/body/eval_jaxpr/all_to_all | solution.py:200
  59.6 5.2 %fusion.96 = f32[1,4,18,2048]{3,2,1,0:T(8,128)S(1)} fusion(bf16[1,2048,2048]{2,1,0:T(8,128)(2,1)} %get-tuple-element.428, f32[1,4,18,2048]{3,1,2,0:T(4,128)S(1)} %get-tuple-element.409, bf16[4,18,2048]{2,0,1:T(4,128)(2,1)S(1)} %bitcast.197, f32[2048]{0:T(1024)S(1)} %bitcast.212), kind=kOutput, calls=%fused_computation.7.clone.1 | convolution fusion | flops 604274688 | bytes 9871360 | tf_op jit(solution)/shard_map/while/body/eval_jaxpr/svcl,slj->svcj/dot_general | solution.py:218
  65.3 0.7 convolution_bitcast_fusion.9
  65.9 0.7 fusion.99
  66.7 0.7 convolution_bitcast_fusion.10
  67.3 0.6 convolution_bitcast_fusion.11
  68.9 6.0 %fusion.91 = bf16[4,18,2048]{2,1,0:T(8,128)(2,1)S(1)} fusion(bf16[1,2048,2048]{2,1,0:T(8,128)(2,1)} %get-tuple-element.428, bf16[4,18,2048]{2,0,1:T(4,128)(2,1)S(1)} %convert_bitcast_fusion.2), kind=kOutput, calls=%fused_computation.8.clone.1 | convolution fusion | flops 604127232 | bytes 8978432 | tf_op jit(solution)/shard_map/while/body/eval_jaxpr/svcj,slj->svcl/dot_general | solution.py:184
  75.8 0.7 copy.164
  76.5 2.7 %all-to-all-start = ((bf16[32,12,128]{2,1,0:T(8,128)(2,1)}), bf16[32,12,128]{2,1,0:T(8,128)(2,1)S(1)}, u32[]{:S(2)}, u32[]{:S(2)}) async-start(bf16[32,12,128]{2,1,0:T(8,128)(2,1)} %copy.164), calls=%async_computation | async-start | bytes 262144 | tf_op jit(solution)/shard_map/while/body/eval_jaxpr/all_to_all | solution.py:189
  79.5 0.7 fusion.98
  80.2 0.7 compare_convert_fusion.2
  80.8 6.8 %all-to-all-done = bf16[32,12,128]{2,1,0:T(8,128)(2,1)S(1)} async-done(((bf16[32,12,128]{2,1,0:T(8,128)(2,1)}), bf16[32,12,128]{2,1,0:T(8,128)(2,1)S(1)}, u32[]{:S(2)}, u32[]{:S(2)}) %all-to-all-start) | async-done | bytes 98336 | tf_op jit(solution)/shard_map/while/body/eval_jaxpr/all_to_all | solution.py:189
  88.6 0.8 maximum_bitcast_fusion.2.lhs_ref
  89.4 8.9 %eval_jaxpr.3 = (f32[768,128]{1,0:T(8,128)}, f32[768,64]{1,0:T(8,128)}) custom-call(bf16[768,64]{1,0:T(8,128)(2,1)} %maximum_bitcast_fusion.2.lhs_ref, bf16[128,4096]{1,0:T(8,128)(2,1)} %get-tuple-element.432.tab_ref, f32[64,4096]{1,0:T(8,128)} %get-tuple-element.433.tide_ref), custom_call_target="tpu_custom_call" | custom-call | flops 2013265920 | bytes 2686976 | tf_op jit(solution)/shard_map/while/body/eval_jaxpr/pallas_call | solution.py:59
  98.3 1.4 multiply_bitcast_fusion.2
  100.2 0.4 pad_maximum_fusion.7
  100.9 0.8 copy.170
  101.7 2.6 %all-to-all-start.1 = ((f32[32,12,128]{2,1,0:T(8,128)}), f32[32,12,128]{2,1,0:T(8,128)S(1)}, u32[]{:S(2)}, u32[]{:S(2)}) async-start(f32[32,12,128]{2,1,0:T(8,128)} %copy.170), calls=%async_computation.1 | async-start | bytes 524288 | tf_op jit(solution)/shard_map/while/body/eval_jaxpr/all_to_all | solution.py:200
  104.4 10.1 %all-to-all-done.1 = f32[32,12,128]{2,1,0:T(8,128)S(1)} async-done(((f32[32,12,128]{2,1,0:T(8,128)}), f32[32,12,128]{2,1,0:T(8,128)S(1)}, u32[]{:S(2)}, u32[]{:S(2)}) %all-to-all-start.1) | async-done | bytes 196640 | tf_op jit(solution)/shard_map/while/body/eval_jaxpr/all_to_all | solution.py:200
  115.3 5.2 %fusion.96 = f32[1,4,18,2048]{3,2,1,0:T(8,128)S(1)} fusion(bf16[1,2048,2048]{2,1,0:T(8,128)(2,1)} %get-tuple-element.428, f32[1,4,18,2048]{3,1,2,0:T(4,128)S(1)} %get-tuple-element.409, bf16[4,18,2048]{2,0,1:T(4,128)(2,1)S(1)} %bitcast.197, f32[2048]{0:T(1024)S(1)} %bitcast.212), kind=kOutput, calls=%fused_computation.7.clone.1 | convolution fusion | flops 604274688 | bytes 9871360 | tf_op jit(solution)/shard_map/while/body/eval_jaxpr/svcl,slj->svcj/dot_general | solution.py:218
  120.9 0.7 convolution_bitcast_fusion.9
  121.6 0.7 fusion.99
  122.3 0.7 convolution_bitcast_fusion.10
  123.0 0.6 convolution_bitcast_fusion.11
  124.6 6.0 %fusion.91 = bf16[4,18,2048]{2,1,0:T(8,128)(2,1)S(1)} fusion(bf16[1,2048,2048]{2,1,0:T(8,128)(2,1)} %get-tuple-element.428, bf16[4,18,2048]{2,0,1:T(4,128)(2,1)S(1)} %convert_bitcast_fusion.2), kind=kOutput, calls=%fused_computation.8.clone.1 | convolution fusion | flops 604127232 | bytes 8978432 | tf_op jit(solution)/shard_map/while/body/eval_jaxpr/svcj,slj->svcl/dot_general | solution.py:184
  131.5 0.7 copy.164
  132.2 2.7 %all-to-all-start = ((bf16[32,12,128]{2,1,0:T(8,128)(2,1)}), bf16[32,12,128]{2,1,0:T(8,128)(2,1)S(1)}, u32[]{:S(2)}, u32[]{:S(2)}) async-start(bf16[32,12,128]{2,1,0:T(8,128)(2,1)} %copy.164), calls=%async_computation | async-start | bytes 262144 | tf_op jit(solution)/shard_map/while/body/eval_jaxpr/all_to_all | solution.py:189
  135.2 0.7 fusion.98
  135.8 0.7 compare_convert_fusion.2
  136.5 6.8 %all-to-all-done = bf16[32,12,128]{2,1,0:T(8,128)(2,1)S(1)} async-done(((bf16[32,12,128]{2,1,0:T(8,128)(2,1)}), bf16[32,12,128]{2,1,0:T(8,128)(2,1)S(1)}, u32[]{:S(2)}, u32[]{:S(2)}) %all-to-all-start) | async-done | bytes 98336 | tf_op jit(solution)/shard_map/while/body/eval_jaxpr/all_to_all | solution.py:189
  144.2 0.8 maximum_bitcast_fusion.2.lhs_ref
  145.0 8.9 %eval_jaxpr.3 = (f32[768,128]{1,0:T(8,128)}, f32[768,64]{1,0:T(8,128)}) custom-call(bf16[768,64]{1,0:T(8,128)(2,1)} %maximum_bitcast_fusion.2.lhs_ref, bf16[128,4096]{1,0:T(8,128)(2,1)} %get-tuple-element.432.tab_ref, f32[64,4096]{1,0:T(8,128)} %get-tuple-element.433.tide_ref), custom_call_target="tpu_custom_call" | custom-call | flops 2013265920 | bytes 2686976 | tf_op jit(solution)/shard_map/while/body/eval_jaxpr/pallas_call | solution.py:59
  153.9 1.4 multiply_bitcast_fusion.2
  155.8 0.4 pad_maximum_fusion.7
  156.5 0.8 copy.170
  157.4 2.6 %all-to-all-start.1 = ((f32[32,12,128]{2,1,0:T(8,128)}), f32[32,12,128]{2,1,0:T(8,128)S(1)}, u32[]{:S(2)}, u32[]{:S(2)}) async-start(f32[32,12,128]{2,1,0:T(8,128)} %copy.170), calls=%async_computation.1 | async-start | bytes 524288 | tf_op jit(solution)/shard_map/while/body/eval_jaxpr/all_to_all | solution.py:200
  160.0 10.1 %all-to-all-done.1 = f32[32,12,128]{2,1,0:T(8,128)S(1)} async-done(((f32[32,12,128]{2,1,0:T(8,128)}), f32[32,12,128]{2,1,0:T(8,128)S(1)}, u32[]{:S(2)}, u32[]{:S(2)}) %all-to-all-start.1) | async-done | bytes 196640 | tf_op jit(solution)/shard_map/while/body/eval_jaxpr/all_to_all | solution.py:200
  171.0 5.2 %fusion.96 = f32[1,4,18,2048]{3,2,1,0:T(8,128)S(1)} fusion(bf16[1,2048,2048]{2,1,0:T(8,128)(2,1)} %get-tuple-element.428, f32[1,4,18,2048]{3,1,2,0:T(4,128)S(1)} %get-tuple-element.409, bf16[4,18,2048]{2,0,1:T(4,128)(2,1)S(1)} %bitcast.197, f32[2048]{0:T(1024)S(1)} %bitcast.212), kind=kOutput, calls=%fused_computation.7.clone.1 | convolution fusion | flops 604274688 | bytes 9871360 | tf_op jit(solution)/shard_map/while/body/eval_jaxpr/svcl,slj->svcj/dot_general | solution.py:218
  176.6 0.7 convolution_bitcast_fusion.9
  177.3 0.7 fusion.99
  178.0 0.7 convolution_bitcast_fusion.10
  178.7 0.6 convolution_bitcast_fusion.11
  180.8 2.4 %multiply_reduce_fusion.1 = (f32[4,4]{1,0:T(4,128)S(1)}, f32[4,4]{1,0:T(4,128)S(1)}) fusion(f32[4,18,2048]{2,0,1:T(4,128)S(1)} %bitcast.194, f32[4,18,2048]{2,1,0:T(8,128)} %copy.111, f32[4,18,2048]{2,0,1:T(4,128)S(1)} %fusion.61), kind=kLoop, calls=%fused_computation.56 | loop fusion | flops 2359264 | bytes 1769600 | tf_op jit(solution)/shard_map/reduce_sum | solution.py:233
  183.4 9.7 %all_to_all.24 = f32[32,1,36]{2,1,0:T(1,128)S(1)} all-to-all(f32[32,1,36]{2,1,0:T(1,128)S(1)} %broadcast_in_dim.2), channel_id=1, replica_groups=mesh['lat'=8,'wave'=4] {'lat','wave'}, dimensions={0} | all-to-all | bytes 9216 | tf_op jit(solution)/shard_map/all_to_all | solution.py:129
  194.0 1.9 fusion.37
  195.9 0.7 copy.115
  (147 shorter events, 16.9 us)
Async XLA Ops:
  0.6 3.0 %copy-start.10 = (s32[32]{0:T(128)S(1)}, s32[32]{0:T(128)}, u32[]{:S(2)}) copy-start(s32[32]{0:T(128)} %param.15) | copy-start | bytes 388
  0.6 4.9 %copy-start.1 = (f32[1,4,18,2048]{3,1,2,0:T(4,128)S(1)}, f32[1,4,18,2048]{3,1,2,0:T(4,128)}, u32[]{:S(2)}) copy-start(f32[1,4,18,2048]{3,1,2,0:T(4,128)} %param.13) | copy-start | bytes 1769476
  3.5 2.4 %copy-start.9 = (s32[2048]{0:T(1024)S(1)}, s32[2048]{0:T(1024)}, u32[]{:S(2)}) copy-start(s32[2048]{0:T(1024)} %param.16) | copy-start | bytes 24580
  5.5 1.7 copy-start.8
  5.7 1.6 copy-start.2
  5.9 2.5 %copy-start = (f32[3,2048]{1,0:T(4,128)S(1)}, f32[3,2048]{1,0:T(4,128)}, u32[]{:S(2)}) copy-start(f32[3,2048]{1,0:T(4,128)} %param.19) | copy-start | bytes 73732
  5.9 2.5 %copy-start.4 = (f32[2048]{0:T(1024)S(1)}, f32[2048]{0:T(1024)}, u32[]{:S(2)}) copy-start(f32[2048]{0:T(1024)} %param.17) | copy-start | bytes 24580
  5.9 2.5 %copy-start.5 = (f32[3,3]{1,0:T(4,128)S(1)}, f32[3,3]{1,0:T(4,128)}, u32[]{:S(2)}) copy-start(f32[3,3]{1,0:T(4,128)} %param.21) | copy-start | bytes 112
  5.9 2.5 %copy-start.6 = (f32[3,3]{1,0:T(4,128)S(1)}, f32[3,3]{1,0:T(4,128)}, u32[]{:S(2)}) copy-start(f32[3,3]{1,0:T(4,128)} %param.22) | copy-start | bytes 112
  5.9 2.4 %copy-start.7 = (f32[3]{0:T(128)S(1)}, f32[3]{0:T(128)}, u32[]{:S(2)}) copy-start(f32[3]{0:T(128)} %param.23) | copy-start | bytes 40
  16.3 15.7 %all-to-all-start = ((bf16[32,12,128]{2,1,0:T(8,128)(2,1)}), bf16[32,12,128]{2,1,0:T(8,128)(2,1)S(1)}, u32[]{:S(2)}, u32[]{:S(2)}) async-start(bf16[32,12,128]{2,1,0:T(8,128)(2,1)} %copy.164), calls=%async_computation | async-start | bytes 262144 | tf_op jit(solution)/shard_map/while/body/eval_jaxpr/all_to_all | solution.py:189
  46.0 12.8 %all-to-all-start.1 = ((f32[32,12,128]{2,1,0:T(8,128)}), f32[32,12,128]{2,1,0:T(8,128)S(1)}, u32[]{:S(2)}, u32[]{:S(2)}) async-start(f32[32,12,128]{2,1,0:T(8,128)} %copy.170), calls=%async_computation.1 | async-start | bytes 524288 | tf_op jit(solution)/shard_map/while/body/eval_jaxpr/all_to_all | solution.py:200
  76.5 11.1 %all-to-all-start = ((bf16[32,12,128]{2,1,0:T(8,128)(2,1)}), bf16[32,12,128]{2,1,0:T(8,128)(2,1)S(1)}, u32[]{:S(2)}, u32[]{:S(2)}) async-start(bf16[32,12,128]{2,1,0:T(8,128)(2,1)} %copy.164), calls=%async_computation | async-start | bytes 262144 | tf_op jit(solution)/shard_map/while/body/eval_jaxpr/all_to_all | solution.py:189
  101.7 12.8 %all-to-all-start.1 = ((f32[32,12,128]{2,1,0:T(8,128)}), f32[32,12,128]{2,1,0:T(8,128)S(1)}, u32[]{:S(2)}, u32[]{:S(2)}) async-start(f32[32,12,128]{2,1,0:T(8,128)} %copy.170), calls=%async_computation.1 | async-start | bytes 524288 | tf_op jit(solution)/shard_map/while/body/eval_jaxpr/all_to_all | solution.py:200
  132.2 11.1 %all-to-all-start = ((bf16[32,12,128]{2,1,0:T(8,128)(2,1)}), bf16[32,12,128]{2,1,0:T(8,128)(2,1)S(1)}, u32[]{:S(2)}, u32[]{:S(2)}) async-start(bf16[32,12,128]{2,1,0:T(8,128)(2,1)} %copy.164), calls=%async_computation | async-start | bytes 262144 | tf_op jit(solution)/shard_map/while/body/eval_jaxpr/all_to_all | solution.py:189
  157.4 12.8 %all-to-all-start.1 = ((f32[32,12,128]{2,1,0:T(8,128)}), f32[32,12,128]{2,1,0:T(8,128)S(1)}, u32[]{:S(2)}, u32[]{:S(2)}) async-start(f32[32,12,128]{2,1,0:T(8,128)} %copy.170), calls=%async_computation.1 | async-start | bytes 524288 | tf_op jit(solution)/shard_map/while/body/eval_jaxpr/all_to_all | solution.py:200
  180.4 13.6 %copy-start.3 = (f32[1,4,18,2048]{3,1,2,0:T(4,128)S(1)}, f32[1,4,18,2048]{3,1,2,0:T(4,128)}, u32[]{:S(2)}) copy-start(f32[1,4,18,2048]{3,1,2,0:T(4,128)} %copy-done.2) | copy-start | bytes 1769476
  194.0 2.6 %copy-start.11 = (f32[4]{0:T(128)}, f32[4]{0:T(128)S(1)}, u32[]{:S(2)}) copy-start(f32[4]{0:T(128)S(1)} %add_sqrt_fusion) | copy-start | bytes 52

commit v7 on v4

--- a/solution.py
+++ b/solution.py
@@ -107,16 +107,16 @@
     laplace = (degree_f * (degree_f + 1.0) / float(ntrunc * ntrunc))[:, None, None, None, :]
     speeds = mode_speed[None, None, :, None, None]
     div_modes = jnp.einsum(
-        "pk,svkrj->svprj", layer_to_mode, explicit[:, :, :, 2:4, :], precision=HIGHEST_PRECISION
+        "pk,svkrj->svprj", layer_to_mode, explicit[:, :, :, 2:4, :], precision=lax.Precision.HIGH
     )
     height_modes = jnp.einsum(
-        "pk,svkrj->svprj", layer_to_mode, explicit[:, :, :, 4:6, :], precision=HIGHEST_PRECISION
+        "pk,svkrj->svprj", layer_to_mode, explicit[:, :, :, 4:6, :], precision=lax.Precision.HIGH
     )
     div_new = (div_modes + laplace * speeds * height_modes) / (1.0 + laplace * speeds * speeds)
     height_new = height_modes - speeds * div_new
-    div_layers = jnp.einsum("kp,svprj->svkrj", mode_to_layer, div_new, precision=HIGHEST_PRECISION)
+    div_layers = jnp.einsum("kp,svprj->svkrj", mode_to_layer, div_new, precision=lax.Precision.HIGH)
     height_layers = jnp.einsum(
-        "kp,svprj->svkrj", mode_to_layer, height_new, precision=HIGHEST_PRECISION
+        "kp,svprj->svkrj", mode_to_layer, height_new, precision=lax.Precision.HIGH
     )
     return jnp.concatenate([explicit[:, :, :, 0:2, :], div_layers, height_layers], axis=3)
 

time: 193 us -> 190 us (0.984)
  matrix products: 43.7 us -> 40.9 us
where the time goes in v7:
time: 190 us; the launch traced here: 189 us
  waiting for transfers between devices  50.8 us (27%)
  matrix products  40.9 us (22%)
  other arithmetic  25.2 us (13%)
  Pallas kernels  21.9 us (12%)
  starting transfers between devices  20.4 us (11%)
  local copies, waits for them, and re-layouts  17.7 us (9%)
  blocking collectives  9.66 us (5%)
    all_to_all x3, waiting for transfers between devices, one_step(): returned = lax.all_to_all(back, axes, 0, 0, tiled=True)  30.3 us
    pallas_call x3, Pallas kernels, tide_term(): pl.pallas_call(functools.partial(tide_kernel, items * lays, pairs, rows),...  21.9 us
    all_to_all x3, waiting for transfers between devices, one_step(): received = lax.all_to_all(sent, axes, 0, 0, tiled=True)  20.4 us
    dot_general x3, matrix products, one_step(): jnp.einsum('svcj,slj->svcl', spectral_b, legendre, preferred_element_type...  18.1 us
    dot_general x3, matrix products, one_step(): jnp.einsum('svcl,slj->svcj', weighted, legendre, preferred_element_type=j...  15.6 us
    all_to_all x3, starting transfers between devices, one_step(): received = lax.all_to_all(sent, axes, 0, 0, tiled=True)  12.7 us
    all_to_all x1, blocking collectives, exchange_sum(): gathered = lax.all_to_all(rows, ('lat', 'wave'), 0, 0, tiled=True)  9.66 us
    all_to_all x3, starting transfers between devices, one_step(): returned = lax.all_to_all(back, axes, 0, 0, tiled=True)  7.75 us
  transfers between devices with their start and end apart: 6, of which 6 were waited for; matrix products, arithmetic and copies ran while one was open for 3% of the time, Pallas kernels for 0%

profile of v7, /device:TPU:0, one launch (start us, length us, event | category | flops | bytes accessed | tf_op | source)
XLA Modules:
  0.0 189.3 jit_solution(4998405142427366139)
XLA Ops:
  0.7 2.8 %fusion.48 = (f32[32,4096]{1,0:T(8,128)S(1)}, f32[32,4096]{1,0:T(8,128)S(1)}) fusion(s32[32]{0:T(128)} %param.15), kind=kLoop, calls=%fused_computation.79 | loop fusion | flops 1835008 | bytes 1048704 | tf_op jit(solution)/shard_map/cos | solution.py:21
  3.6 0.6 dynamic_slice.3
  4.9 0.7 fusion.50
  6.0 1.3 copy.111
  7.3 1.0 pad_maximum_fusion.3
  8.4 164.7 %while.13 = (s32[]{:T(128)}, f32[1,4,18,2048]{3,1,2,0:T(4,128)S(1)}, f32[2048]{0:T(1024)S(1)}, f32[1,1,3,2048]{3,2,1,0:T(4,128)S(1)}, bf16[1,2048,2048]{2,1,0:T(...) while((s32[]{:T(128)}, ...), condition=%wide.region_1.2_spmd.clone, body=%wide.region_0.1_spmd.clone.sunk | while | flops 3228043264 | bytes 42901892 | solution.py:229
  8.7 6.0 %fusion.91 = bf16[4,18,2048]{2,1,0:T(8,128)(2,1)S(1)} fusion(bf16[1,2048,2048]{2,1,0:T(8,128)(2,1)} %get-tuple-element.428, bf16[4,18,2048]{2,0,1:T(4,128)(2,1)S(1)} %convert_bitcast_fusion.2), kind=kOutput, calls=%fused_computation.8.clone.1 | convolution fusion | flops 604127232 | bytes 8978432 | tf_op jit(solution)/shard_map/while/body/eval_jaxpr/svcj,slj->svcl/dot_general | solution.py:182
  15.6 0.7 copy.164
  16.3 7.3 %all-to-all-start = ((bf16[32,12,128]{2,1,0:T(8,128)(2,1)}), bf16[32,12,128]{2,1,0:T(8,128)(2,1)S(1)}, u32[]{:S(2)}, u32[]{:S(2)}) async-start(bf16[32,12,128]{2,1,0:T(8,128)(2,1)} %copy.164), calls=%async_computation | async-start | bytes 262144 | tf_op jit(solution)/shard_map/while/body/eval_jaxpr/all_to_all | solution.py:187
  23.8 0.7 fusion.98
  24.5 0.7 compare_convert_fusion.2
  25.2 6.8 %all-to-all-done = bf16[32,12,128]{2,1,0:T(8,128)(2,1)S(1)} async-done(((bf16[32,12,128]{2,1,0:T(8,128)(2,1)}), bf16[32,12,128]{2,1,0:T(8,128)(2,1)S(1)}, u32[]{:S(2)}, u32[]{:S(2)}) %all-to-all-start) | async-done | bytes 98336 | tf_op jit(solution)/shard_map/while/body/eval_jaxpr/all_to_all | solution.py:187
  32.1 0.4 fusion.92
  32.9 0.9 maximum_bitcast_fusion.2.lhs_ref
  33.8 7.3 %eval_jaxpr.3 = (f32[768,128]{1,0:T(8,128)}, f32[768,64]{1,0:T(8,128)}) custom-call(bf16[768,128]{1,0:T(8,128)(2,1)} %maximum_bitcast_fusion.2.lhs_ref, bf16[128,4096]{1,0:T(8,128)(2,1)} %get-tuple-element.432.tab_ref, f32[64,4096]{1,0:T(8,128)} %get-tuple-element.433.tide_ref), custom_call_target="tpu_custom_call" | custom-call | flops 2013265920 | bytes 2686976 | tf_op jit(solution)/shard_map/while/body/eval_jaxpr/pallas_call | solution.py:57
  41.1 1.4 multiply_bitcast_fusion.2
  43.0 0.4 pad_maximum_fusion.7
  43.7 0.8 copy.170
  44.5 2.6 %all-to-all-start.1 = ((f32[32,12,128]{2,1,0:T(8,128)}), f32[32,12,128]{2,1,0:T(8,128)S(1)}, u32[]{:S(2)}, u32[]{:S(2)}) async-start(f32[32,12,128]{2,1,0:T(8,128)} %copy.170), calls=%async_computation.1 | async-start | bytes 524288 | tf_op jit(solution)/shard_map/while/body/eval_jaxpr/all_to_all | solution.py:198
  47.2 10.1 %all-to-all-done.1 = f32[32,12,128]{2,1,0:T(8,128)S(1)} async-done(((f32[32,12,128]{2,1,0:T(8,128)}), f32[32,12,128]{2,1,0:T(8,128)S(1)}, u32[]{:S(2)}, u32[]{:S(2)}) %all-to-all-start.1) | async-done | bytes 196640 | tf_op jit(solution)/shard_map/while/body/eval_jaxpr/all_to_all | solution.py:198
  58.2 5.2 %fusion.96 = f32[1,4,18,2048]{3,2,1,0:T(8,128)S(1)} fusion(bf16[1,2048,2048]{2,1,0:T(8,128)(2,1)} %get-tuple-element.428, f32[1,4,18,2048]{3,1,2,0:T(4,128)S(1)} %get-tuple-element.409, bf16[4,18,2048]{2,0,1:T(4,128)(2,1)S(1)} %bitcast.197, f32[2048]{0:T(1024)S(1)} %bitcast.212), kind=kOutput, calls=%fused_computation.7.clone.1 | convolution fusion | flops 604274688 | bytes 9871360 | tf_op jit(solution)/shard_map/while/body/eval_jaxpr/svcl,slj->svcj/dot_general | solution.py:216
  63.8 0.4 convolution_bitcast_fusion.9
  64.2 0.5 fusion.99
  64.7 0.4 convolution_bitcast_fusion.10
  66.5 6.0 %fusion.91 = bf16[4,18,2048]{2,1,0:T(8,128)(2,1)S(1)} fusion(bf16[1,2048,2048]{2,1,0:T(8,128)(2,1)} %get-tuple-element.428, bf16[4,18,2048]{2,0,1:T(4,128)(2,1)S(1)} %convert_bitcast_fusion.2), kind=kOutput, calls=%fused_computation.8.clone.1 | convolution fusion | flops 604127232 | bytes 8978432 | tf_op jit(solution)/shard_map/while/body/eval_jaxpr/svcj,slj->svcl/dot_general | solution.py:182
  73.4 0.7 copy.164
  74.1 2.7 %all-to-all-start = ((bf16[32,12,128]{2,1,0:T(8,128)(2,1)}), bf16[32,12,128]{2,1,0:T(8,128)(2,1)S(1)}, u32[]{:S(2)}, u32[]{:S(2)}) async-start(bf16[32,12,128]{2,1,0:T(8,128)(2,1)} %copy.164), calls=%async_computation | async-start | bytes 262144 | tf_op jit(solution)/shard_map/while/body/eval_jaxpr/all_to_all | solution.py:187
  77.1 0.7 fusion.98
  77.7 0.7 compare_convert_fusion.2
  78.4 6.8 %all-to-all-done = bf16[32,12,128]{2,1,0:T(8,128)(2,1)S(1)} async-done(((bf16[32,12,128]{2,1,0:T(8,128)(2,1)}), bf16[32,12,128]{2,1,0:T(8,128)(2,1)S(1)}, u32[]{:S(2)}, u32[]{:S(2)}) %all-to-all-start) | async-done | bytes 98336 | tf_op jit(solution)/shard_map/while/body/eval_jaxpr/all_to_all | solution.py:187
  85.4 0.4 fusion.92
  86.1 0.9 maximum_bitcast_fusion.2.lhs_ref
  87.1 7.3 %eval_jaxpr.3 = (f32[768,128]{1,0:T(8,128)}, f32[768,64]{1,0:T(8,128)}) custom-call(bf16[768,128]{1,0:T(8,128)(2,1)} %maximum_bitcast_fusion.2.lhs_ref, bf16[128,4096]{1,0:T(8,128)(2,1)} %get-tuple-element.432.tab_ref, f32[64,4096]{1,0:T(8,128)} %get-tuple-element.433.tide_ref), custom_call_target="tpu_custom_call" | custom-call | flops 2013265920 | bytes 2686976 | tf_op jit(solution)/shard_map/while/body/eval_jaxpr/pallas_call | solution.py:57
  94.4 1.4 multiply_bitcast_fusion.2
  96.3 0.4 pad_maximum_fusion.7
  97.0 0.8 copy.170
  97.8 2.6 %all-to-all-start.1 = ((f32[32,12,128]{2,1,0:T(8,128)}), f32[32,12,128]{2,1,0:T(8,128)S(1)}, u32[]{:S(2)}, u32[]{:S(2)}) async-start(f32[32,12,128]{2,1,0:T(8,128)} %copy.170), calls=%async_computation.1 | async-start | bytes 524288 | tf_op jit(solution)/shard_map/while/body/eval_jaxpr/all_to_all | solution.py:198
  100.5 10.1 %all-to-all-done.1 = f32[32,12,128]{2,1,0:T(8,128)S(1)} async-done(((f32[32,12,128]{2,1,0:T(8,128)}), f32[32,12,128]{2,1,0:T(8,128)S(1)}, u32[]{:S(2)}, u32[]{:S(2)}) %all-to-all-start.1) | async-done | bytes 196640 | tf_op jit(solution)/shard_map/while/body/eval_jaxpr/all_to_all | solution.py:198
  111.4 5.2 %fusion.96 = f32[1,4,18,2048]{3,2,1,0:T(8,128)S(1)} fusion(bf16[1,2048,2048]{2,1,0:T(8,128)(2,1)} %get-tuple-element.428, f32[1,4,18,2048]{3,1,2,0:T(4,128)S(1)} %get-tuple-element.409, bf16[4,18,2048]{2,0,1:T(4,128)(2,1)S(1)} %bitcast.197, f32[2048]{0:T(1024)S(1)} %bitcast.212), kind=kOutput, calls=%fused_computation.7.clone.1 | convolution fusion | flops 604274688 | bytes 9871360 | tf_op jit(solution)/shard_map/while/body/eval_jaxpr/svcl,slj->svcj/dot_general | solution.py:216
  117.0 0.4 convolution_bitcast_fusion.9
  117.5 0.5 fusion.99
  117.9 0.4 convolution_bitcast_fusion.10
  119.8 6.0 %fusion.91 = bf16[4,18,2048]{2,1,0:T(8,128)(2,1)S(1)} fusion(bf16[1,2048,2048]{2,1,0:T(8,128)(2,1)} %get-tuple-element.428, bf16[4,18,2048]{2,0,1:T(4,128)(2,1)S(1)} %convert_bitcast_fusion.2), kind=kOutput, calls=%fused_computation.8.clone.1 | convolution fusion | flops 604127232 | bytes 8978432 | tf_op jit(solution)/shard_map/while/body/eval_jaxpr/svcj,slj->svcl/dot_general | solution.py:182
  126.7 0.7 copy.164
  127.3 2.7 %all-to-all-start = ((bf16[32,12,128]{2,1,0:T(8,128)(2,1)}), bf16[32,12,128]{2,1,0:T(8,128)(2,1)S(1)}, u32[]{:S(2)}, u32[]{:S(2)}) async-start(bf16[32,12,128]{2,1,0:T(8,128)(2,1)} %copy.164), calls=%async_computation | async-start | bytes 262144 | tf_op jit(solution)/shard_map/while/body/eval_jaxpr/all_to_all | solution.py:187
  130.3 0.7 fusion.98
  131.0 0.7 compare_convert_fusion.2
  131.6 6.8 %all-to-all-done = bf16[32,12,128]{2,1,0:T(8,128)(2,1)S(1)} async-done(((bf16[32,12,128]{2,1,0:T(8,128)(2,1)}), bf16[32,12,128]{2,1,0:T(8,128)(2,1)S(1)}, u32[]{:S(2)}, u32[]{:S(2)}) %all-to-all-start) | async-done | bytes 98336 | tf_op jit(solution)/shard_map/while/body/eval_jaxpr/all_to_all | solution.py:187
  138.6 0.4 fusion.92
  139.4 0.9 maximum_bitcast_fusion.2.lhs_ref
  140.3 7.3 %eval_jaxpr.3 = (f32[768,128]{1,0:T(8,128)}, f32[768,64]{1,0:T(8,128)}) custom-call(bf16[768,128]{1,0:T(8,128)(2,1)} %maximum_bitcast_fusion.2.lhs_ref, bf16[128,4096]{1,0:T(8,128)(2,1)} %get-tuple-element.432.tab_ref, f32[64,4096]{1,0:T(8,128)} %get-tuple-element.433.tide_ref), custom_call_target="tpu_custom_call" | custom-call | flops 2013265920 | bytes 2686976 | tf_op jit(solution)/shard_map/while/body/eval_jaxpr/pallas_call | solution.py:57
  147.6 1.4 multiply_bitcast_fusion.2
  149.5 0.4 pad_maximum_fusion.7
  150.2 0.8 copy.170
  151.0 2.6 %all-to-all-start.1 = ((f32[32,12,128]{2,1,0:T(8,128)}), f32[32,12,128]{2,1,0:T(8,128)S(1)}, u32[]{:S(2)}, u32[]{:S(2)}) async-start(f32[32,12,128]{2,1,0:T(8,128)} %copy.170), calls=%async_computation.1 | async-start | bytes 524288 | tf_op jit(solution)/shard_map/while/body/eval_jaxpr/all_to_all | solution.py:198
  153.7 10.1 %all-to-all-done.1 = f32[32,12,128]{2,1,0:T(8,128)S(1)} async-done(((f32[32,12,128]{2,1,0:T(8,128)}), f32[32,12,128]{2,1,0:T(8,128)S(1)}, u32[]{:S(2)}, u32[]{:S(2)}) %all-to-all-start.1) | async-done | bytes 196640 | tf_op jit(solution)/shard_map/while/body/eval_jaxpr/all_to_all | solution.py:198
  164.6 5.2 %fusion.96 = f32[1,4,18,2048]{3,2,1,0:T(8,128)S(1)} fusion(bf16[1,2048,2048]{2,1,0:T(8,128)(2,1)} %get-tuple-element.428, f32[1,4,18,2048]{3,1,2,0:T(4,128)S(1)} %get-tuple-element.409, bf16[4,18,2048]{2,0,1:T(4,128)(2,1)S(1)} %bitcast.197, f32[2048]{0:T(1024)S(1)} %bitcast.212), kind=kOutput, calls=%fused_computation.7.clone.1 | convolution fusion | flops 604274688 | bytes 9871360 | tf_op jit(solution)/shard_map/while/body/eval_jaxpr/svcl,slj->svcj/dot_general | solution.py:216
  170.3 0.4 convolution_bitcast_fusion.9
  170.7 0.5 fusion.99
  171.2 0.4 convolution_bitcast_fusion.10
  173.5 2.4 %multiply_reduce_fusion.1 = (f32[4,4]{1,0:T(4,128)S(1)}, f32[4,4]{1,0:T(4,128)S(1)}) fusion(f32[4,18,2048]{2,0,1:T(4,128)S(1)} %bitcast.194, f32[4,18,2048]{2,1,0:T(8,128)} %copy.111, f32[4,18,2048]{2,0,1:T(4,128)S(1)} %fusion.61), kind=kLoop, calls=%fused_computation.56 | loop fusion | flops 2359264 | bytes 1769600 | tf_op jit(solution)/shard_map/reduce_sum | solution.py:231
  176.2 9.7 %all_to_all.24 = f32[32,1,36]{2,1,0:T(1,128)S(1)} all-to-all(f32[32,1,36]{2,1,0:T(1,128)S(1)} %broadcast_in_dim.2), channel_id=1, replica_groups=mesh['lat'=8,'wave'=4] {'lat','wave'}, dimensions={0} | all-to-all | bytes 9216 | tf_op jit(solution)/shard_map/all_to_all | solution.py:127
  186.7 1.9 %fusion.37 = f32[1,4,18,2048]{3,1,2,0:T(4,128)} fusion(f32[1,4,18,2048]{3,1,2,0:T(4,128)S(1)} %get-tuple-element.178, f32[4]{0:T(128)S(1)} %add_sqrt_fusion, f32[4,4]{0,1:T(4,128)S(1)} %copy.113, f32[1,4,18,2048]{3,1,2,0:T(4,128)S(1)} %copy-done.3), kind=kOutput, calls=%fused_computation.59 | convolution fusion | flops 7372816 | bytes 1769552 | tf_op jit(solution)/shard_map/skcj,kv->svcj/dot_general | solution.py:236
  188.6 0.7 copy.115
  (147 shorter events, 16.6 us)
Async XLA Ops:
  0.6 3.0 %copy-start.10 = (s32[32]{0:T(128)S(1)}, s32[32]{0:T(128)}, u32[]{:S(2)}) copy-start(s32[32]{0:T(128)} %param.15) | copy-start | bytes 388
  0.6 4.9 %copy-start.1 = (f32[1,4,18,2048]{3,1,2,0:T(4,128)S(1)}, f32[1,4,18,2048]{3,1,2,0:T(4,128)}, u32[]{:S(2)}) copy-start(f32[1,4,18,2048]{3,1,2,0:T(4,128)} %param.13) | copy-start | bytes 1769476
  3.5 2.4 %copy-start.9 = (s32[2048]{0:T(1024)S(1)}, s32[2048]{0:T(1024)}, u32[]{:S(2)}) copy-start(s32[2048]{0:T(1024)} %param.16) | copy-start | bytes 24580
  5.5 1.7 copy-start.8
  5.7 1.6 copy-start.2
  5.9 2.5 %copy-start = (f32[3,2048]{1,0:T(4,128)S(1)}, f32[3,2048]{1,0:T(4,128)}, u32[]{:S(2)}) copy-start(f32[3,2048]{1,0:T(4,128)} %param.19) | copy-start | bytes 73732
  5.9 2.5 %copy-start.4 = (f32[2048]{0:T(1024)S(1)}, f32[2048]{0:T(1024)}, u32[]{:S(2)}) copy-start(f32[2048]{0:T(1024)} %param.17) | copy-start | bytes 24580
  5.9 2.5 %copy-start.5 = (f32[3,3]{1,0:T(4,128)S(1)}, f32[3,3]{1,0:T(4,128)}, u32[]{:S(2)}) copy-start(f32[3,3]{1,0:T(4,128)} %param.21) | copy-start | bytes 112
  5.9 2.5 %copy-start.6 = (f32[3,3]{1,0:T(4,128)S(1)}, f32[3,3]{1,0:T(4,128)}, u32[]{:S(2)}) copy-start(f32[3,3]{1,0:T(4,128)} %param.22) | copy-start | bytes 112
  5.9 2.4 %copy-start.7 = (f32[3]{0:T(128)S(1)}, f32[3]{0:T(128)}, u32[]{:S(2)}) copy-start(f32[3]{0:T(128)} %param.23) | copy-start | bytes 40
  16.3 15.7 %all-to-all-start = ((bf16[32,12,128]{2,1,0:T(8,128)(2,1)}), bf16[32,12,128]{2,1,0:T(8,128)(2,1)S(1)}, u32[]{:S(2)}, u32[]{:S(2)}) async-start(bf16[32,12,128]{2,1,0:T(8,128)(2,1)} %copy.164), calls=%async_computation | async-start | bytes 262144 | tf_op jit(solution)/shard_map/while/body/eval_jaxpr/all_to_all | solution.py:187
  44.5 12.8 %all-to-all-start.1 = ((f32[32,12,128]{2,1,0:T(8,128)}), f32[32,12,128]{2,1,0:T(8,128)S(1)}, u32[]{:S(2)}, u32[]{:S(2)}) async-start(f32[32,12,128]{2,1,0:T(8,128)} %copy.170), calls=%async_computation.1 | async-start | bytes 524288 | tf_op jit(solution)/shard_map/while/body/eval_jaxpr/all_to_all | solution.py:198
  74.1 11.1 %all-to-all-start = ((bf16[32,12,128]{2,1,0:T(8,128)(2,1)}), bf16[32,12,128]{2,1,0:T(8,128)(2,1)S(1)}, u32[]{:S(2)}, u32[]{:S(2)}) async-start(bf16[32,12,128]{2,1,0:T(8,128)(2,1)} %copy.164), calls=%async_computation | async-start | bytes 262144 | tf_op jit(solution)/shard_map/while/body/eval_jaxpr/all_to_all | solution.py:187
  97.8 12.8 %all-to-all-start.1 = ((f32[32,12,128]{2,1,0:T(8,128)}), f32[32,12,128]{2,1,0:T(8,128)S(1)}, u32[]{:S(2)}, u32[]{:S(2)}) async-start(f32[32,12,128]{2,1,0:T(8,128)} %copy.170), calls=%async_computation.1 | async-start | bytes 524288 | tf_op jit(solution)/shard_map/while/body/eval_jaxpr/all_to_all | solution.py:198
  127.3 11.1 %all-to-all-start = ((bf16[32,12,128]{2,1,0:T(8,128)(2,1)}), bf16[32,12,128]{2,1,0:T(8,128)(2,1)S(1)}, u32[]{:S(2)}, u32[]{:S(2)}) async-start(bf16[32,12,128]{2,1,0:T(8,128)(2,1)} %copy.164), calls=%async_computation | async-start | bytes 262144 | tf_op jit(solution)/shard_map/while/body/eval_jaxpr/all_to_all | solution.py:187
  151.0 12.8 %all-to-all-start.1 = ((f32[32,12,128]{2,1,0:T(8,128)}), f32[32,12,128]{2,1,0:T(8,128)S(1)}, u32[]{:S(2)}, u32[]{:S(2)}) async-start(f32[32,12,128]{2,1,0:T(8,128)} %copy.170), calls=%async_computation.1 | async-start | bytes 524288 | tf_op jit(solution)/shard_map/while/body/eval_jaxpr/all_to_all | solution.py:198
  173.1 13.6 %copy-start.3 = (f32[1,4,18,2048]{3,1,2,0:T(4,128)S(1)}, f32[1,4,18,2048]{3,1,2,0:T(4,128)}, u32[]{:S(2)}) copy-start(f32[1,4,18,2048]{3,1,2,0:T(4,128)} %copy-done.2) | copy-start | bytes 1769476
  186.7 2.6 %copy-start.11 = (f32[4]{0:T(128)}, f32[4]{0:T(128)S(1)}, u32[]{:S(2)}) copy-start(f32[4]{0:T(128)S(1)} %add_sqrt_fusion) | copy-start | bytes 52

commit v8 on v7

--- a/solution.py
+++ b/solution.py
@@ -170,14 +170,15 @@
     degrees = local_waves[:, None] + jnp.arange(ndeg, dtype=jnp.int32)[None, :]
     truncation = (degrees <= ntrunc).astype(jnp.float32)[:, None, None, :]
     basis = arnoldi_block * truncation
-    tables = angle_tables(wave_index, tide_height.shape[1])
-    tables_upper = tables.astype(jnp.bfloat16)
-    tables_lower = (tables - tables_upper.astype(jnp.float32)).astype(jnp.bfloat16)
     coriolis = (2 * lat_index + 1).astype(jnp.float32) / nlat - 1.0
     advect = (
         local_waves.astype(jnp.float32)[:, None, None, None] * zonal_flow[None, None, :, :] / ntrunc
     )
     def one_step(step_index, spectral):
+        step_waves, spectral = lax.optimization_barrier((wave_index, spectral))
+        tables = angle_tables(step_waves, tide_height.shape[1])
+        tables_upper = tables.astype(jnp.bfloat16)
+        tables_lower = (tables - tables_upper.astype(jnp.float32)).astype(jnp.bfloat16)
         spectral_b = spectral.astype(jnp.bfloat16)
         grid_b = jnp.einsum(
             "svcj,slj->svcl", spectral_b, legendre, preferred_element_type=jnp.float32

time: 190 us -> 189 us (level)
  waiting for transfers between devices: 50.8 us -> 40.5 us
  other arithmetic: 25.2 us -> 34.1 us
    all_to_all x3, waiting for transfers between devices: 20.4 us -> 10.2 us  [one_step(): received = lax.all_to_all(sent, axes, 0, 0, tiled=True)]
    cos x1 -> x3, other arithmetic: 2.83 us -> 6.33 us  [angle_tables(): return jnp.concatenate([jnp.cos(theta), jnp.sin(theta)], axis=0)]
    concatenate x1 -> x3, other arithmetic: 1.04 us -> 3.22 us  [tide_term(): tabs = jnp.concatenate([tables_upper, tables_lower], axis=0)]
  transfers between devices with their start and end apart: 6 -> 6, of which waited for: 6 -> 6; matrix products, arithmetic and copies ran while one was open for 3% -> 8% of each run, Pallas kernels for 0% -> 0%
where the time goes in v8:
time: 189 us; the launch traced here: 188 us
  matrix products  40.9 us (22%)
  waiting for transfers between devices  40.5 us (21%)
  other arithmetic  34.1 us (18%)
  Pallas kernels  21.5 us (11%)
  starting transfers between devices  20.4 us (11%)
  local copies, waits for them, and re-layouts  18.4 us (10%)
  blocking collectives  9.68 us (5%)
    all_to_all x3, waiting for transfers between devices, one_step(): returned = lax.all_to_all(back, axes, 0, 0, tiled=True)  30.3 us
    pallas_call x3, Pallas kernels, tide_term(): pl.pallas_call(functools.partial(tide_kernel, items * lays, pairs, rows),...  21.5 us
    dot_general x3, matrix products, one_step(): jnp.einsum('svcj,slj->svcl', spectral_b, legendre, preferred_element_type...  18.1 us
    dot_general x3, matrix products, one_step(): jnp.einsum('svcl,slj->svcj', weighted, legendre, preferred_element_type=j...  15.7 us
    all_to_all x3, starting transfers between devices, one_step(): received = lax.all_to_all(sent, axes, 0, 0, tiled=True)  12.7 us
    all_to_all x3, waiting for transfers between devices, one_step(): received = lax.all_to_all(sent, axes, 0, 0, tiled=True)  10.2 us
    all_to_all x1, blocking collectives, exchange_sum(): gathered = lax.all_to_all(rows, ('lat', 'wave'), 0, 0, tiled=True)  9.68 us
    all_to_all x3, starting transfers between devices, one_step(): returned = lax.all_to_all(back, axes, 0, 0, tiled=True)  7.75 us
  transfers between devices with their start and end apart: 6, of which 6 were waited for; matrix products, arithmetic and copies ran while one was open for 8% of the time, Pallas kernels for 0%

profile of v8, /device:TPU:0, one launch (start us, length us, event | category | flops | bytes accessed | tf_op | source)
XLA Modules:
  0.0 188.2 jit_solution(4624660983999432093)
XLA Ops:
  0.6 1.2 dynamic_slice.3
  2.5 0.7 fusion.50
  3.3 1.2 broadcast_multiply_fusion.2
  4.5 1.4 fusion.61
  6.1 1.3 copy.111
  7.4 164.3 %while.13 = (s32[]{:T(128)}, f32[1,4,18,2048]{3,1,2,0:T(4,128)S(1)}, s32[32]{0:T(128)S(1)}, f32[2048]{0:T(1024)S(1)}, f32[1,1,3,2048]{3,2,1,0:T(4,128)S(1)}, /*i...) while((s32[]{:T(128)}, ...), condition=%wide.region_1.2_spmd.clone, body=%wide.region_0.1_spmd.clone.sunk | while | flops 3234334720 | bytes 53387808 | solution.py:230
  7.6 6.0 %fusion.93 = bf16[4,18,2048]{2,1,0:T(8,128)(2,1)S(1)} fusion(bf16[1,2048,2048]{2,1,0:T(8,128)(2,1)} %get-tuple-element.447, bf16[4,18,2048]{2,0,1:T(4,128)(2,1)S(1)} %convert_bitcast_fusion.2), kind=kOutput, calls=%fused_computation.8.clone.1 | convolution fusion | flops 604127232 | bytes 8978432 | tf_op jit(solution)/shard_map/while/body/eval_jaxpr/svcj,slj->svcl/dot_general | solution.py:183
  14.5 0.7 copy.164
  15.2 7.3 %all-to-all-start = ((bf16[32,12,128]{2,1,0:T(8,128)(2,1)}), bf16[32,12,128]{2,1,0:T(8,128)(2,1)S(1)}, u32[]{:S(2)}, u32[]{:S(2)}) async-start(bf16[32,12,128]{2,1,0:T(8,128)(2,1)} %copy.164), calls=%async_computation | async-start | bytes 262144 | tf_op jit(solution)/shard_map/while/body/eval_jaxpr/all_to_all | solution.py:188
  22.5 2.1 %fusion.95 = (f32[32,4096]{1,0:T(8,128)S(1)}, f32[32,4096]{1,0:T(8,128)S(1)}) fusion(s32[32]{0:T(128)S(1)} %get-tuple-element.398), kind=kLoop, calls=%fused_computation.44.clone.1 | loop fusion | flops 1835008 | bytes 1048704 | tf_op jit(solution)/shard_map/while/body/eval_jaxpr/cos | solution.py:21
  25.0 0.7 fusion.102
  25.6 1.1 pad_maximum_fusion.8.tab_ref
  26.7 0.7 compare_convert_fusion.2
  27.5 3.4 %all-to-all-done = bf16[32,12,128]{2,1,0:T(8,128)(2,1)S(1)} async-done(((bf16[32,12,128]{2,1,0:T(8,128)(2,1)}), bf16[32,12,128]{2,1,0:T(8,128)(2,1)S(1)}, u32[]{:S(2)}, u32[]{:S(2)}) %all-to-all-start) | async-done | bytes 98336 | tf_op jit(solution)/shard_map/while/body/eval_jaxpr/all_to_all | solution.py:188
  31.0 0.4 fusion.94
  31.8 0.9 maximum_bitcast_fusion.2.lhs_ref
  32.7 7.2 %eval_jaxpr.4 = (f32[768,128]{1,0:T(8,128)}, f32[768,64]{1,0:T(8,128)}) custom-call(bf16[768,128]{1,0:T(8,128)(2,1)} %maximum_bitcast_fusion.2.lhs_ref, bf16[128,4096]{1,0:T(8,128)(2,1)} %pad_maximum_fusion.8.tab_ref, f32[64,4096]{1,0:T(8,128)S(1)} %copy-done.12), custom_call_target="tpu_custom_call" | custom-call | flops 2013265920 | bytes 2686976 | tf_op jit(solution)/shard_map/while/body/eval_jaxpr/pallas_call | solution.py:57
  39.9 1.4 multiply_bitcast_fusion.2
  41.8 0.4 pad_maximum_fusion.9
  42.5 0.8 copy.170
  43.4 2.6 %all-to-all-start.1 = ((f32[32,12,128]{2,1,0:T(8,128)}), f32[32,12,128]{2,1,0:T(8,128)S(1)}, u32[]{:S(2)}, u32[]{:S(2)}) async-start(f32[32,12,128]{2,1,0:T(8,128)} %copy.170), calls=%async_computation.1 | async-start | bytes 524288 | tf_op jit(solution)/shard_map/while/body/eval_jaxpr/all_to_all | solution.py:199
  46.0 10.1 %all-to-all-done.1 = f32[32,12,128]{2,1,0:T(8,128)S(1)} async-done(((f32[32,12,128]{2,1,0:T(8,128)}), f32[32,12,128]{2,1,0:T(8,128)S(1)}, u32[]{:S(2)}, u32[]{:S(2)}) %all-to-all-start.1) | async-done | bytes 196640 | tf_op jit(solution)/shard_map/while/body/eval_jaxpr/all_to_all | solution.py:199
  57.0 5.2 %fusion.100 = f32[1,4,18,2048]{3,2,1,0:T(8,128)S(1)} fusion(bf16[1,2048,2048]{2,1,0:T(8,128)(2,1)} %get-tuple-element.447, f32[1,4,18,2048]{3,1,2,0:T(4,128)S(1)} %get-tuple-element.395, bf16[4,18,2048]{2,0,1:T(4,128)(2,1)S(1)} %bitcast.197, f32[2048]{0:T(1024)S(1)} %bitcast.212), kind=kOutput, calls=%fused_computation.7.clone.1 | convolution fusion | flops 604274688 | bytes 9871360 | tf_op jit(solution)/shard_map/while/body/eval_jaxpr/svcl,slj->svcj/dot_general | solution.py:217
  63.1 0.5 fusion.103
  65.4 6.0 %fusion.93 = bf16[4,18,2048]{2,1,0:T(8,128)(2,1)S(1)} fusion(bf16[1,2048,2048]{2,1,0:T(8,128)(2,1)} %get-tuple-element.447, bf16[4,18,2048]{2,0,1:T(4,128)(2,1)S(1)} %convert_bitcast_fusion.2), kind=kOutput, calls=%fused_computation.8.clone.1 | convolution fusion | flops 604127232 | bytes 8978432 | tf_op jit(solution)/shard_map/while/body/eval_jaxpr/svcj,slj->svcl/dot_general | solution.py:183
  72.3 0.7 copy.164
  73.0 2.7 %all-to-all-start = ((bf16[32,12,128]{2,1,0:T(8,128)(2,1)}), bf16[32,12,128]{2,1,0:T(8,128)(2,1)S(1)}, u32[]{:S(2)}, u32[]{:S(2)}) async-start(bf16[32,12,128]{2,1,0:T(8,128)(2,1)} %copy.164), calls=%async_computation | async-start | bytes 262144 | tf_op jit(solution)/shard_map/while/body/eval_jaxpr/all_to_all | solution.py:188
  75.7 2.1 %fusion.95 = (f32[32,4096]{1,0:T(8,128)S(1)}, f32[32,4096]{1,0:T(8,128)S(1)}) fusion(s32[32]{0:T(128)S(1)} %get-tuple-element.398), kind=kLoop, calls=%fused_computation.44.clone.1 | loop fusion | flops 1835008 | bytes 1048704 | tf_op jit(solution)/shard_map/while/body/eval_jaxpr/cos | solution.py:21
  78.2 0.7 fusion.102
  78.8 1.1 pad_maximum_fusion.8.tab_ref
  79.9 0.7 compare_convert_fusion.2
  80.7 3.4 %all-to-all-done = bf16[32,12,128]{2,1,0:T(8,128)(2,1)S(1)} async-done(((bf16[32,12,128]{2,1,0:T(8,128)(2,1)}), bf16[32,12,128]{2,1,0:T(8,128)(2,1)S(1)}, u32[]{:S(2)}, u32[]{:S(2)}) %all-to-all-start) | async-done | bytes 98336 | tf_op jit(solution)/shard_map/while/body/eval_jaxpr/all_to_all | solution.py:188
  84.2 0.4 fusion.94
  85.0 0.9 maximum_bitcast_fusion.2.lhs_ref
  85.9 7.2 %eval_jaxpr.4 = (f32[768,128]{1,0:T(8,128)}, f32[768,64]{1,0:T(8,128)}) custom-call(bf16[768,128]{1,0:T(8,128)(2,1)} %maximum_bitcast_fusion.2.lhs_ref, bf16[128,4096]{1,0:T(8,128)(2,1)} %pad_maximum_fusion.8.tab_ref, f32[64,4096]{1,0:T(8,128)S(1)} %copy-done.12), custom_call_target="tpu_custom_call" | custom-call | flops 2013265920 | bytes 2686976 | tf_op jit(solution)/shard_map/while/body/eval_jaxpr/pallas_call | solution.py:57
  93.1 1.4 multiply_bitcast_fusion.2
  95.0 0.4 pad_maximum_fusion.9
  95.7 0.8 copy.170
  96.5 2.6 %all-to-all-start.1 = ((f32[32,12,128]{2,1,0:T(8,128)}), f32[32,12,128]{2,1,0:T(8,128)S(1)}, u32[]{:S(2)}, u32[]{:S(2)}) async-start(f32[32,12,128]{2,1,0:T(8,128)} %copy.170), calls=%async_computation.1 | async-start | bytes 524288 | tf_op jit(solution)/shard_map/while/body/eval_jaxpr/all_to_all | solution.py:199
  99.2 10.1 %all-to-all-done.1 = f32[32,12,128]{2,1,0:T(8,128)S(1)} async-done(((f32[32,12,128]{2,1,0:T(8,128)}), f32[32,12,128]{2,1,0:T(8,128)S(1)}, u32[]{:S(2)}, u32[]{:S(2)}) %all-to-all-start.1) | async-done | bytes 196640 | tf_op jit(solution)/shard_map/while/body/eval_jaxpr/all_to_all | solution.py:199
  110.2 5.2 %fusion.100 = f32[1,4,18,2048]{3,2,1,0:T(8,128)S(1)} fusion(bf16[1,2048,2048]{2,1,0:T(8,128)(2,1)} %get-tuple-element.447, f32[1,4,18,2048]{3,1,2,0:T(4,128)S(1)} %get-tuple-element.395, bf16[4,18,2048]{2,0,1:T(4,128)(2,1)S(1)} %bitcast.197, f32[2048]{0:T(1024)S(1)} %bitcast.212), kind=kOutput, calls=%fused_computation.7.clone.1 | convolution fusion | flops 604274688 | bytes 9871360 | tf_op jit(solution)/shard_map/while/body/eval_jaxpr/svcl,slj->svcj/dot_general | solution.py:217
  116.3 0.5 fusion.103
  118.5 6.0 %fusion.93 = bf16[4,18,2048]{2,1,0:T(8,128)(2,1)S(1)} fusion(bf16[1,2048,2048]{2,1,0:T(8,128)(2,1)} %get-tuple-element.447, bf16[4,18,2048]{2,0,1:T(4,128)(2,1)S(1)} %convert_bitcast_fusion.2), kind=kOutput, calls=%fused_computation.8.clone.1 | convolution fusion | flops 604127232 | bytes 8978432 | tf_op jit(solution)/shard_map/while/body/eval_jaxpr/svcj,slj->svcl/dot_general | solution.py:183
  125.4 0.7 copy.164
  126.1 2.7 %all-to-all-start = ((bf16[32,12,128]{2,1,0:T(8,128)(2,1)}), bf16[32,12,128]{2,1,0:T(8,128)(2,1)S(1)}, u32[]{:S(2)}, u32[]{:S(2)}) async-start(bf16[32,12,128]{2,1,0:T(8,128)(2,1)} %copy.164), calls=%async_computation | async-start | bytes 262144 | tf_op jit(solution)/shard_map/while/body/eval_jaxpr/all_to_all | solution.py:188
  128.8 2.1 %fusion.95 = (f32[32,4096]{1,0:T(8,128)S(1)}, f32[32,4096]{1,0:T(8,128)S(1)}) fusion(s32[32]{0:T(128)S(1)} %get-tuple-element.398), kind=kLoop, calls=%fused_computation.44.clone.1 | loop fusion | flops 1835008 | bytes 1048704 | tf_op jit(solution)/shard_map/while/body/eval_jaxpr/cos | solution.py:21
  131.4 0.7 fusion.102
  132.0 1.1 pad_maximum_fusion.8.tab_ref
  133.1 0.7 compare_convert_fusion.2
  133.8 3.4 %all-to-all-done = bf16[32,12,128]{2,1,0:T(8,128)(2,1)S(1)} async-done(((bf16[32,12,128]{2,1,0:T(8,128)(2,1)}), bf16[32,12,128]{2,1,0:T(8,128)(2,1)S(1)}, u32[]{:S(2)}, u32[]{:S(2)}) %all-to-all-start) | async-done | bytes 98336 | tf_op jit(solution)/shard_map/while/body/eval_jaxpr/all_to_all | solution.py:188
  137.4 0.4 fusion.94
  138.2 0.9 maximum_bitcast_fusion.2.lhs_ref
  139.1 7.2 %eval_jaxpr.4 = (f32[768,128]{1,0:T(8,128)}, f32[768,64]{1,0:T(8,128)}) custom-call(bf16[768,128]{1,0:T(8,128)(2,1)} %maximum_bitcast_fusion.2.lhs_ref, bf16[128,4096]{1,0:T(8,128)(2,1)} %pad_maximum_fusion.8.tab_ref, f32[64,4096]{1,0:T(8,128)S(1)} %copy-done.12), custom_call_target="tpu_custom_call" | custom-call | flops 2013265920 | bytes 2686976 | tf_op jit(solution)/shard_map/while/body/eval_jaxpr/pallas_call | solution.py:57
  146.3 1.4 multiply_bitcast_fusion.2
  148.2 0.4 pad_maximum_fusion.9
  148.9 0.8 copy.170
  149.7 2.6 %all-to-all-start.1 = ((f32[32,12,128]{2,1,0:T(8,128)}), f32[32,12,128]{2,1,0:T(8,128)S(1)}, u32[]{:S(2)}, u32[]{:S(2)}) async-start(f32[32,12,128]{2,1,0:T(8,128)} %copy.170), calls=%async_computation.1 | async-start | bytes 524288 | tf_op jit(solution)/shard_map/while/body/eval_jaxpr/all_to_all | solution.py:199
  152.4 10.1 %all-to-all-done.1 = f32[32,12,128]{2,1,0:T(8,128)S(1)} async-done(((f32[32,12,128]{2,1,0:T(8,128)}), f32[32,12,128]{2,1,0:T(8,128)S(1)}, u32[]{:S(2)}, u32[]{:S(2)}) %all-to-all-start.1) | async-done | bytes 196640 | tf_op jit(solution)/shard_map/while/body/eval_jaxpr/all_to_all | solution.py:199
  163.3 5.2 %fusion.100 = f32[1,4,18,2048]{3,2,1,0:T(8,128)S(1)} fusion(bf16[1,2048,2048]{2,1,0:T(8,128)(2,1)} %get-tuple-element.447, f32[1,4,18,2048]{3,1,2,0:T(4,128)S(1)} %get-tuple-element.395, bf16[4,18,2048]{2,0,1:T(4,128)(2,1)S(1)} %bitcast.197, f32[2048]{0:T(1024)S(1)} %bitcast.212), kind=kOutput, calls=%fused_computation.7.clone.1 | convolution fusion | flops 604274688 | bytes 9871360 | tf_op jit(solution)/shard_map/while/body/eval_jaxpr/svcl,slj->svcj/dot_general | solution.py:217
  169.4 0.5 fusion.103
  172.2 2.5 %multiply_reduce_fusion.1 = (f32[4,4]{1,0:T(4,128)S(1)}, f32[4,4]{1,0:T(4,128)S(1)}) fusion(f32[4,18,2048]{2,0,1:T(4,128)S(1)} %bitcast.194, f32[4,18,2048]{2,1,0:T(8,128)} %copy.111, f32[4,18,2048]{2,0,1:T(4,128)} %copy-done), kind=kLoop, calls=%fused_computation.71 | loop fusion | flops 2359264 | bytes 1769600 | tf_op jit(solution)/shard_map/reduce_sum | solution.py:232
  175.0 9.7 %all_to_all.26 = f32[32,1,36]{2,1,0:T(1,128)S(1)} all-to-all(f32[32,1,36]{2,1,0:T(1,128)S(1)} %broadcast_in_dim.2), channel_id=1, replica_groups=mesh['lat'=8,'wave'=4] {'lat','wave'}, dimensions={0} | all-to-all | bytes 9216 | tf_op jit(solution)/shard_map/all_to_all | solution.py:127
  185.6 1.9 %fusion.46 = f32[1,4,18,2048]{3,1,2,0:T(4,128)} fusion(f32[1,4,18,2048]{3,1,2,0:T(4,128)S(1)} %get-tuple-element.186, f32[4]{0:T(128)S(1)} %add_sqrt_fusion, f32[4,4]{0,1:T(4,128)S(1)} %copy.113, f32[1,4,18,2048]{3,1,2,0:T(4,128)S(1)} %copy-done.3), kind=kOutput, calls=%fused_computation.74 | convolution fusion | flops 7372816 | bytes 1769552 | tf_op jit(solution)/shard_map/skcj,kv->svcj/dot_general | solution.py:237
  187.5 0.7 copy.115
  (161 shorter events, 19.2 us)
Async XLA Ops:
  0.6 5.4 %copy-start.10 = (s32[2048]{0:T(1024)S(1)}, s32[2048]{0:T(1024)}, u32[]{:S(2)}) copy-start(s32[2048]{0:T(1024)} %param.16) | copy-start | bytes 24580
  3.2 4.2 %copy-start.8 = (f32[3,2048]{1,0:T(4,128)S(1)}, f32[3,2048]{1,0:T(4,128)}, u32[]{:S(2)}) copy-start(f32[3,2048]{1,0:T(4,128)} %param.18) | copy-start | bytes 73732
  3.2 4.2 %copy-start.1 = (f32[3,2048]{1,0:T(4,128)S(1)}, f32[3,2048]{1,0:T(4,128)}, u32[]{:S(2)}) copy-start(f32[3,2048]{1,0:T(4,128)} %param.19) | copy-start | bytes 73732
  3.2 4.2 %copy-start.4 = (f32[2048]{0:T(1024)S(1)}, f32[2048]{0:T(1024)}, u32[]{:S(2)}) copy-start(f32[2048]{0:T(1024)} %param.17) | copy-start | bytes 24580
  3.2 4.2 %copy-start.5 = (f32[3,3]{1,0:T(4,128)S(1)}, f32[3,3]{1,0:T(4,128)}, u32[]{:S(2)}) copy-start(f32[3,3]{1,0:T(4,128)} %param.21) | copy-start | bytes 112
  3.2 4.2 %copy-start.6 = (f32[3,3]{1,0:T(4,128)S(1)}, f32[3,3]{1,0:T(4,128)}, u32[]{:S(2)}) copy-start(f32[3,3]{1,0:T(4,128)} %param.22) | copy-start | bytes 112
  3.3 4.2 %copy-start.7 = (f32[3]{0:T(128)S(1)}, f32[3]{0:T(128)}, u32[]{:S(2)}) copy-start(f32[3]{0:T(128)} %param.23) | copy-start | bytes 40
  3.3 4.2 %copy-start.9 = (s32[32]{0:T(128)S(1)}, s32[32]{0:T(128)}, u32[]{:S(2)}) copy-start(s32[32]{0:T(128)} %param.15) | copy-start | bytes 388
  4.5 2.8 %copy-start.2 = (f32[1,4,18,2048]{3,1,2,0:T(4,128)}, f32[1,4,18,2048]{3,1,2,0:T(4,128)S(1)}, u32[]{:S(2)}) copy-start(f32[1,4,18,2048]{3,1,2,0:T(4,128)S(1)} %broadcast_multiply_fusion.2) | copy-start | bytes 1769476
  6.0 1.4 copy-start
  15.2 15.7 %all-to-all-start = ((bf16[32,12,128]{2,1,0:T(8,128)(2,1)}), bf16[32,12,128]{2,1,0:T(8,128)(2,1)S(1)}, u32[]{:S(2)}, u32[]{:S(2)}) async-start(bf16[32,12,128]{2,1,0:T(8,128)(2,1)} %copy.164), calls=%async_computation | async-start | bytes 262144 | tf_op jit(solution)/shard_map/while/body/eval_jaxpr/all_to_all | solution.py:188
  26.7 6.0 %copy-start.12 = (f32[64,4096]{1,0:T(8,128)S(1)}, f32[64,4096]{1,0:T(8,128)}, u32[]{:S(2)}) copy-start(f32[64,4096]{1,0:T(8,128)} %get-tuple-element.451.tide_ref) | copy-start | bytes 3145732 | tf_op jit(solution)/shard_map/while
  43.4 12.8 %all-to-all-start.1 = ((f32[32,12,128]{2,1,0:T(8,128)}), f32[32,12,128]{2,1,0:T(8,128)S(1)}, u32[]{:S(2)}, u32[]{:S(2)}) async-start(f32[32,12,128]{2,1,0:T(8,128)} %copy.170), calls=%async_computation.1 | async-start | bytes 524288 | tf_op jit(solution)/shard_map/while/body/eval_jaxpr/all_to_all | solution.py:199
  73.0 11.1 %all-to-all-start = ((bf16[32,12,128]{2,1,0:T(8,128)(2,1)}), bf16[32,12,128]{2,1,0:T(8,128)(2,1)S(1)}, u32[]{:S(2)}, u32[]{:S(2)}) async-start(bf16[32,12,128]{2,1,0:T(8,128)(2,1)} %copy.164), calls=%async_computation | async-start | bytes 262144 | tf_op jit(solution)/shard_map/while/body/eval_jaxpr/all_to_all | solution.py:188
  79.9 6.0 %copy-start.12 = (f32[64,4096]{1,0:T(8,128)S(1)}, f32[64,4096]{1,0:T(8,128)}, u32[]{:S(2)}) copy-start(f32[64,4096]{1,0:T(8,128)} %get-tuple-element.451.tide_ref) | copy-start | bytes 3145732 | tf_op jit(solution)/shard_map/while
  96.5 12.8 %all-to-all-start.1 = ((f32[32,12,128]{2,1,0:T(8,128)}), f32[32,12,128]{2,1,0:T(8,128)S(1)}, u32[]{:S(2)}, u32[]{:S(2)}) async-start(f32[32,12,128]{2,1,0:T(8,128)} %copy.170), calls=%async_computation.1 | async-start | bytes 524288 | tf_op jit(solution)/shard_map/while/body/eval_jaxpr/all_to_all | solution.py:199
  126.1 11.1 %all-to-all-start = ((bf16[32,12,128]{2,1,0:T(8,128)(2,1)}), bf16[32,12,128]{2,1,0:T(8,128)(2,1)S(1)}, u32[]{:S(2)}, u32[]{:S(2)}) async-start(bf16[32,12,128]{2,1,0:T(8,128)(2,1)} %copy.164), calls=%async_computation | async-start | bytes 262144 | tf_op jit(solution)/shard_map/while/body/eval_jaxpr/all_to_all | solution.py:188
  133.1 6.0 %copy-start.12 = (f32[64,4096]{1,0:T(8,128)S(1)}, f32[64,4096]{1,0:T(8,128)}, u32[]{:S(2)}) copy-start(f32[64,4096]{1,0:T(8,128)} %get-tuple-element.451.tide_ref) | copy-start | bytes 3145732 | tf_op jit(solution)/shard_map/while
  149.7 12.8 %all-to-all-start.1 = ((f32[32,12,128]{2,1,0:T(8,128)}), f32[32,12,128]{2,1,0:T(8,128)S(1)}, u32[]{:S(2)}, u32[]{:S(2)}) async-start(f32[32,12,128]{2,1,0:T(8,128)} %copy.170), calls=%async_computation.1 | async-start | bytes 524288 | tf_op jit(solution)/shard_map/while/body/eval_jaxpr/all_to_all | solution.py:199
  171.8 13.8 %copy-start.3 = (f32[1,4,18,2048]{3,1,2,0:T(4,128)S(1)}, f32[1,4,18,2048]{3,1,2,0:T(4,128)}, u32[]{:S(2)}) copy-start(f32[1,4,18,2048]{3,1,2,0:T(4,128)} %copy-done.2) | copy-start | bytes 1769476
  185.6 2.6 %copy-start.11 = (f32[4]{0:T(128)}, f32[4]{0:T(128)S(1)}, u32[]{:S(2)}) copy-start(f32[4]{0:T(128)S(1)} %add_sqrt_fusion) | copy-start | bytes 52

commit v9 on v8

--- a/solution.py
+++ b/solution.py
@@ -235,7 +235,7 @@
     projection, self_sum, gram = exchange_sum((local_proj, local_self, local_gram), device_count)
     hessenberg = projection / entries
     residual = spectral - jnp.einsum(
-        "skcj,kv->svcj", basis, hessenberg, precision=HIGHEST_PRECISION
+        "skcj,kv->svcj", basis, hessenberg, precision=lax.Precision.HIGH
     )
     quadratic = jnp.einsum("kv,kq,qv->v", hessenberg, gram, hessenberg, precision=HIGHEST_PRECISION)
     norm_sq = (self_sum - 2.0 * jnp.sum(hessenberg * projection, axis=0) + quadratic) / entries

time: 189 us -> 189 us (level)
  no operation moved by 1% of the time
where the time goes in v9:
time: 189 us; the launch traced here: 188 us
  matrix products  40.5 us (21%)
  waiting for transfers between devices  40.5 us (21%)
  other arithmetic  34.1 us (18%)
  Pallas kernels  21.5 us (11%)
  starting transfers between devices  20.4 us (11%)
  local copies, waits for them, and re-layouts  18.4 us (10%)
  blocking collectives  9.68 us (5%)
    all_to_all x3, waiting for transfers between devices, one_step(): returned = lax.all_to_all(back, axes, 0, 0, tiled=True)  30.3 us
    pallas_call x3, Pallas kernels, tide_term(): pl.pallas_call(functools.partial(tide_kernel, items * lays, pairs, rows),...  21.5 us
    dot_general x3, matrix products, one_step(): jnp.einsum('svcj,slj->svcl', spectral_b, legendre, preferred_element_type...  18.1 us
    dot_general x3, matrix products, one_step(): jnp.einsum('svcl,slj->svcj', weighted, legendre, preferred_element_type=j...  15.7 us
    all_to_all x3, starting transfers between devices, one_step(): received = lax.all_to_all(sent, axes, 0, 0, tiled=True)  12.7 us
    all_to_all x3, waiting for transfers between devices, one_step(): received = lax.all_to_all(sent, axes, 0, 0, tiled=True)  10.2 us
    all_to_all x1, blocking collectives, exchange_sum(): gathered = lax.all_to_all(rows, ('lat', 'wave'), 0, 0, tiled=True)  9.68 us
    all_to_all x3, starting transfers between devices, one_step(): returned = lax.all_to_all(back, axes, 0, 0, tiled=True)  7.75 us
  transfers between devices with their start and end apart: 6, of which 6 were waited for; matrix products, arithmetic and copies ran while one was open for 8% of the time, Pallas kernels for 0%

profile of v9, /device:TPU:0, one launch (start us, length us, event | category | flops | bytes accessed | tf_op | source)
XLA Modules:
  0.0 187.7 jit_solution(9339314466445694969)
XLA Ops:
  0.6 1.2 dynamic_slice.3
  2.5 0.7 fusion.50
  3.3 1.2 broadcast_multiply_fusion.2
  4.5 1.4 fusion.61
  6.1 1.3 copy.111
  7.4 164.3 %while.13 = (s32[]{:T(128)}, f32[1,4,18,2048]{3,1,2,0:T(4,128)S(1)}, s32[32]{0:T(128)S(1)}, f32[2048]{0:T(1024)S(1)}, f32[1,1,3,2048]{3,2,1,0:T(4,128)S(1)}, /*i...) while((s32[]{:T(128)}, ...), condition=%wide.region_1.2_spmd.clone, body=%wide.region_0.1_spmd.clone.sunk | while | flops 3234334720 | bytes 53387808 | solution.py:230
  7.6 6.0 %fusion.93 = bf16[4,18,2048]{2,1,0:T(8,128)(2,1)S(1)} fusion(bf16[1,2048,2048]{2,1,0:T(8,128)(2,1)} %get-tuple-element.447, bf16[4,18,2048]{2,0,1:T(4,128)(2,1)S(1)} %convert_bitcast_fusion.2), kind=kOutput, calls=%fused_computation.8.clone.1 | convolution fusion | flops 604127232 | bytes 8978432 | tf_op jit(solution)/shard_map/while/body/eval_jaxpr/svcj,slj->svcl/dot_general | solution.py:183
  14.5 0.7 copy.164
  15.2 7.3 %all-to-all-start = ((bf16[32,12,128]{2,1,0:T(8,128)(2,1)}), bf16[32,12,128]{2,1,0:T(8,128)(2,1)S(1)}, u32[]{:S(2)}, u32[]{:S(2)}) async-start(bf16[32,12,128]{2,1,0:T(8,128)(2,1)} %copy.164), calls=%async_computation | async-start | bytes 262144 | tf_op jit(solution)/shard_map/while/body/eval_jaxpr/all_to_all | solution.py:188
  22.5 2.1 %fusion.95 = (f32[32,4096]{1,0:T(8,128)S(1)}, f32[32,4096]{1,0:T(8,128)S(1)}) fusion(s32[32]{0:T(128)S(1)} %get-tuple-element.398), kind=kLoop, calls=%fused_computation.44.clone.1 | loop fusion | flops 1835008 | bytes 1048704 | tf_op jit(solution)/shard_map/while/body/eval_jaxpr/cos | solution.py:21
  25.0 0.7 fusion.102
  25.6 1.1 pad_maximum_fusion.8.tab_ref
  26.7 0.7 compare_convert_fusion.2
  27.5 3.4 %all-to-all-done = bf16[32,12,128]{2,1,0:T(8,128)(2,1)S(1)} async-done(((bf16[32,12,128]{2,1,0:T(8,128)(2,1)}), bf16[32,12,128]{2,1,0:T(8,128)(2,1)S(1)}, u32[]{:S(2)}, u32[]{:S(2)}) %all-to-all-start) | async-done | bytes 98336 | tf_op jit(solution)/shard_map/while/body/eval_jaxpr/all_to_all | solution.py:188
  31.0 0.4 fusion.94
  31.8 0.9 maximum_bitcast_fusion.2.lhs_ref
  32.7 7.2 %eval_jaxpr.4 = (f32[768,128]{1,0:T(8,128)}, f32[768,64]{1,0:T(8,128)}) custom-call(bf16[768,128]{1,0:T(8,128)(2,1)} %maximum_bitcast_fusion.2.lhs_ref, bf16[128,4096]{1,0:T(8,128)(2,1)} %pad_maximum_fusion.8.tab_ref, f32[64,4096]{1,0:T(8,128)S(1)} %copy-done.12), custom_call_target="tpu_custom_call" | custom-call | flops 2013265920 | bytes 2686976 | tf_op jit(solution)/shard_map/while/body/eval_jaxpr/pallas_call | solution.py:57
  39.9 1.4 multiply_bitcast_fusion.2
  41.8 0.4 pad_maximum_fusion.9
  42.5 0.8 copy.170
  43.4 2.6 %all-to-all-start.1 = ((f32[32,12,128]{2,1,0:T(8,128)}), f32[32,12,128]{2,1,0:T(8,128)S(1)}, u32[]{:S(2)}, u32[]{:S(2)}) async-start(f32[32,12,128]{2,1,0:T(8,128)} %copy.170), calls=%async_computation.1 | async-start | bytes 524288 | tf_op jit(solution)/shard_map/while/body/eval_jaxpr/all_to_all | solution.py:199
  46.0 10.1 %all-to-all-done.1 = f32[32,12,128]{2,1,0:T(8,128)S(1)} async-done(((f32[32,12,128]{2,1,0:T(8,128)}), f32[32,12,128]{2,1,0:T(8,128)S(1)}, u32[]{:S(2)}, u32[]{:S(2)}) %all-to-all-start.1) | async-done | bytes 196640 | tf_op jit(solution)/shard_map/while/body/eval_jaxpr/all_to_all | solution.py:199
  57.0 5.2 %fusion.100 = f32[1,4,18,2048]{3,2,1,0:T(8,128)S(1)} fusion(bf16[1,2048,2048]{2,1,0:T(8,128)(2,1)} %get-tuple-element.447, f32[1,4,18,2048]{3,1,2,0:T(4,128)S(1)} %get-tuple-element.395, bf16[4,18,2048]{2,0,1:T(4,128)(2,1)S(1)} %bitcast.197, f32[2048]{0:T(1024)S(1)} %bitcast.212), kind=kOutput, calls=%fused_computation.7.clone.1 | convolution fusion | flops 604274688 | bytes 9871360 | tf_op jit(solution)/shard_map/while/body/eval_jaxpr/svcl,slj->svcj/dot_general | solution.py:217
  63.1 0.5 fusion.103
  65.4 6.0 %fusion.93 = bf16[4,18,2048]{2,1,0:T(8,128)(2,1)S(1)} fusion(bf16[1,2048,2048]{2,1,0:T(8,128)(2,1)} %get-tuple-element.447, bf16[4,18,2048]{2,0,1:T(4,128)(2,1)S(1)} %convert_bitcast_fusion.2), kind=kOutput, calls=%fused_computation.8.clone.1 | convolution fusion | flops 604127232 | bytes 8978432 | tf_op jit(solution)/shard_map/while/body/eval_jaxpr/svcj,slj->svcl/dot_general | solution.py:183
  72.3 0.7 copy.164
  73.0 2.7 %all-to-all-start = ((bf16[32,12,128]{2,1,0:T(8,128)(2,1)}), bf16[32,12,128]{2,1,0:T(8,128)(2,1)S(1)}, u32[]{:S(2)}, u32[]{:S(2)}) async-start(bf16[32,12,128]{2,1,0:T(8,128)(2,1)} %copy.164), calls=%async_computation | async-start | bytes 262144 | tf_op jit(solution)/shard_map/while/body/eval_jaxpr/all_to_all | solution.py:188
  75.7 2.1 %fusion.95 = (f32[32,4096]{1,0:T(8,128)S(1)}, f32[32,4096]{1,0:T(8,128)S(1)}) fusion(s32[32]{0:T(128)S(1)} %get-tuple-element.398), kind=kLoop, calls=%fused_computation.44.clone.1 | loop fusion | flops 1835008 | bytes 1048704 | tf_op jit(solution)/shard_map/while/body/eval_jaxpr/cos | solution.py:21
  78.2 0.7 fusion.102
  78.8 1.1 pad_maximum_fusion.8.tab_ref
  79.9 0.7 compare_convert_fusion.2
  80.7 3.4 %all-to-all-done = bf16[32,12,128]{2,1,0:T(8,128)(2,1)S(1)} async-done(((bf16[32,12,128]{2,1,0:T(8,128)(2,1)}), bf16[32,12,128]{2,1,0:T(8,128)(2,1)S(1)}, u32[]{:S(2)}, u32[]{:S(2)}) %all-to-all-start) | async-done | bytes 98336 | tf_op jit(solution)/shard_map/while/body/eval_jaxpr/all_to_all | solution.py:188
  84.2 0.4 fusion.94
  85.0 0.9 maximum_bitcast_fusion.2.lhs_ref
  85.9 7.2 %eval_jaxpr.4 = (f32[768,128]{1,0:T(8,128)}, f32[768,64]{1,0:T(8,128)}) custom-call(bf16[768,128]{1,0:T(8,128)(2,1)} %maximum_bitcast_fusion.2.lhs_ref, bf16[128,4096]{1,0:T(8,128)(2,1)} %pad_maximum_fusion.8.tab_ref, f32[64,4096]{1,0:T(8,128)S(1)} %copy-done.12), custom_call_target="tpu_custom_call" | custom-call | flops 2013265920 | bytes 2686976 | tf_op jit(solution)/shard_map/while/body/eval_jaxpr/pallas_call | solution.py:57
  93.1 1.4 multiply_bitcast_fusion.2
  95.0 0.4 pad_maximum_fusion.9
  95.7 0.8 copy.170
  96.5 2.6 %all-to-all-start.1 = ((f32[32,12,128]{2,1,0:T(8,128)}), f32[32,12,128]{2,1,0:T(8,128)S(1)}, u32[]{:S(2)}, u32[]{:S(2)}) async-start(f32[32,12,128]{2,1,0:T(8,128)} %copy.170), calls=%async_computation.1 | async-start | bytes 524288 | tf_op jit(solution)/shard_map/while/body/eval_jaxpr/all_to_all | solution.py:199
  99.2 10.1 %all-to-all-done.1 = f32[32,12,128]{2,1,0:T(8,128)S(1)} async-done(((f32[32,12,128]{2,1,0:T(8,128)}), f32[32,12,128]{2,1,0:T(8,128)S(1)}, u32[]{:S(2)}, u32[]{:S(2)}) %all-to-all-start.1) | async-done | bytes 196640 | tf_op jit(solution)/shard_map/while/body/eval_jaxpr/all_to_all | solution.py:199
  110.2 5.2 %fusion.100 = f32[1,4,18,2048]{3,2,1,0:T(8,128)S(1)} fusion(bf16[1,2048,2048]{2,1,0:T(8,128)(2,1)} %get-tuple-element.447, f32[1,4,18,2048]{3,1,2,0:T(4,128)S(1)} %get-tuple-element.395, bf16[4,18,2048]{2,0,1:T(4,128)(2,1)S(1)} %bitcast.197, f32[2048]{0:T(1024)S(1)} %bitcast.212), kind=kOutput, calls=%fused_computation.7.clone.1 | convolution fusion | flops 604274688 | bytes 9871360 | tf_op jit(solution)/shard_map/while/body/eval_jaxpr/svcl,slj->svcj/dot_general | solution.py:217
  116.3 0.5 fusion.103
  118.5 6.0 %fusion.93 = bf16[4,18,2048]{2,1,0:T(8,128)(2,1)S(1)} fusion(bf16[1,2048,2048]{2,1,0:T(8,128)(2,1)} %get-tuple-element.447, bf16[4,18,2048]{2,0,1:T(4,128)(2,1)S(1)} %convert_bitcast_fusion.2), kind=kOutput, calls=%fused_computation.8.clone.1 | convolution fusion | flops 604127232 | bytes 8978432 | tf_op jit(solution)/shard_map/while/body/eval_jaxpr/svcj,slj->svcl/dot_general | solution.py:183
  125.4 0.7 copy.164
  126.1 2.7 %all-to-all-start = ((bf16[32,12,128]{2,1,0:T(8,128)(2,1)}), bf16[32,12,128]{2,1,0:T(8,128)(2,1)S(1)}, u32[]{:S(2)}, u32[]{:S(2)}) async-start(bf16[32,12,128]{2,1,0:T(8,128)(2,1)} %copy.164), calls=%async_computation | async-start | bytes 262144 | tf_op jit(solution)/shard_map/while/body/eval_jaxpr/all_to_all | solution.py:188
  128.8 2.1 %fusion.95 = (f32[32,4096]{1,0:T(8,128)S(1)}, f32[32,4096]{1,0:T(8,128)S(1)}) fusion(s32[32]{0:T(128)S(1)} %get-tuple-element.398), kind=kLoop, calls=%fused_computation.44.clone.1 | loop fusion | flops 1835008 | bytes 1048704 | tf_op jit(solution)/shard_map/while/body/eval_jaxpr/cos | solution.py:21
  131.4 0.7 fusion.102
  132.0 1.1 pad_maximum_fusion.8.tab_ref
  133.1 0.7 compare_convert_fusion.2
  133.8 3.4 %all-to-all-done = bf16[32,12,128]{2,1,0:T(8,128)(2,1)S(1)} async-done(((bf16[32,12,128]{2,1,0:T(8,128)(2,1)}), bf16[32,12,128]{2,1,0:T(8,128)(2,1)S(1)}, u32[]{:S(2)}, u32[]{:S(2)}) %all-to-all-start) | async-done | bytes 98336 | tf_op jit(solution)/shard_map/while/body/eval_jaxpr/all_to_all | solution.py:188
  137.4 0.4 fusion.94
  138.2 0.9 maximum_bitcast_fusion.2.lhs_ref
  139.1 7.2 %eval_jaxpr.4 = (f32[768,128]{1,0:T(8,128)}, f32[768,64]{1,0:T(8,128)}) custom-call(bf16[768,128]{1,0:T(8,128)(2,1)} %maximum_bitcast_fusion.2.lhs_ref, bf16[128,4096]{1,0:T(8,128)(2,1)} %pad_maximum_fusion.8.tab_ref, f32[64,4096]{1,0:T(8,128)S(1)} %copy-done.12), custom_call_target="tpu_custom_call" | custom-call | flops 2013265920 | bytes 2686976 | tf_op jit(solution)/shard_map/while/body/eval_jaxpr/pallas_call | solution.py:57
  146.3 1.4 multiply_bitcast_fusion.2
  148.2 0.4 pad_maximum_fusion.9
  148.9 0.8 copy.170
  149.7 2.6 %all-to-all-start.1 = ((f32[32,12,128]{2,1,0:T(8,128)}), f32[32,12,128]{2,1,0:T(8,128)S(1)}, u32[]{:S(2)}, u32[]{:S(2)}) async-start(f32[32,12,128]{2,1,0:T(8,128)} %copy.170), calls=%async_computation.1 | async-start | bytes 524288 | tf_op jit(solution)/shard_map/while/body/eval_jaxpr/all_to_all | solution.py:199
  152.4 10.1 %all-to-all-done.1 = f32[32,12,128]{2,1,0:T(8,128)S(1)} async-done(((f32[32,12,128]{2,1,0:T(8,128)}), f32[32,12,128]{2,1,0:T(8,128)S(1)}, u32[]{:S(2)}, u32[]{:S(2)}) %all-to-all-start.1) | async-done | bytes 196640 | tf_op jit(solution)/shard_map/while/body/eval_jaxpr/all_to_all | solution.py:199
  163.3 5.2 %fusion.100 = f32[1,4,18,2048]{3,2,1,0:T(8,128)S(1)} fusion(bf16[1,2048,2048]{2,1,0:T(8,128)(2,1)} %get-tuple-element.447, f32[1,4,18,2048]{3,1,2,0:T(4,128)S(1)} %get-tuple-element.395, bf16[4,18,2048]{2,0,1:T(4,128)(2,1)S(1)} %bitcast.197, f32[2048]{0:T(1024)S(1)} %bitcast.212), kind=kOutput, calls=%fused_computation.7.clone.1 | convolution fusion | flops 604274688 | bytes 9871360 | tf_op jit(solution)/shard_map/while/body/eval_jaxpr/svcl,slj->svcj/dot_general | solution.py:217
  169.4 0.5 fusion.103
  172.2 2.5 %multiply_reduce_fusion.1 = (f32[4,4]{1,0:T(4,128)S(1)}, f32[4,4]{1,0:T(4,128)S(1)}) fusion(f32[4,18,2048]{2,0,1:T(4,128)S(1)} %bitcast.194, f32[4,18,2048]{2,1,0:T(8,128)} %copy.111, f32[4,18,2048]{2,0,1:T(4,128)} %copy-done), kind=kLoop, calls=%fused_computation.71 | loop fusion | flops 2359264 | bytes 1769600 | tf_op jit(solution)/shard_map/reduce_sum | solution.py:232
  175.0 9.7 %all_to_all.26 = f32[32,1,36]{2,1,0:T(1,128)S(1)} all-to-all(f32[32,1,36]{2,1,0:T(1,128)S(1)} %broadcast_in_dim.2), channel_id=1, replica_groups=mesh['lat'=8,'wave'=4] {'lat','wave'}, dimensions={0} | all-to-all | bytes 9216 | tf_op jit(solution)/shard_map/all_to_all | solution.py:127
  185.6 1.5 fusion.46
  187.1 0.7 copy.115
  (161 shorter events, 19.2 us)
Async XLA Ops:
  0.6 5.4 %copy-start.10 = (s32[2048]{0:T(1024)S(1)}, s32[2048]{0:T(1024)}, u32[]{:S(2)}) copy-start(s32[2048]{0:T(1024)} %param.16) | copy-start | bytes 24580
  3.2 4.2 %copy-start.8 = (f32[3,2048]{1,0:T(4,128)S(1)}, f32[3,2048]{1,0:T(4,128)}, u32[]{:S(2)}) copy-start(f32[3,2048]{1,0:T(4,128)} %param.18) | copy-start | bytes 73732
  3.2 4.2 %copy-start.1 = (f32[3,2048]{1,0:T(4,128)S(1)}, f32[3,2048]{1,0:T(4,128)}, u32[]{:S(2)}) copy-start(f32[3,2048]{1,0:T(4,128)} %param.19) | copy-start | bytes 73732
  3.2 4.2 %copy-start.4 = (f32[2048]{0:T(1024)S(1)}, f32[2048]{0:T(1024)}, u32[]{:S(2)}) copy-start(f32[2048]{0:T(1024)} %param.17) | copy-start | bytes 24580
  3.2 4.2 %copy-start.5 = (f32[3,3]{1,0:T(4,128)S(1)}, f32[3,3]{1,0:T(4,128)}, u32[]{:S(2)}) copy-start(f32[3,3]{1,0:T(4,128)} %param.21) | copy-start | bytes 112
  3.2 4.2 %copy-start.6 = (f32[3,3]{1,0:T(4,128)S(1)}, f32[3,3]{1,0:T(4,128)}, u32[]{:S(2)}) copy-start(f32[3,3]{1,0:T(4,128)} %param.22) | copy-start | bytes 112
  3.3 4.2 %copy-start.7 = (f32[3]{0:T(128)S(1)}, f32[3]{0:T(128)}, u32[]{:S(2)}) copy-start(f32[3]{0:T(128)} %param.23) | copy-start | bytes 40
  3.3 4.2 %copy-start.9 = (s32[32]{0:T(128)S(1)}, s32[32]{0:T(128)}, u32[]{:S(2)}) copy-start(s32[32]{0:T(128)} %param.15) | copy-start | bytes 388
  4.5 2.8 %copy-start.2 = (f32[1,4,18,2048]{3,1,2,0:T(4,128)}, f32[1,4,18,2048]{3,1,2,0:T(4,128)S(1)}, u32[]{:S(2)}) copy-start(f32[1,4,18,2048]{3,1,2,0:T(4,128)S(1)} %broadcast_multiply_fusion.2) | copy-start | bytes 1769476
  6.0 1.4 copy-start
  15.2 15.7 %all-to-all-start = ((bf16[32,12,128]{2,1,0:T(8,128)(2,1)}), bf16[32,12,128]{2,1,0:T(8,128)(2,1)S(1)}, u32[]{:S(2)}, u32[]{:S(2)}) async-start(bf16[32,12,128]{2,1,0:T(8,128)(2,1)} %copy.164), calls=%async_computation | async-start | bytes 262144 | tf_op jit(solution)/shard_map/while/body/eval_jaxpr/all_to_all | solution.py:188
  26.7 6.0 %copy-start.12 = (f32[64,4096]{1,0:T(8,128)S(1)}, f32[64,4096]{1,0:T(8,128)}, u32[]{:S(2)}) copy-start(f32[64,4096]{1,0:T(8,128)} %get-tuple-element.451.tide_ref) | copy-start | bytes 3145732 | tf_op jit(solution)/shard_map/while
  43.4 12.8 %all-to-all-start.1 = ((f32[32,12,128]{2,1,0:T(8,128)}), f32[32,12,128]{2,1,0:T(8,128)S(1)}, u32[]{:S(2)}, u32[]{:S(2)}) async-start(f32[32,12,128]{2,1,0:T(8,128)} %copy.170), calls=%async_computation.1 | async-start | bytes 524288 | tf_op jit(solution)/shard_map/while/body/eval_jaxpr/all_to_all | solution.py:199
  73.0 11.1 %all-to-all-start = ((bf16[32,12,128]{2,1,0:T(8,128)(2,1)}), bf16[32,12,128]{2,1,0:T(8,128)(2,1)S(1)}, u32[]{:S(2)}, u32[]{:S(2)}) async-start(bf16[32,12,128]{2,1,0:T(8,128)(2,1)} %copy.164), calls=%async_computation | async-start | bytes 262144 | tf_op jit(solution)/shard_map/while/body/eval_jaxpr/all_to_all | solution.py:188
  79.9 6.0 %copy-start.12 = (f32[64,4096]{1,0:T(8,128)S(1)}, f32[64,4096]{1,0:T(8,128)}, u32[]{:S(2)}) copy-start(f32[64,4096]{1,0:T(8,128)} %get-tuple-element.451.tide_ref) | copy-start | bytes 3145732 | tf_op jit(solution)/shard_map/while
  96.5 12.8 %all-to-all-start.1 = ((f32[32,12,128]{2,1,0:T(8,128)}), f32[32,12,128]{2,1,0:T(8,128)S(1)}, u32[]{:S(2)}, u32[]{:S(2)}) async-start(f32[32,12,128]{2,1,0:T(8,128)} %copy.170), calls=%async_computation.1 | async-start | bytes 524288 | tf_op jit(solution)/shard_map/while/body/eval_jaxpr/all_to_all | solution.py:199
  126.1 11.1 %all-to-all-start = ((bf16[32,12,128]{2,1,0:T(8,128)(2,1)}), bf16[32,12,128]{2,1,0:T(8,128)(2,1)S(1)}, u32[]{:S(2)}, u32[]{:S(2)}) async-start(bf16[32,12,128]{2,1,0:T(8,128)(2,1)} %copy.164), calls=%async_computation | async-start | bytes 262144 | tf_op jit(solution)/shard_map/while/body/eval_jaxpr/all_to_all | solution.py:188
  133.1 6.0 %copy-start.12 = (f32[64,4096]{1,0:T(8,128)S(1)}, f32[64,4096]{1,0:T(8,128)}, u32[]{:S(2)}) copy-start(f32[64,4096]{1,0:T(8,128)} %get-tuple-element.451.tide_ref) | copy-start | bytes 3145732 | tf_op jit(solution)/shard_map/while
  149.7 12.8 %all-to-all-start.1 = ((f32[32,12,128]{2,1,0:T(8,128)}), f32[32,12,128]{2,1,0:T(8,128)S(1)}, u32[]{:S(2)}, u32[]{:S(2)}) async-start(f32[32,12,128]{2,1,0:T(8,128)} %copy.170), calls=%async_computation.1 | async-start | bytes 524288 | tf_op jit(solution)/shard_map/while/body/eval_jaxpr/all_to_all | solution.py:199
  171.8 13.8 %copy-start.3 = (f32[1,4,18,2048]{3,1,2,0:T(4,128)S(1)}, f32[1,4,18,2048]{3,1,2,0:T(4,128)}, u32[]{:S(2)}) copy-start(f32[1,4,18,2048]{3,1,2,0:T(4,128)} %copy-done.2) | copy-start | bytes 1769476
  185.6 2.1 %copy-start.11 = (f32[4]{0:T(128)}, f32[4]{0:T(128)S(1)}, u32[]{:S(2)}) copy-start(f32[4]{0:T(128)S(1)} %add_sqrt_fusion) | copy-start | bytes 52

commit v10 on v8

--- a/solution.py
+++ b/solution.py
@@ -229,6 +229,8 @@
 
     spectral = lax.fori_loop(0, STEPS, one_step, basis)
     entries = float(local_slots * device_count * channels * ndeg)
+    block_end, spectral = lax.optimization_barrier((arnoldi_block, spectral))
+    basis = block_end * truncation
     local_proj = jnp.sum(basis[:, :, None] * spectral[:, None, :], axis=(0, 3, 4))
     local_self = jnp.sum(spectral * spectral, axis=(0, 2, 3))
     local_gram = jnp.sum(basis[:, :, None] * basis[:, None, :], axis=(0, 3, 4))

time: 189 us -> 189 us (level)
  no operation moved by 1% of the time
where the time goes in v10:
time: 189 us; the launch traced here: 188 us
  matrix products  40.9 us (22%)
  waiting for transfers between devices  40.5 us (21%)
  other arithmetic  34 us (18%)
  Pallas kernels  21.5 us (11%)
  starting transfers between devices  20.4 us (11%)
  local copies, waits for them, and re-layouts  18.1 us (10%)
  blocking collectives  9.67 us (5%)
    all_to_all x3, waiting for transfers between devices, one_step(): returned = lax.all_to_all(back, axes, 0, 0, tiled=True)  30.3 us
    pallas_call x3, Pallas kernels, tide_term(): pl.pallas_call(functools.partial(tide_kernel, items * lays, pairs, rows),...  21.5 us
    dot_general x3, matrix products, one_step(): jnp.einsum('svcj,slj->svcl', spectral_b, legendre, preferred_element_type...  18.1 us
    dot_general x3, matrix products, one_step(): jnp.einsum('svcl,slj->svcj', weighted, legendre, preferred_element_type=j...  15.7 us
    all_to_all x3, starting transfers between devices, one_step(): received = lax.all_to_all(sent, axes, 0, 0, tiled=True)  12.7 us
    all_to_all x3, waiting for transfers between devices, one_step(): received = lax.all_to_all(sent, axes, 0, 0, tiled=True)  10.2 us
    all_to_all x1, blocking collectives, exchange_sum(): gathered = lax.all_to_all(rows, ('lat', 'wave'), 0, 0, tiled=True)  9.67 us
    all_to_all x3, starting transfers between devices, one_step(): returned = lax.all_to_all(back, axes, 0, 0, tiled=True)  7.76 us
  transfers between devices with their start and end apart: 6, of which 6 were waited for; matrix products, arithmetic and copies ran while one was open for 8% of the time, Pallas kernels for 0%

profile of v10, /device:TPU:0, one launch (start us, length us, event | category | flops | bytes accessed | tf_op | source)
XLA Modules:
  0.0 188.0 jit_solution(16124763076575851728)
XLA Ops:
  0.6 1.2 dynamic_slice.3
  2.5 0.7 fusion.50
  3.2 0.7 multiply_add_fusion.1
  3.9 1.2 broadcast_multiply_fusion.2
  5.1 0.8 negate_bitcast_fusion
  5.9 165.3 %while.13 = (s32[]{:T(128)}, f32[1,4,18,2048]{3,1,2,0:T(4,128)S(1)}, s32[32]{0:T(128)}, f32[2048]{0:T(1024)}, f32[1,1,3,2048]{3,2,1,0:T(4,128)S(1)}, /*index=5*/...) while((s32[]{:T(128)}, ...), condition=%wide.region_1.2_spmd.clone, body=%wide.region_0.1_spmd.clone.sunk | while | flops 3234334720 | bytes 53519896 | solution.py:230
  6.0 6.0 %fusion.92 = bf16[4,18,2048]{2,1,0:T(8,128)(2,1)S(1)} fusion(bf16[1,2048,2048]{2,1,0:T(8,128)(2,1)} %get-tuple-element.451, bf16[4,18,2048]{2,0,1:T(4,128)(2,1)S(1)} %convert_bitcast_fusion.2), kind=kOutput, calls=%fused_computation.8.clone.1 | convolution fusion | flops 604127232 | bytes 8978432 | tf_op jit(solution)/shard_map/while/body/eval_jaxpr/svcj,slj->svcl/dot_general | solution.py:183
  12.9 0.7 copy.165
  13.6 7.3 %all-to-all-start = ((bf16[32,12,128]{2,1,0:T(8,128)(2,1)}), bf16[32,12,128]{2,1,0:T(8,128)(2,1)S(1)}, u32[]{:S(2)}, u32[]{:S(2)}) async-start(bf16[32,12,128]{2,1,0:T(8,128)(2,1)} %copy.165), calls=%async_computation | async-start | bytes 262144 | tf_op jit(solution)/shard_map/while/body/eval_jaxpr/all_to_all | solution.py:188
  20.9 2.1 %fusion.94 = (f32[32,4096]{1,0:T(8,128)S(1)}, f32[32,4096]{1,0:T(8,128)S(1)}) fusion(s32[32]{0:T(128)S(1)} %copy-done.5), kind=kLoop, calls=%fused_computation.44.clone.1 | loop fusion | flops 1835008 | bytes 1048704 | tf_op jit(solution)/shard_map/while/body/eval_jaxpr/cos | solution.py:21
  23.4 0.7 fusion.101
  24.1 1.1 pad_maximum_fusion.8.tab_ref
  25.2 0.7 compare_convert_fusion.2
  25.9 3.4 %all-to-all-done = bf16[32,12,128]{2,1,0:T(8,128)(2,1)S(1)} async-done(((bf16[32,12,128]{2,1,0:T(8,128)(2,1)}), bf16[32,12,128]{2,1,0:T(8,128)(2,1)S(1)}, u32[]{:S(2)}, u32[]{:S(2)}) %all-to-all-start) | async-done | bytes 98336 | tf_op jit(solution)/shard_map/while/body/eval_jaxpr/all_to_all | solution.py:188
  29.5 0.4 fusion.93
  30.3 0.9 maximum_bitcast_fusion.2.lhs_ref
  31.2 7.2 %eval_jaxpr.4 = (f32[768,128]{1,0:T(8,128)}, f32[768,64]{1,0:T(8,128)}) custom-call(bf16[768,128]{1,0:T(8,128)(2,1)} %maximum_bitcast_fusion.2.lhs_ref, bf16[128,4096]{1,0:T(8,128)(2,1)} %pad_maximum_fusion.8.tab_ref, f32[64,4096]{1,0:T(8,128)S(1)} %copy-done.7), custom_call_target="tpu_custom_call" | custom-call | flops 2013265920 | bytes 2686976 | tf_op jit(solution)/shard_map/while/body/eval_jaxpr/pallas_call | solution.py:57
  38.4 1.4 multiply_bitcast_fusion.3
  40.3 0.4 pad_maximum_fusion.9
  41.0 0.8 copy.171
  41.8 2.6 %all-to-all-start.1 = ((f32[32,12,128]{2,1,0:T(8,128)}), f32[32,12,128]{2,1,0:T(8,128)S(1)}, u32[]{:S(2)}, u32[]{:S(2)}) async-start(f32[32,12,128]{2,1,0:T(8,128)} %copy.171), calls=%async_computation.1 | async-start | bytes 524288 | tf_op jit(solution)/shard_map/while/body/eval_jaxpr/all_to_all | solution.py:199
  44.5 10.1 %all-to-all-done.1 = f32[32,12,128]{2,1,0:T(8,128)S(1)} async-done(((f32[32,12,128]{2,1,0:T(8,128)}), f32[32,12,128]{2,1,0:T(8,128)S(1)}, u32[]{:S(2)}, u32[]{:S(2)}) %all-to-all-start.1) | async-done | bytes 196640 | tf_op jit(solution)/shard_map/while/body/eval_jaxpr/all_to_all | solution.py:199
  55.4 5.2 %fusion.99 = f32[1,4,18,2048]{3,2,1,0:T(8,128)S(1)} fusion(bf16[1,2048,2048]{2,1,0:T(8,128)(2,1)} %get-tuple-element.451, f32[1,4,18,2048]{3,1,2,0:T(4,128)S(1)} %get-tuple-element.399, bf16[4,18,2048]{2,0,1:T(4,128)(2,1)S(1)} %bitcast.196, f32[2048]{0:T(1024)S(1)} %bitcast.211), kind=kOutput, calls=%fused_computation.7.clone.1 | convolution fusion | flops 604274688 | bytes 9871360 | tf_op jit(solution)/shard_map/while/body/eval_jaxpr/svcl,slj->svcj/dot_general | solution.py:217
  61.8 0.5 fusion.102
  64.1 6.0 %fusion.92 = bf16[4,18,2048]{2,1,0:T(8,128)(2,1)S(1)} fusion(bf16[1,2048,2048]{2,1,0:T(8,128)(2,1)} %get-tuple-element.451, bf16[4,18,2048]{2,0,1:T(4,128)(2,1)S(1)} %convert_bitcast_fusion.2), kind=kOutput, calls=%fused_computation.8.clone.1 | convolution fusion | flops 604127232 | bytes 8978432 | tf_op jit(solution)/shard_map/while/body/eval_jaxpr/svcj,slj->svcl/dot_general | solution.py:183
  71.0 0.7 copy.165
  71.7 2.7 %all-to-all-start = ((bf16[32,12,128]{2,1,0:T(8,128)(2,1)}), bf16[32,12,128]{2,1,0:T(8,128)(2,1)S(1)}, u32[]{:S(2)}, u32[]{:S(2)}) async-start(bf16[32,12,128]{2,1,0:T(8,128)(2,1)} %copy.165), calls=%async_computation | async-start | bytes 262144 | tf_op jit(solution)/shard_map/while/body/eval_jaxpr/all_to_all | solution.py:188
  74.4 2.1 %fusion.94 = (f32[32,4096]{1,0:T(8,128)S(1)}, f32[32,4096]{1,0:T(8,128)S(1)}) fusion(s32[32]{0:T(128)S(1)} %copy-done.5), kind=kLoop, calls=%fused_computation.44.clone.1 | loop fusion | flops 1835008 | bytes 1048704 | tf_op jit(solution)/shard_map/while/body/eval_jaxpr/cos | solution.py:21
  77.0 0.7 fusion.101
  77.6 1.1 pad_maximum_fusion.8.tab_ref
  78.7 0.7 compare_convert_fusion.2
  79.4 3.4 %all-to-all-done = bf16[32,12,128]{2,1,0:T(8,128)(2,1)S(1)} async-done(((bf16[32,12,128]{2,1,0:T(8,128)(2,1)}), bf16[32,12,128]{2,1,0:T(8,128)(2,1)S(1)}, u32[]{:S(2)}, u32[]{:S(2)}) %all-to-all-start) | async-done | bytes 98336 | tf_op jit(solution)/shard_map/while/body/eval_jaxpr/all_to_all | solution.py:188
  83.0 0.4 fusion.93
  83.8 0.9 maximum_bitcast_fusion.2.lhs_ref
  84.7 7.2 %eval_jaxpr.4 = (f32[768,128]{1,0:T(8,128)}, f32[768,64]{1,0:T(8,128)}) custom-call(bf16[768,128]{1,0:T(8,128)(2,1)} %maximum_bitcast_fusion.2.lhs_ref, bf16[128,4096]{1,0:T(8,128)(2,1)} %pad_maximum_fusion.8.tab_ref, f32[64,4096]{1,0:T(8,128)S(1)} %copy-done.7), custom_call_target="tpu_custom_call" | custom-call | flops 2013265920 | bytes 2686976 | tf_op jit(solution)/shard_map/while/body/eval_jaxpr/pallas_call | solution.py:57
  91.9 1.4 multiply_bitcast_fusion.3
  93.8 0.4 pad_maximum_fusion.9
  94.5 0.8 copy.171
  95.3 2.6 %all-to-all-start.1 = ((f32[32,12,128]{2,1,0:T(8,128)}), f32[32,12,128]{2,1,0:T(8,128)S(1)}, u32[]{:S(2)}, u32[]{:S(2)}) async-start(f32[32,12,128]{2,1,0:T(8,128)} %copy.171), calls=%async_computation.1 | async-start | bytes 524288 | tf_op jit(solution)/shard_map/while/body/eval_jaxpr/all_to_all | solution.py:199
  98.0 10.1 %all-to-all-done.1 = f32[32,12,128]{2,1,0:T(8,128)S(1)} async-done(((f32[32,12,128]{2,1,0:T(8,128)}), f32[32,12,128]{2,1,0:T(8,128)S(1)}, u32[]{:S(2)}, u32[]{:S(2)}) %all-to-all-start.1) | async-done | bytes 196640 | tf_op jit(solution)/shard_map/while/body/eval_jaxpr/all_to_all | solution.py:199
  109.0 5.2 %fusion.99 = f32[1,4,18,2048]{3,2,1,0:T(8,128)S(1)} fusion(bf16[1,2048,2048]{2,1,0:T(8,128)(2,1)} %get-tuple-element.451, f32[1,4,18,2048]{3,1,2,0:T(4,128)S(1)} %get-tuple-element.399, bf16[4,18,2048]{2,0,1:T(4,128)(2,1)S(1)} %bitcast.196, f32[2048]{0:T(1024)S(1)} %bitcast.211), kind=kOutput, calls=%fused_computation.7.clone.1 | convolution fusion | flops 604274688 | bytes 9871360 | tf_op jit(solution)/shard_map/while/body/eval_jaxpr/svcl,slj->svcj/dot_general | solution.py:217
  115.3 0.5 fusion.102
  117.6 6.0 %fusion.92 = bf16[4,18,2048]{2,1,0:T(8,128)(2,1)S(1)} fusion(bf16[1,2048,2048]{2,1,0:T(8,128)(2,1)} %get-tuple-element.451, bf16[4,18,2048]{2,0,1:T(4,128)(2,1)S(1)} %convert_bitcast_fusion.2), kind=kOutput, calls=%fused_computation.8.clone.1 | convolution fusion | flops 604127232 | bytes 8978432 | tf_op jit(solution)/shard_map/while/body/eval_jaxpr/svcj,slj->svcl/dot_general | solution.py:183
  124.5 0.7 copy.165
  125.2 2.7 %all-to-all-start = ((bf16[32,12,128]{2,1,0:T(8,128)(2,1)}), bf16[32,12,128]{2,1,0:T(8,128)(2,1)S(1)}, u32[]{:S(2)}, u32[]{:S(2)}) async-start(bf16[32,12,128]{2,1,0:T(8,128)(2,1)} %copy.165), calls=%async_computation | async-start | bytes 262144 | tf_op jit(solution)/shard_map/while/body/eval_jaxpr/all_to_all | solution.py:188
  128.0 2.1 %fusion.94 = (f32[32,4096]{1,0:T(8,128)S(1)}, f32[32,4096]{1,0:T(8,128)S(1)}) fusion(s32[32]{0:T(128)S(1)} %copy-done.5), kind=kLoop, calls=%fused_computation.44.clone.1 | loop fusion | flops 1835008 | bytes 1048704 | tf_op jit(solution)/shard_map/while/body/eval_jaxpr/cos | solution.py:21
  130.5 0.7 fusion.101
  131.1 1.1 pad_maximum_fusion.8.tab_ref
  132.2 0.7 compare_convert_fusion.2
  133.0 3.4 %all-to-all-done = bf16[32,12,128]{2,1,0:T(8,128)(2,1)S(1)} async-done(((bf16[32,12,128]{2,1,0:T(8,128)(2,1)}), bf16[32,12,128]{2,1,0:T(8,128)(2,1)S(1)}, u32[]{:S(2)}, u32[]{:S(2)}) %all-to-all-start) | async-done | bytes 98336 | tf_op jit(solution)/shard_map/while/body/eval_jaxpr/all_to_all | solution.py:188
  137.3 0.9 maximum_bitcast_fusion.2.lhs_ref
  138.2 7.2 %eval_jaxpr.4 = (f32[768,128]{1,0:T(8,128)}, f32[768,64]{1,0:T(8,128)}) custom-call(bf16[768,128]{1,0:T(8,128)(2,1)} %maximum_bitcast_fusion.2.lhs_ref, bf16[128,4096]{1,0:T(8,128)(2,1)} %pad_maximum_fusion.8.tab_ref, f32[64,4096]{1,0:T(8,128)S(1)} %copy-done.7), custom_call_target="tpu_custom_call" | custom-call | flops 2013265920 | bytes 2686976 | tf_op jit(solution)/shard_map/while/body/eval_jaxpr/pallas_call | solution.py:57
  145.4 1.4 multiply_bitcast_fusion.3
  147.3 0.4 pad_maximum_fusion.9
  148.0 0.8 copy.171
  148.9 2.6 %all-to-all-start.1 = ((f32[32,12,128]{2,1,0:T(8,128)}), f32[32,12,128]{2,1,0:T(8,128)S(1)}, u32[]{:S(2)}, u32[]{:S(2)}) async-start(f32[32,12,128]{2,1,0:T(8,128)} %copy.171), calls=%async_computation.1 | async-start | bytes 524288 | tf_op jit(solution)/shard_map/while/body/eval_jaxpr/all_to_all | solution.py:199
  151.5 10.1 %all-to-all-done.1 = f32[32,12,128]{2,1,0:T(8,128)S(1)} async-done(((f32[32,12,128]{2,1,0:T(8,128)}), f32[32,12,128]{2,1,0:T(8,128)S(1)}, u32[]{:S(2)}, u32[]{:S(2)}) %all-to-all-start.1) | async-done | bytes 196640 | tf_op jit(solution)/shard_map/while/body/eval_jaxpr/all_to_all | solution.py:199
  162.5 5.2 %fusion.99 = f32[1,4,18,2048]{3,2,1,0:T(8,128)S(1)} fusion(bf16[1,2048,2048]{2,1,0:T(8,128)(2,1)} %get-tuple-element.451, f32[1,4,18,2048]{3,1,2,0:T(4,128)S(1)} %get-tuple-element.399, bf16[4,18,2048]{2,0,1:T(4,128)(2,1)S(1)} %bitcast.196, f32[2048]{0:T(1024)S(1)} %bitcast.211), kind=kOutput, calls=%fused_computation.7.clone.1 | convolution fusion | flops 604274688 | bytes 9871360 | tf_op jit(solution)/shard_map/while/body/eval_jaxpr/svcl,slj->svcj/dot_general | solution.py:217
  168.8 0.5 fusion.102
  171.2 1.2 multiply_bitcast_fusion.1
  173.2 1.4 multiply_reduce_fusion.1
  174.8 9.7 %all_to_all.26 = f32[32,1,36]{2,1,0:T(1,128)S(1)} all-to-all(f32[32,1,36]{2,1,0:T(1,128)S(1)} %broadcast_in_dim.2), channel_id=1, replica_groups=mesh['lat'=8,'wave'=4] {'lat','wave'}, dimensions={0} | all-to-all | bytes 9216 | tf_op jit(solution)/shard_map/all_to_all | solution.py:127
  185.4 1.9 %fusion.46 = f32[1,4,18,2048]{3,1,2,0:T(4,128)} fusion(f32[1,4,18,2048]{3,1,2,0:T(4,128)S(1)} %get-tuple-element.189, f32[4,18,2048]{2,0,1:T(4,128)S(1)} %multiply_bitcast_fusion.1, f32[4]{0:T(128)S(1)} %add_sqrt_fusion, f32[4,4]{0,1:T(4,128)S(1)} %copy.114), kind=kOutput, calls=%fused_computation.74 | convolution fusion | flops 7372816 | bytes 1769552 | tf_op jit(solution)/shard_map/skcj,kv->svcj/dot_general | solution.py:239
  187.3 0.7 copy.116
  (174 shorter events, 20.7 us)
Async XLA Ops:
  12.1 8.9 %copy-start.5 = (s32[32]{0:T(128)S(1)}, s32[32]{0:T(128)}, u32[]{:S(2)}) copy-start(s32[32]{0:T(128)} %get-tuple-element.402) | copy-start | bytes 388 | tf_op jit(solution)/shard_map/while
  13.6 15.7 %all-to-all-start = ((bf16[32,12,128]{2,1,0:T(8,128)(2,1)}), bf16[32,12,128]{2,1,0:T(8,128)(2,1)S(1)}, u32[]{:S(2)}, u32[]{:S(2)}) async-start(bf16[32,12,128]{2,1,0:T(8,128)(2,1)} %copy.165), calls=%async_computation | async-start | bytes 262144 | tf_op jit(solution)/shard_map/while/body/eval_jaxpr/all_to_all | solution.py:188
  25.2 6.0 %copy-start.7 = (f32[64,4096]{1,0:T(8,128)S(1)}, f32[64,4096]{1,0:T(8,128)}, u32[]{:S(2)}) copy-start(f32[64,4096]{1,0:T(8,128)} %get-tuple-element.455.tide_ref) | copy-start | bytes 3145732 | tf_op jit(solution)/shard_map/while
  39.8 4.6 %copy-start.4 = (f32[3]{0:T(128)S(1)}, f32[3]{0:T(128)}, u32[]{:S(2)}) copy-start(f32[3]{0:T(128)} %get-tuple-element.458) | copy-start | bytes 40 | tf_op jit(solution)/shard_map/while
  40.3 14.9 %copy-start = (f32[3,2048]{1,0:T(4,128)S(1)}, f32[3,2048]{1,0:T(4,128)}, u32[]{:S(2)}) copy-start(f32[3,2048]{1,0:T(4,128)} %get-tuple-element.454) | copy-start | bytes 73732 | tf_op jit(solution)/shard_map/while
  40.7 14.6 %copy-start.1 = (f32[2048]{0:T(1024)S(1)}, f32[2048]{0:T(1024)}, u32[]{:S(2)}) copy-start(f32[2048]{0:T(1024)} %get-tuple-element.449) | copy-start | bytes 24580 | tf_op jit(solution)/shard_map/while
  41.8 12.8 %all-to-all-start.1 = ((f32[32,12,128]{2,1,0:T(8,128)}), f32[32,12,128]{2,1,0:T(8,128)S(1)}, u32[]{:S(2)}, u32[]{:S(2)}) async-start(f32[32,12,128]{2,1,0:T(8,128)} %copy.171), calls=%async_computation.1 | async-start | bytes 524288 | tf_op jit(solution)/shard_map/while/body/eval_jaxpr/all_to_all | solution.py:199
  60.7 0.7 copy-start.3
  60.7 1.6 copy-start.2
  70.2 4.3 %copy-start.5 = (s32[32]{0:T(128)S(1)}, s32[32]{0:T(128)}, u32[]{:S(2)}) copy-start(s32[32]{0:T(128)} %get-tuple-element.402) | copy-start | bytes 388 | tf_op jit(solution)/shard_map/while
  71.7 11.1 %all-to-all-start = ((bf16[32,12,128]{2,1,0:T(8,128)(2,1)}), bf16[32,12,128]{2,1,0:T(8,128)(2,1)S(1)}, u32[]{:S(2)}, u32[]{:S(2)}) async-start(bf16[32,12,128]{2,1,0:T(8,128)(2,1)} %copy.165), calls=%async_computation | async-start | bytes 262144 | tf_op jit(solution)/shard_map/while/body/eval_jaxpr/all_to_all | solution.py:188
  78.7 6.0 %copy-start.7 = (f32[64,4096]{1,0:T(8,128)S(1)}, f32[64,4096]{1,0:T(8,128)}, u32[]{:S(2)}) copy-start(f32[64,4096]{1,0:T(8,128)} %get-tuple-element.455.tide_ref) | copy-start | bytes 3145732 | tf_op jit(solution)/shard_map/while
  93.3 4.6 %copy-start.4 = (f32[3]{0:T(128)S(1)}, f32[3]{0:T(128)}, u32[]{:S(2)}) copy-start(f32[3]{0:T(128)} %get-tuple-element.458) | copy-start | bytes 40 | tf_op jit(solution)/shard_map/while
  93.8 14.9 %copy-start = (f32[3,2048]{1,0:T(4,128)S(1)}, f32[3,2048]{1,0:T(4,128)}, u32[]{:S(2)}) copy-start(f32[3,2048]{1,0:T(4,128)} %get-tuple-element.454) | copy-start | bytes 73732 | tf_op jit(solution)/shard_map/while
  94.3 14.6 %copy-start.1 = (f32[2048]{0:T(1024)S(1)}, f32[2048]{0:T(1024)}, u32[]{:S(2)}) copy-start(f32[2048]{0:T(1024)} %get-tuple-element.449) | copy-start | bytes 24580 | tf_op jit(solution)/shard_map/while
  95.3 12.8 %all-to-all-start.1 = ((f32[32,12,128]{2,1,0:T(8,128)}), f32[32,12,128]{2,1,0:T(8,128)S(1)}, u32[]{:S(2)}, u32[]{:S(2)}) async-start(f32[32,12,128]{2,1,0:T(8,128)} %copy.171), calls=%async_computation.1 | async-start | bytes 524288 | tf_op jit(solution)/shard_map/while/body/eval_jaxpr/all_to_all | solution.py:199
  114.2 0.7 copy-start.3
  114.2 1.6 copy-start.2
  123.7 4.3 %copy-start.5 = (s32[32]{0:T(128)S(1)}, s32[32]{0:T(128)}, u32[]{:S(2)}) copy-start(s32[32]{0:T(128)} %get-tuple-element.402) | copy-start | bytes 388 | tf_op jit(solution)/shard_map/while
  125.2 11.1 %all-to-all-start = ((bf16[32,12,128]{2,1,0:T(8,128)(2,1)}), bf16[32,12,128]{2,1,0:T(8,128)(2,1)S(1)}, u32[]{:S(2)}, u32[]{:S(2)}) async-start(bf16[32,12,128]{2,1,0:T(8,128)(2,1)} %copy.165), calls=%async_computation | async-start | bytes 262144 | tf_op jit(solution)/shard_map/while/body/eval_jaxpr/all_to_all | solution.py:188
  132.2 6.0 %copy-start.7 = (f32[64,4096]{1,0:T(8,128)S(1)}, f32[64,4096]{1,0:T(8,128)}, u32[]{:S(2)}) copy-start(f32[64,4096]{1,0:T(8,128)} %get-tuple-element.455.tide_ref) | copy-start | bytes 3145732 | tf_op jit(solution)/shard_map/while
  146.8 4.6 %copy-start.4 = (f32[3]{0:T(128)S(1)}, f32[3]{0:T(128)}, u32[]{:S(2)}) copy-start(f32[3]{0:T(128)} %get-tuple-element.458) | copy-start | bytes 40 | tf_op jit(solution)/shard_map/while
  147.3 14.9 %copy-start = (f32[3,2048]{1,0:T(4,128)S(1)}, f32[3,2048]{1,0:T(4,128)}, u32[]{:S(2)}) copy-start(f32[3,2048]{1,0:T(4,128)} %get-tuple-element.454) | copy-start | bytes 73732 | tf_op jit(solution)/shard_map/while
  147.8 14.6 %copy-start.1 = (f32[2048]{0:T(1024)S(1)}, f32[2048]{0:T(1024)}, u32[]{:S(2)}) copy-start(f32[2048]{0:T(1024)} %get-tuple-element.449) | copy-start | bytes 24580 | tf_op jit(solution)/shard_map/while
  148.9 12.8 %all-to-all-start.1 = ((f32[32,12,128]{2,1,0:T(8,128)}), f32[32,12,128]{2,1,0:T(8,128)S(1)}, u32[]{:S(2)}, u32[]{:S(2)}) async-start(f32[32,12,128]{2,1,0:T(8,128)} %copy.171), calls=%async_computation.1 | async-start | bytes 524288 | tf_op jit(solution)/shard_map/while/body/eval_jaxpr/all_to_all | solution.py:199
  167.7 0.7 copy-start.3
  167.7 1.6 copy-start.2
  185.4 2.6 %copy-start.6 = (f32[4]{0:T(128)}, f32[4]{0:T(128)S(1)}, u32[]{:S(2)}) copy-start(f32[4]{0:T(128)S(1)} %add_sqrt_fusion) | copy-start | bytes 52

commit v11 on v8

--- a/solution.py
+++ b/solution.py
@@ -174,8 +174,10 @@
     advect = (
         local_waves.astype(jnp.float32)[:, None, None, None] * zonal_flow[None, None, :, :] / ntrunc
     )
-    def one_step(step_index, spectral):
-        step_waves, spectral = lax.optimization_barrier((wave_index, spectral))
+    def one_step(step_index, carry):
+        spectral, _ = carry
+        step_waves, step_basis, spectral = lax.optimization_barrier((wave_index, basis, spectral))
+        step_gram = jnp.sum(step_basis[:, :, None] * step_basis[:, None, :], axis=(0, 3, 4))
         tables = angle_tables(step_waves, tide_height.shape[1])
         tables_upper = tables.astype(jnp.bfloat16)
         tables_lower = (tables - tables_upper.astype(jnp.float32)).astype(jnp.bfloat16)
@@ -225,13 +227,13 @@
             ).reshape(local_slots, vectors, channels, ndeg)
             * truncation
         )
-        return spectral
-
-    spectral = lax.fori_loop(0, STEPS, one_step, basis)
+        return spectral, step_gram
+
+    gram_shape = jnp.zeros((vectors, vectors), jnp.float32)
+    spectral, local_gram = lax.fori_loop(0, STEPS, one_step, (basis, gram_shape))
     entries = float(local_slots * device_count * channels * ndeg)
     local_proj = jnp.sum(basis[:, :, None] * spectral[:, None, :], axis=(0, 3, 4))
     local_self = jnp.sum(spectral * spectral, axis=(0, 2, 3))
-    local_gram = jnp.sum(basis[:, :, None] * basis[:, None, :], axis=(0, 3, 4))
     projection, self_sum, gram = exchange_sum((local_proj, local_self, local_gram), device_count)
     hessenberg = projection / entries
     residual = spectral - jnp.einsum(

time: 189 us -> 199 us (1.053)
  waiting for transfers between devices: 40.5 us -> 30.3 us
  starting transfers between devices: 20.4 us -> 30.2 us
  other arithmetic: 34.1 us -> 42.1 us
    all_to_all x3, waiting for transfers between devices: 10.2 us -> 0.01 us  [one_step(): received = lax.all_to_all(sent, axes, 0, 0, tiled=True)]
    all_to_all x3, starting transfers between devices: 7.75 us -> 17.5 us  [one_step(): returned = lax.all_to_all(back, axes, 0, 0, tiled=True)]
    reduce_sum x0 -> x3, other arithmetic: none -> 3.97 us  [one_step(): jnp.sum(step_basis[:, :, None] * step_basis[:, None, :], axis=(0, 3, 4))]
    concatenate x3, other arithmetic: 3.22 us -> 6.31 us  [tide_term(): tabs = jnp.concatenate([tables_upper, tables_lower], axis=0)]
    convert_element_type x3, other arithmetic: 0.19 us -> 2.6 us  [one_step(): (tables - tables_upper.astype(jnp.float32)).astype(jnp.bfloat16)]
  transfers between devices with their start and end apart: 6 -> 6, of which waited for: 6 -> 3; matrix products, arithmetic and copies ran while one was open for 8% -> 13% of each run, Pallas kernels for 0% -> 0%
where the time goes in v11:
time: 199 us; the launch traced here: 198 us
  other arithmetic  42.1 us (21%)
  matrix products  41 us (21%)
  waiting for transfers between devices  30.3 us (15%)
  starting transfers between devices  30.2 us (15%)
  Pallas kernels  21.5 us (11%)
  local copies, waits for them, and re-layouts  20.1 us (10%)
  blocking collectives  9.71 us (5%)
    all_to_all x3, waiting for transfers between devices, one_step(): returned = lax.all_to_all(back, axes, 0, 0, tiled=True)  30.3 us
    pallas_call x3, Pallas kernels, tide_term(): pl.pallas_call(functools.partial(tide_kernel, items * lays, pairs, rows),...  21.5 us
    dot_general x3, matrix products, one_step(): jnp.einsum('svcj,slj->svcl', spectral_b, legendre, preferred_element_type...  18.1 us
    all_to_all x3, starting transfers between devices, one_step(): returned = lax.all_to_all(back, axes, 0, 0, tiled=True)  17.5 us
    dot_general x3, matrix products, one_step(): jnp.einsum('svcl,slj->svcj', weighted, legendre, preferred_element_type=j...  15.7 us
    all_to_all x3, starting transfers between devices, one_step(): received = lax.all_to_all(sent, axes, 0, 0, tiled=True)  12.8 us
    all_to_all x1, blocking collectives, exchange_sum(): gathered = lax.all_to_all(rows, ('lat', 'wave'), 0, 0, tiled=True)  9.71 us
    cos x3, other arithmetic, angle_tables(): return jnp.concatenate([jnp.cos(theta), jnp.sin(theta)], axis=0)  6.33 us
  transfers between devices with their start and end apart: 6, of which 3 were waited for; matrix products, arithmetic and copies ran while one was open for 13% of the time, Pallas kernels for 0%

profile of v11, /device:TPU:0, one launch (start us, length us, event | category | flops | bytes accessed | tf_op | source)
XLA Modules:
  0.0 197.7 jit_solution(17007379192017090706)
XLA Ops:
  0.7 1.3 dynamic_slice.3
  2.6 0.6 fusion.50
  3.3 1.2 broadcast_multiply_fusion.2
  4.5 1.2 fusion.61
  5.8 1.3 copy.113
  7.2 174.1 %while.15 = (s32[]{:T(128)}, f32[1,4,18,2048]{3,1,2,0:T(4,128)S(1)}, f32[4,4]{1,0:T(4,128)}, s32[32]{0:T(128)S(1)}, f32[1,4,18,2048]{3,1,2,0:T(4,128)S(1)}, /*in...) while((s32[]{:T(128)}, ...), condition=%wide.region_2.3_spmd.clone, body=%wide.region_0.2_spmd.clone.sunk | while | flops 3235514368 | bytes 60465832 | solution.py:233
  7.3 6.0 %fusion.93 = bf16[4,18,2048]{2,1,0:T(8,128)(2,1)S(1)} fusion(bf16[1,2048,2048]{2,1,0:T(8,128)(2,1)} %get-tuple-element.528, bf16[4,18,2048]{2,0,1:T(4,128)(2,1)S(1)} %convert_bitcast_fusion.2), kind=kOutput, calls=%fused_computation.9.clone.1 | convolution fusion | flops 604127232 | bytes 8978432 | tf_op jit(solution)/shard_map/while/body/eval_jaxpr/svcj,slj->svcl/dot_general | solution.py:185
  14.2 0.7 copy.167
  14.9 7.3 %all-to-all-start = ((bf16[32,12,128]{2,1,0:T(8,128)(2,1)}), bf16[32,12,128]{2,1,0:T(8,128)(2,1)S(1)}, u32[]{:S(2)}, u32[]{:S(2)}) async-start(bf16[32,12,128]{2,1,0:T(8,128)(2,1)} %copy.167), calls=%async_computation | async-start | bytes 262144 | tf_op jit(solution)/shard_map/while/body/eval_jaxpr/all_to_all | solution.py:190
  22.2 2.1 %fusion.95 = (f32[32,4096]{1,0:T(8,128)S(1)}, f32[32,4096]{1,0:T(8,128)S(1)}) fusion(s32[32]{0:T(128)S(1)} %get-tuple-element.472), kind=kLoop, calls=%fused_computation.45.clone.1 | loop fusion | flops 1835008 | bytes 1048704 | tf_op jit(solution)/shard_map/while/body/eval_jaxpr/cos | solution.py:21
  24.4 0.9 subtract_convert_fusion.2
  25.6 0.6 compare_convert_fusion.2
  26.2 0.6 fusion.102
  27.2 2.1 %pad_maximum_fusion.8.tab_ref = bf16[128,4096]{1,0:T(8,128)(2,1)} fusion(bf16[64,4096]{1,0:T(8,128)(2,1)} %subtract_convert_fusion.2, bf16[64,4096]{1,0:T(8,128)(2,1)S(1)} %fusion.96), kind=kLoop, calls=%fused_computation.17.clone.1 | loop fusion | flops 2097152 | bytes 2097152 | tf_op jit(solution)/shard_map/while/body/eval_jaxpr/concatenate | solution.py:54
  29.3 1.3 multiply_reduce_fusion.5
  31.6 0.9 maximum_bitcast_fusion.2.lhs_ref
  32.5 7.2 %eval_jaxpr.4 = (f32[768,128]{1,0:T(8,128)}, f32[768,64]{1,0:T(8,128)}) custom-call(bf16[768,128]{1,0:T(8,128)(2,1)} %maximum_bitcast_fusion.2.lhs_ref, bf16[128,4096]{1,0:T(8,128)(2,1)} %pad_maximum_fusion.8.tab_ref, f32[64,4096]{1,0:T(8,128)S(1)} %copy-done.11), custom_call_target="tpu_custom_call" | custom-call | flops 2013265920 | bytes 2686976 | tf_op jit(solution)/shard_map/while/body/eval_jaxpr/pallas_call | solution.py:57
  39.6 1.4 multiply_bitcast_fusion.2
  41.6 0.4 pad_maximum_fusion.9
  42.2 0.8 copy.173
  43.1 5.8 %all-to-all-start.1 = ((f32[32,12,128]{2,1,0:T(8,128)}), f32[32,12,128]{2,1,0:T(8,128)S(1)}, u32[]{:S(2)}, u32[]{:S(2)}) async-start(f32[32,12,128]{2,1,0:T(8,128)} %copy.173), calls=%async_computation.1 | async-start | bytes 524288 | tf_op jit(solution)/shard_map/while/body/eval_jaxpr/all_to_all | solution.py:201
  49.0 10.1 %all-to-all-done.1 = f32[32,12,128]{2,1,0:T(8,128)S(1)} async-done(((f32[32,12,128]{2,1,0:T(8,128)}), f32[32,12,128]{2,1,0:T(8,128)S(1)}, u32[]{:S(2)}, u32[]{:S(2)}) %all-to-all-start.1) | async-done | bytes 196640 | tf_op jit(solution)/shard_map/while/body/eval_jaxpr/all_to_all | solution.py:201
  59.9 5.2 %fusion.100 = f32[1,4,18,2048]{3,2,1,0:T(8,128)S(1)} fusion(bf16[1,2048,2048]{2,1,0:T(8,128)(2,1)} %get-tuple-element.528, f32[1,4,18,2048]{3,1,2,0:T(4,128)S(1)} %get-tuple-element.469, bf16[4,18,2048]{2,0,1:T(4,128)(2,1)S(1)} %bitcast.202, f32[2048]{0:T(1024)S(1)} %bitcast.217), kind=kOutput, calls=%fused_computation.7.clone.1 | convolution fusion | flops 604274688 | bytes 9871360 | tf_op jit(solution)/shard_map/while/body/eval_jaxpr/svcl,slj->svcj/dot_general | solution.py:219
  66.0 0.5 fusion.103
  68.3 6.0 %fusion.93 = bf16[4,18,2048]{2,1,0:T(8,128)(2,1)S(1)} fusion(bf16[1,2048,2048]{2,1,0:T(8,128)(2,1)} %get-tuple-element.528, bf16[4,18,2048]{2,0,1:T(4,128)(2,1)S(1)} %convert_bitcast_fusion.2), kind=kOutput, calls=%fused_computation.9.clone.1 | convolution fusion | flops 604127232 | bytes 8978432 | tf_op jit(solution)/shard_map/while/body/eval_jaxpr/svcj,slj->svcl/dot_general | solution.py:185
  75.2 0.7 copy.167
  75.9 2.7 %all-to-all-start = ((bf16[32,12,128]{2,1,0:T(8,128)(2,1)}), bf16[32,12,128]{2,1,0:T(8,128)(2,1)S(1)}, u32[]{:S(2)}, u32[]{:S(2)}) async-start(bf16[32,12,128]{2,1,0:T(8,128)(2,1)} %copy.167), calls=%async_computation | async-start | bytes 262144 | tf_op jit(solution)/shard_map/while/body/eval_jaxpr/all_to_all | solution.py:190
  78.7 2.1 %fusion.95 = (f32[32,4096]{1,0:T(8,128)S(1)}, f32[32,4096]{1,0:T(8,128)S(1)}) fusion(s32[32]{0:T(128)S(1)} %get-tuple-element.472), kind=kLoop, calls=%fused_computation.45.clone.1 | loop fusion | flops 1835008 | bytes 1048704 | tf_op jit(solution)/shard_map/while/body/eval_jaxpr/cos | solution.py:21
  80.9 0.9 subtract_convert_fusion.2
  82.0 0.6 compare_convert_fusion.2
  82.7 0.6 fusion.102
  83.7 2.1 %pad_maximum_fusion.8.tab_ref = bf16[128,4096]{1,0:T(8,128)(2,1)} fusion(bf16[64,4096]{1,0:T(8,128)(2,1)} %subtract_convert_fusion.2, bf16[64,4096]{1,0:T(8,128)(2,1)S(1)} %fusion.96), kind=kLoop, calls=%fused_computation.17.clone.1 | loop fusion | flops 2097152 | bytes 2097152 | tf_op jit(solution)/shard_map/while/body/eval_jaxpr/concatenate | solution.py:54
  85.8 1.3 multiply_reduce_fusion.5
  88.0 0.9 maximum_bitcast_fusion.2.lhs_ref
  88.9 7.2 %eval_jaxpr.4 = (f32[768,128]{1,0:T(8,128)}, f32[768,64]{1,0:T(8,128)}) custom-call(bf16[768,128]{1,0:T(8,128)(2,1)} %maximum_bitcast_fusion.2.lhs_ref, bf16[128,4096]{1,0:T(8,128)(2,1)} %pad_maximum_fusion.8.tab_ref, f32[64,4096]{1,0:T(8,128)S(1)} %copy-done.11), custom_call_target="tpu_custom_call" | custom-call | flops 2013265920 | bytes 2686976 | tf_op jit(solution)/shard_map/while/body/eval_jaxpr/pallas_call | solution.py:57
  96.1 1.4 multiply_bitcast_fusion.2
  98.0 0.4 pad_maximum_fusion.9
  98.7 0.8 copy.173
  99.5 5.8 %all-to-all-start.1 = ((f32[32,12,128]{2,1,0:T(8,128)}), f32[32,12,128]{2,1,0:T(8,128)S(1)}, u32[]{:S(2)}, u32[]{:S(2)}) async-start(f32[32,12,128]{2,1,0:T(8,128)} %copy.173), calls=%async_computation.1 | async-start | bytes 524288 | tf_op jit(solution)/shard_map/while/body/eval_jaxpr/all_to_all | solution.py:201
  105.4 10.1 %all-to-all-done.1 = f32[32,12,128]{2,1,0:T(8,128)S(1)} async-done(((f32[32,12,128]{2,1,0:T(8,128)}), f32[32,12,128]{2,1,0:T(8,128)S(1)}, u32[]{:S(2)}, u32[]{:S(2)}) %all-to-all-start.1) | async-done | bytes 196640 | tf_op jit(solution)/shard_map/while/body/eval_jaxpr/all_to_all | solution.py:201
  116.4 5.2 %fusion.100 = f32[1,4,18,2048]{3,2,1,0:T(8,128)S(1)} fusion(bf16[1,2048,2048]{2,1,0:T(8,128)(2,1)} %get-tuple-element.528, f32[1,4,18,2048]{3,1,2,0:T(4,128)S(1)} %get-tuple-element.469, bf16[4,18,2048]{2,0,1:T(4,128)(2,1)S(1)} %bitcast.202, f32[2048]{0:T(1024)S(1)} %bitcast.217), kind=kOutput, calls=%fused_computation.7.clone.1 | convolution fusion | flops 604274688 | bytes 9871360 | tf_op jit(solution)/shard_map/while/body/eval_jaxpr/svcl,slj->svcj/dot_general | solution.py:219
  122.5 0.5 fusion.103
  124.8 6.0 %fusion.93 = bf16[4,18,2048]{2,1,0:T(8,128)(2,1)S(1)} fusion(bf16[1,2048,2048]{2,1,0:T(8,128)(2,1)} %get-tuple-element.528, bf16[4,18,2048]{2,0,1:T(4,128)(2,1)S(1)} %convert_bitcast_fusion.2), kind=kOutput, calls=%fused_computation.9.clone.1 | convolution fusion | flops 604127232 | bytes 8978432 | tf_op jit(solution)/shard_map/while/body/eval_jaxpr/svcj,slj->svcl/dot_general | solution.py:185
  131.7 0.7 copy.167
  132.4 2.7 %all-to-all-start = ((bf16[32,12,128]{2,1,0:T(8,128)(2,1)}), bf16[32,12,128]{2,1,0:T(8,128)(2,1)S(1)}, u32[]{:S(2)}, u32[]{:S(2)}) async-start(bf16[32,12,128]{2,1,0:T(8,128)(2,1)} %copy.167), calls=%async_computation | async-start | bytes 262144 | tf_op jit(solution)/shard_map/while/body/eval_jaxpr/all_to_all | solution.py:190
  135.1 2.1 %fusion.95 = (f32[32,4096]{1,0:T(8,128)S(1)}, f32[32,4096]{1,0:T(8,128)S(1)}) fusion(s32[32]{0:T(128)S(1)} %get-tuple-element.472), kind=kLoop, calls=%fused_computation.45.clone.1 | loop fusion | flops 1835008 | bytes 1048704 | tf_op jit(solution)/shard_map/while/body/eval_jaxpr/cos | solution.py:21
  137.3 0.9 subtract_convert_fusion.2
  138.4 0.6 compare_convert_fusion.2
  139.1 0.6 fusion.102
  140.1 2.1 %pad_maximum_fusion.8.tab_ref = bf16[128,4096]{1,0:T(8,128)(2,1)} fusion(bf16[64,4096]{1,0:T(8,128)(2,1)} %subtract_convert_fusion.2, bf16[64,4096]{1,0:T(8,128)(2,1)S(1)} %fusion.96), kind=kLoop, calls=%fused_computation.17.clone.1 | loop fusion | flops 2097152 | bytes 2097152 | tf_op jit(solution)/shard_map/while/body/eval_jaxpr/concatenate | solution.py:54
  142.2 1.3 multiply_reduce_fusion.5
  144.5 0.9 maximum_bitcast_fusion.2.lhs_ref
  145.4 7.2 %eval_jaxpr.4 = (f32[768,128]{1,0:T(8,128)}, f32[768,64]{1,0:T(8,128)}) custom-call(bf16[768,128]{1,0:T(8,128)(2,1)} %maximum_bitcast_fusion.2.lhs_ref, bf16[128,4096]{1,0:T(8,128)(2,1)} %pad_maximum_fusion.8.tab_ref, f32[64,4096]{1,0:T(8,128)S(1)} %copy-done.11), custom_call_target="tpu_custom_call" | custom-call | flops 2013265920 | bytes 2686976 | tf_op jit(solution)/shard_map/while/body/eval_jaxpr/pallas_call | solution.py:57
  152.5 1.4 multiply_bitcast_fusion.2
  155.1 0.8 copy.173
  156.0 5.8 %all-to-all-start.1 = ((f32[32,12,128]{2,1,0:T(8,128)}), f32[32,12,128]{2,1,0:T(8,128)S(1)}, u32[]{:S(2)}, u32[]{:S(2)}) async-start(f32[32,12,128]{2,1,0:T(8,128)} %copy.173), calls=%async_computation.1 | async-start | bytes 524288 | tf_op jit(solution)/shard_map/while/body/eval_jaxpr/all_to_all | solution.py:201
  161.9 10.1 %all-to-all-done.1 = f32[32,12,128]{2,1,0:T(8,128)S(1)} async-done(((f32[32,12,128]{2,1,0:T(8,128)}), f32[32,12,128]{2,1,0:T(8,128)S(1)}, u32[]{:S(2)}, u32[]{:S(2)}) %all-to-all-start.1) | async-done | bytes 196640 | tf_op jit(solution)/shard_map/while/body/eval_jaxpr/all_to_all | solution.py:201
  172.8 5.2 %fusion.100 = f32[1,4,18,2048]{3,2,1,0:T(8,128)S(1)} fusion(bf16[1,2048,2048]{2,1,0:T(8,128)(2,1)} %get-tuple-element.528, f32[1,4,18,2048]{3,1,2,0:T(4,128)S(1)} %get-tuple-element.469, bf16[4,18,2048]{2,0,1:T(4,128)(2,1)S(1)} %bitcast.202, f32[2048]{0:T(1024)S(1)} %bitcast.217), kind=kOutput, calls=%fused_computation.7.clone.1 | convolution fusion | flops 604274688 | bytes 9871360 | tf_op jit(solution)/shard_map/while/body/eval_jaxpr/svcl,slj->svcj/dot_general | solution.py:219
  178.9 0.5 fusion.103
  181.7 1.9 multiply_reduce_fusion.1
  183.7 0.8 reshape.547
  184.5 9.7 %all_to_all.26 = f32[32,1,36]{2,1,0:T(1,128)S(1)} all-to-all(f32[32,1,36]{2,1,0:T(1,128)S(1)} %broadcast_in_dim.2), channel_id=1, replica_groups=mesh['lat'=8,'wave'=4] {'lat','wave'}, dimensions={0} | all-to-all | bytes 9216 | tf_op jit(solution)/shard_map/all_to_all | solution.py:127
  195.1 1.9 fusion.46
  197.0 0.7 copy.117
  (174 shorter events, 21.7 us)
Async XLA Ops:
  0.6 5.2 %copy-start.9 = (s32[2048]{0:T(1024)S(1)}, s32[2048]{0:T(1024)}, u32[]{:S(2)}) copy-start(s32[2048]{0:T(1024)} %param.16) | copy-start | bytes 24580
  3.2 3.9 %copy-start.7 = (f32[3,2048]{1,0:T(4,128)S(1)}, f32[3,2048]{1,0:T(4,128)}, u32[]{:S(2)}) copy-start(f32[3,2048]{1,0:T(4,128)} %param.18) | copy-start | bytes 73732
  3.2 3.9 %copy-start.2 = (f32[3,2048]{1,0:T(4,128)S(1)}, f32[3,2048]{1,0:T(4,128)}, u32[]{:S(2)}) copy-start(f32[3,2048]{1,0:T(4,128)} %param.19) | copy-start | bytes 73732
  3.2 3.9 %copy-start.3 = (f32[2048]{0:T(1024)S(1)}, f32[2048]{0:T(1024)}, u32[]{:S(2)}) copy-start(f32[2048]{0:T(1024)} %param.17) | copy-start | bytes 24580
  3.2 3.9 %copy-start.4 = (f32[3,3]{1,0:T(4,128)S(1)}, f32[3,3]{1,0:T(4,128)}, u32[]{:S(2)}) copy-start(f32[3,3]{1,0:T(4,128)} %param.21) | copy-start | bytes 112
  3.3 3.9 %copy-start.5 = (f32[3,3]{1,0:T(4,128)S(1)}, f32[3,3]{1,0:T(4,128)}, u32[]{:S(2)}) copy-start(f32[3,3]{1,0:T(4,128)} %param.22) | copy-start | bytes 112
  3.3 3.9 %copy-start.6 = (f32[3]{0:T(128)S(1)}, f32[3]{0:T(128)}, u32[]{:S(2)}) copy-start(f32[3]{0:T(128)} %param.23) | copy-start | bytes 40
  3.3 3.9 %copy-start.8 = (s32[32]{0:T(128)S(1)}, s32[32]{0:T(128)}, u32[]{:S(2)}) copy-start(s32[32]{0:T(128)} %param.15) | copy-start | bytes 388
  14.9 15.7 %all-to-all-start = ((bf16[32,12,128]{2,1,0:T(8,128)(2,1)}), bf16[32,12,128]{2,1,0:T(8,128)(2,1)S(1)}, u32[]{:S(2)}, u32[]{:S(2)}) async-start(bf16[32,12,128]{2,1,0:T(8,128)(2,1)} %copy.167), calls=%async_computation | async-start | bytes 262144 | tf_op jit(solution)/shard_map/while/body/eval_jaxpr/all_to_all | solution.py:190
  25.5 1.3 copy-start
  30.6 1.8 copy-start.11
  41.5 18.1 %copy-start.1 = (f32[1,4,3,6,2048]{4,1,3,2,0:T(4,128)S(1)}, f32[1,4,3,6,2048]{4,1,3,2,0:T(4,128)}, u32[]{:S(2)}) copy-start(f32[1,4,3,6,2048]{4,1,3,2,0:T(4,128)} %copy-done) | copy-start | bytes 1769476 | tf_op jit(solution)/shard_map/while
  43.1 16.0 %all-to-all-start.1 = ((f32[32,12,128]{2,1,0:T(8,128)}), f32[32,12,128]{2,1,0:T(8,128)S(1)}, u32[]{:S(2)}, u32[]{:S(2)}) async-start(f32[32,12,128]{2,1,0:T(8,128)} %copy.173), calls=%async_computation.1 | async-start | bytes 524288 | tf_op jit(solution)/shard_map/while/body/eval_jaxpr/all_to_all | solution.py:201
  75.9 11.2 %all-to-all-start = ((bf16[32,12,128]{2,1,0:T(8,128)(2,1)}), bf16[32,12,128]{2,1,0:T(8,128)(2,1)S(1)}, u32[]{:S(2)}, u32[]{:S(2)}) async-start(bf16[32,12,128]{2,1,0:T(8,128)(2,1)} %copy.167), calls=%async_computation | async-start | bytes 262144 | tf_op jit(solution)/shard_map/while/body/eval_jaxpr/all_to_all | solution.py:190
  82.0 1.3 copy-start
  87.1 1.8 copy-start.11
  98.0 18.1 %copy-start.1 = (f32[1,4,3,6,2048]{4,1,3,2,0:T(4,128)S(1)}, f32[1,4,3,6,2048]{4,1,3,2,0:T(4,128)}, u32[]{:S(2)}) copy-start(f32[1,4,3,6,2048]{4,1,3,2,0:T(4,128)} %copy-done) | copy-start | bytes 1769476 | tf_op jit(solution)/shard_map/while
  99.5 16.0 %all-to-all-start.1 = ((f32[32,12,128]{2,1,0:T(8,128)}), f32[32,12,128]{2,1,0:T(8,128)S(1)}, u32[]{:S(2)}, u32[]{:S(2)}) async-start(f32[32,12,128]{2,1,0:T(8,128)} %copy.173), calls=%async_computation.1 | async-start | bytes 524288 | tf_op jit(solution)/shard_map/while/body/eval_jaxpr/all_to_all | solution.py:201
  132.4 11.2 %all-to-all-start = ((bf16[32,12,128]{2,1,0:T(8,128)(2,1)}), bf16[32,12,128]{2,1,0:T(8,128)(2,1)S(1)}, u32[]{:S(2)}, u32[]{:S(2)}) async-start(bf16[32,12,128]{2,1,0:T(8,128)(2,1)} %copy.167), calls=%async_computation | async-start | bytes 262144 | tf_op jit(solution)/shard_map/while/body/eval_jaxpr/all_to_all | solution.py:190
  138.4 1.3 copy-start
  143.5 1.8 copy-start.11
  154.4 18.1 %copy-start.1 = (f32[1,4,3,6,2048]{4,1,3,2,0:T(4,128)S(1)}, f32[1,4,3,6,2048]{4,1,3,2,0:T(4,128)}, u32[]{:S(2)}) copy-start(f32[1,4,3,6,2048]{4,1,3,2,0:T(4,128)} %copy-done) | copy-start | bytes 1769476 | tf_op jit(solution)/shard_map/while
  156.0 16.0 %all-to-all-start.1 = ((f32[32,12,128]{2,1,0:T(8,128)}), f32[32,12,128]{2,1,0:T(8,128)S(1)}, u32[]{:S(2)}, u32[]{:S(2)}) async-start(f32[32,12,128]{2,1,0:T(8,128)} %copy.173), calls=%async_computation.1 | async-start | bytes 524288 | tf_op jit(solution)/shard_map/while/body/eval_jaxpr/all_to_all | solution.py:201
  195.1 2.6 %copy-start.10 = (f32[4]{0:T(128)}, f32[4]{0:T(128)S(1)}, u32[]{:S(2)}) copy-start(f32[4]{0:T(128)S(1)} %add_sqrt_fusion) | copy-start | bytes 52
